TPU v7x, 256 devices: a whole 4x4x8 slice. The times are simulated.
256 devices in a mesh: lat: 16 (over z_hi, y, core), lon: 16 (over x, z_lo).
Axes of the slice: x: 4, y: 4, z: 8 (z_hi: 2, z_lo: 4; z = z_hi * 4 + z_lo), core: 2. Of those that a mesh axis runs over, the one named last changes fastest.
Arguments:
- forward_state: float32 [256, 32768], P(None, ('lat', 'lon')), may hold values from -6 to 6
- adjoint_state: float32 [256, 32768], P(None, ('lat', 'lon')), may hold values from -6 to 6
- inc_forward: float32 [4, 256, 32768], P(None, None, ('lat', 'lon')), may hold values from -6 to 6
- inc_adjoint: float32 [4, 256, 32768], P(None, None, ('lat', 'lon')), may hold values from -6 to 6
- bulk_modulus: float32 [32768], P(('lat', 'lon')), may hold values from 0.5 to 2
- inverse_size: float32 [32768], P(('lat', 'lon')), may hold values from 0.7 to 1.4
- face_codes: int32 [4, 32768], P(None, ('lat', 'lon')), may hold values from 0 to 7
- block_map: int32 [32768], P(('lat', 'lon')), may hold values from 0 to 255
- probe_dirs: float32 [4, 256], P(None, ('lat', 'lon')), may hold values from -6 to 6
Outputs:
- new_forward: float32 [4, 256, 32768], P(None, None, ('lat', 'lon'))
- new_adjoint: float32 [4, 256, 32768], P(None, None, ('lat', 'lon'))
- hess_vec: float32 [4, 256], P(None, ('lat', 'lon'))
All inputs are finite; a program needn't handle non-finite values.
Results may differ from a plain program's by a relative error of at most 0.00013.
Values sent between devices are 32-bit elements; how exact they have to be, the bound alone decides.
No kernel may reach another device: no remote copies, remote signals or barrier semaphores. Data moves between devices by JAX's collectives and lax.ppermute only.
A program may use at most 64 MiB of HBM per device.

v0:
```python
import jax
import jax.numpy as jnp
import numpy as np
from jax import lax
from jax.sharding import PartitionSpec as P

TIME_STEP = 0.05
PENALTY = 1.0
LIFT_FACTOR = 6.0


def shifted(block, axis, distance):
    devices = range(lax.axis_size(axis))
    route = [(i - distance, i) for i in devices if i - distance in devices]
    return lax.ppermute(block, axis, route)


def from_behind(value, axis, steps):
    count = lax.axis_size(axis)
    pairs = [(source, (source + steps) % count) for source in range(count)]
    return lax.ppermute(value, axis, pairs)


def node_tables():
    spread = 1.0 / np.sqrt(5.0)
    points = np.array([-1.0, -spread, spread, 1.0])
    weights = np.array([1.0, 5.0, 5.0, 1.0]) / 6.0
    products = np.array(
        [np.prod([points[j] - points[k] for k in range(4) if k != j]) for j in range(4)]
    )
    derivative = np.zeros((4, 4))
    for i in range(4):
        for j in range(4):
            if i != j:
                derivative[i, j] = products[i] / products[j] / (points[i] - points[j])
        derivative[i, i] = np.sum([1.0 / (points[i] - points[k]) for k in range(4) if k != i])
    identity = np.eye(4)
    directional = [
        np.kron(derivative, np.kron(identity, identity)),
        np.kron(identity, np.kron(derivative, identity)),
        np.kron(identity, np.kron(identity, derivative)),
    ]
    coupling = np.zeros((256, 256))
    for d in range(3):
        coupling[64 * (d + 1) : 64 * (d + 2), 0:64] = directional[d].T
        coupling[0:64, 64 * (d + 1) : 64 * (d + 2)] = directional[d].T
    selects = np.zeros((256, 192))
    for f in range(6):
        d = f // 2
        for u in range(4):
            for v in range(4):
                position = [u, v]
                position.insert(d, 3 * (f % 2))
                node_id = 16 * position[0] + 4 * position[1] + position[2]
                selects[node_id, 32 * f + 4 * u + v] = 1.0
                selects[64 * (d + 1) + node_id, 32 * f + 16 + 4 * u + v] = 1.0
    orient = np.zeros((8, 32), np.int32)
    for q in range(8):
        for u in range(4):
            for v in range(4):
                source_u, source_v = (v, u) if q & 1 else (u, v)
                if q & 2:
                    source_u = 3 - source_u
                if q & 4:
                    source_v = 3 - source_v
                orient[q, 4 * u + v] = 4 * source_u + source_v
                orient[q, 16 + 4 * u + v] = 16 + 4 * source_u + source_v
    quadrature = np.kron(weights, np.kron(weights, weights))
    return (
        jnp.asarray(coupling, dtype=jnp.float32),
        jnp.asarray(selects, dtype=jnp.float32),
        orient,
        jnp.asarray(quadrature, dtype=jnp.float32),
    )


def volume_rate(states, coupling, bulk_modulus, inverse_size):
    mixed = jnp.einsum("cd,scr->sdr", coupling, states, precision=lax.Precision.HIGHEST)
    channel = lax.broadcasted_iota(jnp.int32, (256, 1), 0)
    factor = jnp.where(
        channel < 64, -(bulk_modulus * inverse_size)[None, :], -inverse_size[None, :]
    )
    return mixed * factor[None]


def face_term(own_trace, neighbour, bulk_modulus, inverse_size, normal_sign):
    jump_pressure = neighbour[:, :16] - own_trace[:, :16]
    jump_velocity = neighbour[:, 16:] - own_trace[:, 16:]
    modulus = bulk_modulus[None, None, :]
    lift_scale = LIFT_FACTOR * inverse_size[None, None, :]
    on_pressure = lift_scale * (
        -modulus * normal_sign * 0.5 * jump_velocity + 0.5 * PENALTY * jump_pressure
    )
    on_velocity = lift_scale * (-normal_sign * 0.5 * jump_pressure + 0.5 * PENALTY * jump_velocity)
    return jnp.concatenate([on_pressure, on_velocity], 1)


def radial_neighbours(rad_minus, rad_plus):
    below_trace = jnp.concatenate([jnp.zeros_like(rad_plus[..., :1]), rad_plus[..., :-1]], -1)
    above_trace = jnp.concatenate([rad_minus[..., 1:], jnp.zeros_like(rad_minus[..., :1])], -1)
    return (below_trace, above_trace)


def heun_step(states, sources, neighbour_fn, bulk_modulus, inverse_size, coupling, selects):

    def rate_of(field_now):
        traces_all = jnp.einsum("ck,scr->skr", selects, field_now, precision=lax.Precision.HIGHEST)
        traces = [traces_all[:, 32 * f : 32 * f + 32] for f in range(6)]
        neighbours = neighbour_fn(traces)
        face_rates = jnp.concatenate(
            [
                face_term(traces[f], neighbours[f], bulk_modulus, inverse_size, 2.0 * (f % 2) - 1.0)
                for f in range(6)
            ],
            1,
        )
        lifted = jnp.einsum("ck,skr->scr", selects, face_rates, precision=lax.Precision.HIGHEST)
        return volume_rate(field_now, coupling, bulk_modulus, inverse_size) + lifted + sources

    first_rate = rate_of(states)
    second_rate = rate_of(states + TIME_STEP * first_rate)
    return states + 0.5 * TIME_STEP * (first_rate + second_rate)


def divergence(field_state, coupling, inverse_size):
    return -inverse_size * jnp.einsum(
        "cn,...cr->...nr", coupling[:, :64], field_state, precision=lax.Precision.HIGHEST
    )


def pressure_source(perturb, forward_div, adjoint_div):
    source_terms = jnp.concatenate(
        [perturb[:, None, :] * forward_div[None], perturb[:, None, :] * adjoint_div[None]], 0
    )
    return jnp.concatenate(
        [source_terms, jnp.zeros((source_terms.shape[0], 192, source_terms.shape[2]), jnp.float32)],
        1,
    )


def sensitivity(
    new_forward, new_adjoint, forward_div, adjoint_state, inverse_size, coupling, quadrature
):
    new_div = divergence(new_forward, coupling, inverse_size)
    integrand = new_adjoint[:, :64] * forward_div[None] + adjoint_state[None, :64] * new_div
    return jnp.einsum("n,pnr->pr", quadrature, integrand, precision=lax.Precision.HIGHEST) / (
        64.0 * inverse_size**3
    )


def reorient(neighbour, codes_face, orient):
    result = jnp.zeros_like(neighbour)
    for code in range(8):
        permuted = neighbour[:, orient[code], :]
        result = result + jnp.where((codes_face == code)[None, None, :], permuted, 0.0)
    return result


def shift_lat(rim, offset):
    return shifted(rim, "lat", offset)


def shift_lon(rim, offset):
    return from_behind(rim, "lon", offset)


def rims_lat(first_rim, last_rim):
    from_south = shift_lat(last_rim, 1)
    from_north = shift_lat(first_rim, -1)
    return (from_south, from_north)


def rims_lon(first_rim, last_rim):
    from_west = shift_lon(last_rim, 1)
    from_east = shift_lon(first_rim, -1)
    return (from_west, from_east)


def body(
    forward_state,
    adjoint_state,
    inc_forward,
    inc_adjoint,
    bulk_modulus,
    inverse_size,
    face_codes,
    block_map,
    probe_dirs,
):
    coupling, selects, orient, quadrature = node_tables()
    whole_dirs = lax.all_gather(probe_dirs, ("lat", "lon"), axis=1, tiled=True)
    perturb = jnp.take(whole_dirs, block_map, axis=1)
    forward_div = divergence(forward_state, coupling, inverse_size)
    adjoint_div = divergence(adjoint_state, coupling, inverse_size)

    def neighbour_fn(traces):
        from_south, from_north = rims_lat(traces[0], traces[1])
        from_west, from_east = rims_lon(traces[2], traces[3])
        sides = [from_south, from_north, from_west, from_east]
        horizontal = [reorient(sides[f], face_codes[f], orient) for f in range(4)]
        below_trace, above_trace = radial_neighbours(traces[4], traces[5])
        return horizontal + [below_trace, above_trace]

    probe_count = inc_forward.shape[0]
    states = jnp.concatenate([inc_forward, inc_adjoint], 0)
    sources = pressure_source(perturb, forward_div, adjoint_div)
    updated = heun_step(
        states, sources, neighbour_fn, bulk_modulus, inverse_size, coupling, selects
    )
    new_forward = updated[:probe_count]
    new_adjoint = updated[probe_count:]
    element_terms = sensitivity(
        new_forward, new_adjoint, forward_div, adjoint_state, inverse_size, coupling, quadrature
    )
    partial_sums = jax.ops.segment_sum(
        element_terms.T, block_map, num_segments=whole_dirs.shape[1]
    ).T
    hess_vec = lax.psum_scatter(partial_sums, ("lat", "lon"), scatter_dimension=1, tiled=True)
    return (new_forward, new_adjoint, hess_vec)


def solution(mesh):
    placed = (
        P(None, ("lat", "lon")),
        P(None, ("lat", "lon")),
        P(None, None, ("lat", "lon")),
        P(None, None, ("lat", "lon")),
        P(("lat", "lon")),
        P(("lat", "lon")),
        P(None, ("lat", "lon")),
        P(("lat", "lon")),
        P(None, ("lat", "lon")),
    )
    return jax.shard_map(
        body,
        mesh=mesh,
        in_specs=placed,
        out_specs=(
            P(None, None, ("lat", "lon")),
            P(None, None, ("lat", "lon")),
            P(None, ("lat", "lon")),
        ),
        check_vma=False,
    )
```

profile of v0, /device:TPU:1, one launch (start us, length us, event | category | flops | bytes accessed | tf_op | source)
XLA Modules:
  0.0 863.0 jit_solution(8838339508929728169)
XLA Ops:
  4.5 7.4 collective-permute-start.3
  11.9 3.0 collective-permute-start.1
  14.9 3.1 collective-permute-start
  21.9 597.1 %all-gather = f32[256,1,4]{2,1,0:T(1,128)S(1)} all-gather(f32[1,1,4]{2,1,0:T(1,128)S(1)} %bitcast.171), channel_id=1, replica_groups=mesh['lat'=16,'lon'=16] {'lat','lon'}, dimensions={0}, use_global_device_ids=true | all-gather | bytes 4112 | tf_op jit(solution)/shard_map/all_gather | solution.py:191
  622.4 2.1 fusion.7
  627.0 1.2 gather_fusion.24
  628.3 1.2 gather_fusion.25
  631.7 1.2 gather_fusion.17
  633.0 1.3 gather_fusion.26
  634.2 1.2 gather_fusion.18
  635.4 1.2 gather_fusion.27
  636.7 1.2 gather_fusion.19
  637.9 1.2 gather_fusion.28
  639.2 1.3 gather_fusion.20
  642.9 1.3 gather_fusion.30
  644.1 1.2 gather_fusion.22
  646.6 1.2 gather_fusion.23
  649.4 1.2 gather_fusion.9
  650.7 1.2 gather_fusion.10
  651.9 1.3 gather_fusion.11
  653.2 1.2 gather_fusion.12
  654.4 1.3 gather_fusion.13
  655.6 1.2 gather_fusion.14
  656.9 1.2 gather_fusion.15
  659.1 1.2 gather_fusion
  660.3 1.2 gather_fusion.1
  661.6 1.2 gather_fusion.2
  664.1 1.2 gather_fusion.4
  666.5 1.2 gather_fusion.6
  667.8 1.2 gather_fusion.7
  669.7 1.5 bitcast_add_fusion.7
  680.6 2.2 fusion.8
  683.5 1.5 collective-permute-start.6
  684.9 33.6 %collective-permute-start.5 = (f32[8,32,128]{2,1,0:T(8,128)}, f32[8,32,128]{2,1,0:T(8,128)}, u32[]{:S(2)}, u32[]{:S(2)}) collective-permute-start(f32[8,32,128]{2,1,0:T(8,128)} %get-tuple-element.18), channel_id=1, source_target_pairs={{16,0},{32,16},{48,32},{64,48},{80,64},{96,80},{112,96},{128,112},... | collective-permute-start | bytes 393224 | tf_op jit(solution)/shard_map/ppermute | solution.py:15
  718.6 2.1 collective-permute-start.4
  723.9 1.2 gather_fusion.59
  725.2 1.2 gather_fusion.60
  726.4 1.2 gather_fusion.61
  727.6 1.3 gather_fusion.62
  728.9 1.2 gather_fusion.63
  732.4 1.2 gather_fusion.49
  733.6 1.3 gather_fusion.50
  734.8 1.2 gather_fusion.51
  736.1 1.2 gather_fusion.52
  738.6 1.3 gather_fusion.54
  739.8 1.2 gather_fusion.55
  741.0 1.3 gather_fusion.56
  743.3 1.2 gather_fusion.41
  744.5 1.2 gather_fusion.42
  745.8 1.2 gather_fusion.43
  747.0 1.2 gather_fusion.44
  749.5 1.2 gather_fusion.46
  750.7 1.2 gather_fusion.47
  752.0 1.2 gather_fusion.48
  754.2 1.2 gather_fusion.33
  755.4 1.2 gather_fusion.34
  757.9 1.2 gather_fusion.36
  760.4 1.2 gather_fusion.38
  761.6 1.2 gather_fusion.39
  762.8 1.2 gather_fusion.40
  764.2 1.6 bitcast_add_fusion.3
  772.1 1.3 fusion.4
  776.1 1.2 scatter_custom_fusion
  777.4 85.2 %all-reduce.5 = f32[4,256]{0,1:T(8,128)S(1)} all-reduce(f32[4,256]{0,1:T(8,128)S(1)} %bitcast.169), channel_id=2, replica_groups=mesh['lat'=16,'lon'=16] {'lat','lon'}, use_global_device_ids=true, to_apply=%region_1.2.clone | all-reduce | flops 1024 | bytes 8192
  (375 shorter events, 55.7 us)
Async XLA Ops:
  0.6 20.0 %copy-start = (f32[256,128]{1,0:T(8,128)S(1)}, f32[256,128]{1,0:T(8,128)}, u32[]{:S(2)}) copy-start(f32[256,128]{1,0:T(8,128)} %param.140) | copy-start | bytes 393220
  0.6 1.2 copy-start.61
  4.5 621.5 %collective-permute-start.3 = (f32[8,32,128]{2,1,0:T(8,128)}, f32[8,32,128]{2,1,0:T(8,128)}, u32[]{:S(2)}, u32[]{:S(2)}) collective-permute-start(f32[8,32,128]{2,1,0:T(8,128)} %get-tuple-element.22), channel_id=1, source_target_pairs={{0,15},{1,0},{2,1},{3,2},{4,3},{5,4},{6,5},{7,6},{8,7},{9,8},{10,9... | collective-permute-start | bytes 393224 | tf_op jit(solution)/shard_map/ppermute | solution.py:21
  11.9 6.1 copy-start.71
  11.9 617.6 %collective-permute-start.2 = (f32[8,32,128]{2,1,0:T(8,128)}, f32[8,32,128]{2,1,0:T(8,128)}, u32[]{:S(2)}, u32[]{:S(2)}) collective-permute-start(f32[8,32,128]{2,1,0:T(8,128)} %get-tuple-element.23), channel_id=1, source_target_pairs={{0,1},{1,2},{2,3},{3,4},{4,5},{5,6},{6,7},{7,8},{8,9},{9,10},{10,1... | collective-permute-start | bytes 393224 | tf_op jit(solution)/shard_map/ppermute | solution.py:21
  11.9 636.0 %collective-permute-start.1 = (f32[8,32,128]{2,1,0:T(8,128)}, f32[8,32,128]{2,1,0:T(8,128)}, u32[]{:S(2)}, u32[]{:S(2)}) collective-permute-start(f32[8,32,128]{2,1,0:T(8,128)} %get-tuple-element.24), channel_id=1, source_target_pairs={{16,0},{32,16},{48,32},{64,48},{80,64},{96,80},{112,96},{128,112},... | collective-permute-start | bytes 393224 | tf_op jit(solution)/shard_map/ppermute | solution.py:15
  14.9 643.3 %collective-permute-start = (f32[8,32,128]{2,1,0:T(8,128)}, f32[8,32,128]{2,1,0:T(8,128)}, u32[]{:S(2)}, u32[]{:S(2)}) collective-permute-start(f32[8,32,128]{2,1,0:T(8,128)} %get-tuple-element.25), channel_id=1, source_target_pairs={{0,16},{16,32},{32,48},{48,64},{64,80},{80,96},{96,112},{112,128},... | collective-permute-start | bytes 393224 | tf_op jit(solution)/shard_map/ppermute | solution.py:15
  19.3 1.3 copy-start.62
  20.6 601.7 %copy-start.68 = (f32[128]{0:T(128)}, f32[128]{0:T(128)S(1)}, u32[]{:S(2)}) copy-start(f32[128]{0:T(128)S(1)} %get-tuple-element.61) | copy-start | bytes 1540
  622.4 2.1 copy-start.3
  622.4 2.1 copy-start.70
  631.7 1.2 copy-start.67
  634.2 1.2 copy-start.66
  669.7 1.7 copy-start.59
  669.7 1.7 copy-start.60
  671.3 1.0 copy-start.54
  671.3 1.1 copy-start.55
  671.3 1.1 copy-start.109
  671.3 1.1 copy-start.111
  671.3 1.1 copy-start.113
  671.3 1.1 copy-start.115
  671.3 1.1 copy-start.117
  672.8 1.1 copy-start.39
  672.8 1.1 copy-start.93
  672.8 1.1 copy-start.95
  672.8 1.1 copy-start.97
  674.2 1.1 copy-start.23
  674.2 1.1 copy-start.77
  674.2 1.1 copy-start.79
  674.2 1.1 copy-start.81
  683.5 37.9 %collective-permute-start.7 = (f32[8,32,128]{2,1,0:T(8,128)S(1)}, f32[8,32,128]{2,1,0:T(8,128)S(1)}, u32[]{:S(2)}, u32[]{:S(2)}) collective-permute-start(f32[8,32,128]{2,1,0:T(8,128)S(1)} %get-tuple-element.16), channel_id=1, source_target_pairs={{0,15},{1,0},{2,1},{3,2},{4,3},{5,4},{6,5},{7,6},{8,7},{9,8},{10,9... | collective-permute-start | bytes 393224 | tf_op jit(solution)/shard_map/ppermute | solution.py:21
  683.5 47.9 %collective-permute-start.6 = (f32[8,32,128]{2,1,0:T(8,128)}, f32[8,32,128]{2,1,0:T(8,128)}, u32[]{:S(2)}, u32[]{:S(2)}) collective-permute-start(f32[8,32,128]{2,1,0:T(8,128)} %get-tuple-element.17), channel_id=1, source_target_pairs={{0,1},{1,2},{2,3},{3,4},{4,5},{5,6},{6,7},{7,8},{8,9},{9,10},{10,1... | collective-permute-start | bytes 393224 | tf_op jit(solution)/shard_map/ppermute | solution.py:21
  684.9 57.4 %collective-permute-start.5 = (f32[8,32,128]{2,1,0:T(8,128)}, f32[8,32,128]{2,1,0:T(8,128)}, u32[]{:S(2)}, u32[]{:S(2)}) collective-permute-start(f32[8,32,128]{2,1,0:T(8,128)} %get-tuple-element.18), channel_id=1, source_target_pairs={{16,0},{32,16},{48,32},{64,48},{80,64},{96,80},{112,96},{128,112},... | collective-permute-start | bytes 393224 | tf_op jit(solution)/shard_map/ppermute | solution.py:15
  718.6 34.6 %collective-permute-start.4 = (f32[8,32,128]{2,1,0:T(8,128)}, f32[8,32,128]{2,1,0:T(8,128)}, u32[]{:S(2)}, u32[]{:S(2)}) collective-permute-start(f32[8,32,128]{2,1,0:T(8,128)} %get-tuple-element.19), channel_id=1, source_target_pairs={{0,16},{16,32},{32,48},{48,64},{64,80},{80,96},{96,112},{112,128},... | collective-permute-start | bytes 393224 | tf_op jit(solution)/shard_map/ppermute | solution.py:15
  721.4 49.6 %copy-start.11 = (f32[8,32,127]{2,1,0:T(8,128)}, f32[8,32,127]{2,1,0:T(8,128)S(1)}, u32[]{:S(2)}) copy-start(f32[8,32,127]{2,1,0:T(8,128)S(1)} %get-tuple-element.14) | copy-start | bytes 390148
  762.8 1.3 copy-start.120
  762.8 1.3 copy-start.122
  762.8 1.3 copy-start.124
  762.8 1.3 copy-start.125
  764.1 1.8 copy-start.51
  764.1 1.8 copy-start.52
  764.1 1.8 copy-start.53
  764.1 1.8 copy-start.110
  764.1 1.8 copy-start.112
  764.1 1.8 copy-start.114
  764.2 1.8 copy-start.116
  764.2 1.8 copy-start.118
  765.8 1.1 copy-start.47
  765.9 1.1 copy-start.104
  765.9 1.1 copy-start.106
  765.9 1.1 copy-start.108
  767.3 1.1 copy-start.25
  767.3 1.1 copy-start.88
  767.3 1.1 copy-start.90
  767.3 1.1 copy-start.92
  768.7 1.1 copy-start.15
  768.7 1.1 copy-start.74
  768.8 1.1 copy-start.76
  768.8 1.1 copy-start.78
  770.0 1.9 copy-start.1
  771.0 1.1 copy-start.8
  773.4 1.1 slice-start
  773.4 1.1 copy-start.64
  773.4 1.1 copy-start.69
  (84 other events, 78.5 us)
where the time goes:
time: 864 us; the launch traced here: 863 us
  blocking collectives  682 us (79%)
  local copies, waits for them, and re-layouts  107 us (12%)
  starting transfers between devices  50.7 us (6%)
  other arithmetic  11.3 us (1%)
  matrix products  9.57 us (1%)
    all_gather x1, blocking collectives, body(): whole_dirs = lax.all_gather(probe_dirs, ('lat', 'lon'), axis=1, tiled=True)  597 us
    unnamed x1, blocking collectives  85.2 us
    gather x64, local copies, waits for them, and re-layouts, reorient(): permuted = neighbour[:, orient[code], :]  78.6 us
    ppermute x4, starting transfers between devices, shifted(): return lax.ppermute(block, axis, route)  41.9 us
  transfers between devices with their start and end apart: 8, of which 0 were waited for; matrix products, arithmetic and copies ran while one was open for 8% of the time, Pallas kernels for 0%

commit v1 on v0

--- a/solution.py
+++ b/solution.py
@@ -149,11 +149,48 @@
 
 
 def reorient(neighbour, codes_face, orient):
-    result = jnp.zeros_like(neighbour)
-    for code in range(8):
-        permuted = neighbour[:, orient[code], :]
-        result = result + jnp.where((codes_face == code)[None, None, :], permuted, 0.0)
-    return result
+    states, channels, count = neighbour.shape
+    grid = neighbour.reshape(states, channels // 16, 4, 4, count)
+    bits = [(codes_face & (1 << b)) != 0 for b in range(3)]
+    flipped_v = jnp.flip(grid, 3)
+    grid = jnp.where(bits[2][None, None, None, None, :], flipped_v, grid)
+    flipped_u = jnp.flip(grid, 2)
+    grid = jnp.where(bits[1][None, None, None, None, :], flipped_u, grid)
+    swapped = jnp.swapaxes(grid, 2, 3)
+    grid = jnp.where(bits[0][None, None, None, None, :], swapped, grid)
+    return grid.reshape(states, channels, count)
+
+
+def gather_blocks(block):
+    for axis in ("lon", "lat"):
+        size = lax.axis_size(axis)
+        me = lax.axis_index(axis)
+        step = 1
+        while step < size:
+            pairs = [(i, i ^ step) for i in range(size)]
+            other = lax.ppermute(block, axis, pairs)
+            upper = ((me // step) % 2) == 1
+            block = jnp.where(upper, jnp.concatenate([other, block], -1),
+                              jnp.concatenate([block, other], -1))
+            step *= 2
+    return block
+
+
+def scatter_sums(partial):
+    for axis in ("lat", "lon"):
+        size = lax.axis_size(axis)
+        me = lax.axis_index(axis)
+        step = size // 2
+        while step >= 1:
+            half = partial.shape[-1] // 2
+            low, high = partial[..., :half], partial[..., half:]
+            upper = ((me // step) % 2) == 1
+            keep = jnp.where(upper, high, low)
+            give = jnp.where(upper, low, high)
+            pairs = [(i, i ^ step) for i in range(size)]
+            partial = keep + lax.ppermute(give, axis, pairs)
+            step //= 2
+    return partial
 
 
 def shift_lat(rim, offset):
@@ -188,7 +225,7 @@
     probe_dirs,
 ):
     coupling, selects, orient, quadrature = node_tables()
-    whole_dirs = lax.all_gather(probe_dirs, ("lat", "lon"), axis=1, tiled=True)
+    whole_dirs = gather_blocks(probe_dirs)
     perturb = jnp.take(whole_dirs, block_map, axis=1)
     forward_div = divergence(forward_state, coupling, inverse_size)
     adjoint_div = divergence(adjoint_state, coupling, inverse_size)
@@ -215,7 +252,7 @@
     partial_sums = jax.ops.segment_sum(
         element_terms.T, block_map, num_segments=whole_dirs.shape[1]
     ).T
-    hess_vec = lax.psum_scatter(partial_sums, ("lat", "lon"), scatter_dimension=1, tiled=True)
+    hess_vec = scatter_sums(partial_sums)
     return (new_forward, new_adjoint, hess_vec)
 
 

time: 864 us -> 173 us (0.20)
  blocking collectives: 682 us -> 0 us
  local copies, waits for them, and re-layouts: 107 us -> 40.7 us
  waiting for transfers between devices: 0.02 us -> 30.6 us
  other arithmetic: 11.3 us -> 24.6 us
  starting transfers between devices: 50.7 us -> 59.8 us
    all_gather x1 -> x0, blocking collectives: 597 us -> none  [body(): whole_dirs = lax.all_gather(probe_dirs, ('lat', 'lon'), axis=1, tiled=True)]
    unnamed x1 -> x0, blocking collectives: 85.2 us -> none
    gather x64 -> x0, local copies, waits for them, and re-layouts: 78.6 us -> none  [reorient(): permuted = neighbour[:, orient[code], :]]
    ppermute x0 -> x16, starting transfers between devices: none -> 39.4 us  [the longest x8 25.8 us: gather_blocks(): other = lax.ppermute(block, axis, pairs)]
    ppermute x0 -> x16, waiting for transfers between devices: none -> 30.6 us  [the longest x8 20 us: scatter_sums(): partial = keep + lax.ppermute(give, axis, pairs)]
    ppermute x4, starting transfers between devices: 41.9 us -> 13.5 us  [shifted(): return lax.ppermute(block, axis, route)]
    select_n x0 -> x34, other arithmetic: none -> 12.6 us  [the longest x8 8.02 us: reorient(): grid = jnp.where(bits[2][None, None, None, None, :], flipped_v, grid)]
    rev x0 -> x8, local copies, waits for them, and re-layouts: none -> 11.2 us  [reorient(): flipped_v = jnp.flip(grid, 3)]
  transfers between devices with their start and end apart: 8 -> 24, of which waited for: 0 -> 14; matrix products, arithmetic and copies ran while one was open for 8% -> 25% of each run, Pallas kernels for 0% -> 0%
where the time goes in v1:
time: 173 us; the launch traced here: 169 us
  starting transfers between devices  59.8 us (35%)
  local copies, waits for them, and re-layouts  40.7 us (24%)
  waiting for transfers between devices  30.6 us (18%)
  other arithmetic  24.6 us (14%)
  matrix products  12.2 us (7%)
    ppermute x8, starting transfers between devices, gather_blocks(): other = lax.ppermute(block, axis, pairs)  25.8 us
    unnamed x115, local copies, waits for them, and re-layouts  21.4 us
    ppermute x8, waiting for transfers between devices, scatter_sums(): partial = keep + lax.ppermute(give, axis, pairs)  20 us
    ppermute x8, starting transfers between devices, scatter_sums(): partial = keep + lax.ppermute(give, axis, pairs)  13.7 us
    ppermute x4, starting transfers between devices, shifted(): return lax.ppermute(block, axis, route)  13.5 us
    rev x8, local copies, waits for them, and re-layouts, reorient(): flipped_v = jnp.flip(grid, 3)  11.2 us
    ppermute x8, waiting for transfers between devices, gather_blocks(): other = lax.ppermute(block, axis, pairs)  10.5 us
    select_n x8, other arithmetic, reorient(): grid = jnp.where(bits[2][None, None, None, None, :], flipped_v, grid)  8.02 us
  transfers between devices with their start and end apart: 24, of which 14 were waited for; matrix products, arithmetic and copies ran while one was open for 25% of the time, Pallas kernels for 0%

profile of v1, /device:TPU:1, one launch (start us, length us, event | category | flops | bytes accessed | tf_op | source)
XLA Modules:
  0.0 169.4 jit_solution(13108613051613803640)
XLA Ops:
  1.4 2.5 %collective-permute-start.4 = (f32[4,1]{1,0:T(4,128)S(1)}, f32[4,1]{1,0:T(4,128)S(1)}, u32[]{:S(2)}, u32[]{:S(2)}) collective-permute-start(f32[4,1]{1,0:T(4,128)S(1)} %copy.40), channel_id=1, source_target_pairs={{0,1},{1,0},{2,3},{3,2},{4,5},{5,4},{6,7},{7,6},{8,9},{9,8},{10,11... | collective-permute-start | bytes 56 | tf_op jit(solution)/shard_map/ppermute | solution.py:171
  3.9 1.2 copy.33
  6.1 1.2 convolution_bitcast_fusion.5
  7.3 0.8 fusion.46
  8.1 4.0 %collective-permute-start = (f32[8,32,128]{2,1,0:T(8,128)}, f32[8,32,128]{2,1,0:T(8,128)}, u32[]{:S(2)}, u32[]{:S(2)}) collective-permute-start(f32[8,32,128]{2,1,0:T(8,128)} %get-tuple-element.22), channel_id=1, source_target_pairs={{0,16},{16,32},{32,48},{48,64},{64,80},{80,96},{96,112},{112,128},... | collective-permute-start | bytes 393224 | tf_op jit(solution)/shard_map/ppermute | solution.py:15
  12.2 1.9 %collective-permute-start.1 = (f32[8,32,128]{2,1,0:T(8,128)}, f32[8,32,128]{2,1,0:T(8,128)}, u32[]{:S(2)}, u32[]{:S(2)}) collective-permute-start(f32[8,32,128]{2,1,0:T(8,128)} %get-tuple-element.21), channel_id=1, source_target_pairs={{16,0},{32,16},{48,32},{64,48},{80,64},{96,80},{112,96},{128,112},... | collective-permute-start | bytes 393224 | tf_op jit(solution)/shard_map/ppermute | solution.py:15
  14.5 5.0 %collective-permute-start.3 = (f32[8,32,128]{2,1,0:T(8,128)}, f32[8,32,128]{2,1,0:T(8,128)}, u32[]{:S(2)}, u32[]{:S(2)}) collective-permute-start(f32[8,32,128]{2,1,0:T(8,128)} %get-tuple-element.19), channel_id=1, source_target_pairs={{0,15},{1,0},{2,1},{3,2},{4,3},{5,4},{6,5},{7,6},{8,7},{9,8},{10,9... | collective-permute-start | bytes 393224 | tf_op jit(solution)/shard_map/ppermute | solution.py:21
  22.8 1.0 convolution_multiply_fusion.2
  23.8 1.0 convolution_multiply_fusion.1
  25.5 1.0 fusion.7
  26.7 3.3 %collective-permute-done.5 = f32[4,2]{1,0:T(4,128)S(1)} collective-permute-done((f32[4,2]{1,0:T(4,128)S(1)}, f32[4,2]{1,0:T(4,128)S(1)}, u32[]{:S(2)}, u32[]{:S(2)}) %collective-permute-start.5) | collective-permute-done | bytes 64 | tf_op jit(solution)/shard_map/ppermute | solution.py:171
  30.3 2.2 %collective-permute-done.6 = f32[4,4]{1,0:T(4,128)S(1)} collective-permute-done((f32[4,4]{1,0:T(4,128)S(1)}, f32[4,4]{1,0:T(4,128)S(1)}, u32[]{:S(2)}, u32[]{:S(2)}) %collective-permute-start.6) | collective-permute-done | bytes 96 | tf_op jit(solution)/shard_map/ppermute | solution.py:171
  32.6 1.8 %collective-permute-start.7 = (f32[4,8]{1,0:T(4,128)S(1)}, f32[4,8]{1,0:T(4,128)S(1)}, u32[]{:S(2)}, u32[]{:S(2)}) collective-permute-start(f32[4,8]{1,0:T(4,128)S(1)} %maximum_select_fusion.2), channel_id=1, source_target_pairs={{0,8},{1,9},{2,10},{3,11},{4,12},{5,13},{6,14},{7,15},{8,0},{9,1},... | collective-permute-start | bytes 392 | tf_op jit(solution)/shard_map/ppermute | solution.py:171
  34.4 2.2 %collective-permute-done.7 = f32[4,8]{1,0:T(4,128)S(1)} collective-permute-done((f32[4,8]{1,0:T(4,128)S(1)}, f32[4,8]{1,0:T(4,128)S(1)}, u32[]{:S(2)}, u32[]{:S(2)}) %collective-permute-start.7) | collective-permute-done | bytes 160 | tf_op jit(solution)/shard_map/ppermute | solution.py:171
  36.6 2.5 %collective-permute-start.8 = (f32[4,16]{1,0:T(4,128)S(1)}, f32[4,16]{1,0:T(4,128)S(1)}, u32[]{:S(2)}, u32[]{:S(2)}) collective-permute-start(f32[4,16]{1,0:T(4,128)S(1)} %maximum_select_fusion.3), channel_id=1, source_target_pairs={{0,16},{16,0},{32,48},{48,32},{64,80},{80,64},{96,112},{112,96},{1... | collective-permute-start | bytes 776 | tf_op jit(solution)/shard_map/ppermute | solution.py:171
  39.1 0.8 collective-permute-done.8
  40.0 3.4 %collective-permute-start.9 = (f32[4,32]{1,0:T(4,128)S(1)}, f32[4,32]{1,0:T(4,128)S(1)}, u32[]{:S(2)}, u32[]{:S(2)}) collective-permute-start(f32[4,32]{1,0:T(4,128)S(1)} %maximum_select_fusion.4), channel_id=1, source_target_pairs={{0,32},{16,48},{32,0},{48,16},{64,96},{80,112},{96,64},{112,80},{1... | collective-permute-start | bytes 1544 | tf_op jit(solution)/shard_map/ppermute | solution.py:171
  43.4 1.0 collective-permute-done.9
  44.5 3.1 %collective-permute-start.10 = (f32[4,64]{1,0:T(4,128)S(1)}, f32[4,64]{1,0:T(4,128)S(1)}, u32[]{:S(2)}, u32[]{:S(2)}) collective-permute-start(f32[4,64]{1,0:T(4,128)S(1)} %maximum_select_fusion.5), channel_id=1, source_target_pairs={{0,64},{16,80},{32,96},{48,112},{64,0},{80,16},{96,32},{112,48},{1... | collective-permute-start | bytes 3080 | tf_op jit(solution)/shard_map/ppermute | solution.py:171
  47.6 1.0 collective-permute-done.10
  48.6 12.3 %collective-permute-start.11 = (f32[4,128]{1,0:T(4,128)S(1)}, f32[4,128]{1,0:T(4,128)S(1)}, u32[]{:S(2)}, u32[]{:S(2)}) collective-permute-start(f32[4,128]{1,0:T(4,128)S(1)} %maximum_select_fusion.6), channel_id=1, source_target_pairs={{0,128},{16,144},{32,160},{48,176},{64,192},{80,208},{96,224},{112... | collective-permute-start | bytes 6152 | tf_op jit(solution)/shard_map/ppermute | solution.py:171
  66.7 1.6 broadcast_select_fusion.1
  68.3 1.7 gather_fusion
  70.9 0.9 broadcast_multiply_fusion.1
  71.9 1.7 rev.50
  74.1 1.0 broadcast_select_fusion.9
  77.8 1.7 rev.52
  80.1 1.0 broadcast_select_fusion.7
  85.1 0.9 broadcast_select_fusion.5
  88.8 1.0 rev.56
  89.8 1.0 broadcast_select_fusion.3
  92.2 0.9 copy-done.10
  94.2 0.9 copy-done.3
  95.2 1.8 %fusion.6 = f32[8,256,128]{1,2,0:T(8,128)S(1)} fusion(f32[8,256,128]{1,2,0:T(8,128)S(1)} %fusion.7, f32[8,192,128]{2,1,0:T(8,128)S(1)} %multiply_dynamic-update-slice_fusion.12, f32[256,192,1]{0,1,2:T(8,128)S(1)} %copy-done.2, f32[4,64,128]{1,2,0:T(8,128)S(1)} %copy-done.5, f32[4,64,128]{1,2,0:T(8,128)S(1)} %copy-done.3), kind=kOutput, calls=%fused_computation.11 | convolution fusion | flops 605552640 | bytes 3342336 | tf_op jit(solution)/shard_map/ck,skr->scr/dot_general | solution.py:117
  97.0 1.3 convolution_bitcast_fusion.4
  98.3 2.0 %fusion.8 = f32[8,256,128]{1,2,0:T(8,128)} fusion(f32[256,256,1]{1,0,2:T(8,128)S(1)} %copy-done.16, f32[256,128]{0,1:T(8,128)S(1)} %copy-done.8, f32[8,256,128]{1,2,0:T(8,128)S(1)} %fusion.6, f32[4,256,128]{1,2,0:T(8,128)S(1)} %copy.34, f32[4,256,128]{1,2,0:T(8,128)S(1)} %copy.33), kind=kOutput, calls=%fused_computation.14 | convolution fusion | flops 806354944 | bytes 3538944 | tf_op jit(solution)/shard_map/cd,scr->sdr/dot_general | solution.py:78
  101.1 1.5 collective-permute-start.14
  102.5 5.0 %collective-permute-start.12 = (f32[8,32,128]{2,1,0:T(8,128)}, f32[8,32,128]{2,1,0:T(8,128)}, u32[]{:S(2)}, u32[]{:S(2)}) collective-permute-start(f32[8,32,128]{2,1,0:T(8,128)} %get-tuple-element.16), channel_id=1, source_target_pairs={{0,16},{16,32},{32,48},{48,64},{64,80},{80,96},{96,112},{112,128},... | collective-permute-start | bytes 393224 | tf_op jit(solution)/shard_map/ppermute | solution.py:15
  107.5 2.5 %collective-permute-start.13 = (f32[8,32,128]{2,1,0:T(8,128)}, f32[8,32,128]{2,1,0:T(8,128)}, u32[]{:S(2)}, u32[]{:S(2)}) collective-permute-start(f32[8,32,128]{2,1,0:T(8,128)} %get-tuple-element.15), channel_id=1, source_target_pairs={{16,0},{32,16},{48,32},{64,48},{80,64},{96,80},{112,96},{128,112},... | collective-permute-start | bytes 393224 | tf_op jit(solution)/shard_map/ppermute | solution.py:15
  110.8 1.7 rev.64
  112.4 1.0 broadcast_select_fusion.2
  114.1 1.7 rev.62
  115.8 1.0 broadcast_select_fusion.4
  118.3 1.7 rev.58
  120.0 1.0 broadcast_select_fusion.8
  121.7 1.7 rev.60
  123.4 1.0 broadcast_select_fusion.6
  124.5 0.8 copy-done.14
  125.7 0.8 copy-done.12
  127.9 1.9 %fusion.4 = f32[8,256,128]{1,2,0:T(8,128)S(1)} fusion(f32[8,256,128]{1,2,0:T(8,128)S(1)} %fusion.6, f32[8,256,128]{1,2,0:T(8,128)S(1)} %copy-done.1, f32[8,192,128]{2,1,0:T(8,128)S(1)} %multiply_dynamic-update-slice_fusion, f32[256,192,1]{0,1,2:T(8,128)S(1)} %copy-done.2, f32[4,64,128]{1,2,0:T(8,128)S(1)} %copy-done.6, f32[4,64,128]{1,2,0:T(8,128)S(1)} %copy-done.4, ...), kind=kOutput, calls=%fused_computation.7 | convolution fusion | flops 606601216 | bytes 5439488 | tf_op jit(solution)/shard_map/ck,skr->scr/dot_general | solution.py:117
  131.7 1.2 scatter_custom_fusion
  133.0 2.8 %collective-permute-start.16 = (f32[4,128]{0,1:T(8,128)S(1)}, f32[4,128]{0,1:T(8,128)S(1)}, u32[]{:S(2)}, u32[]{:S(2)}) collective-permute-start(f32[4,128]{0,1:T(8,128)S(1)} %slice_select_fusion), channel_id=1, source_target_pairs={{0,128},{16,144},{32,160},{48,176},{64,192},{80,208},{96,224},{112... | collective-permute-start | bytes 6152 | tf_op jit(solution)/shard_map/ppermute | solution.py:191
  135.8 5.0 %collective-permute-done.16 = f32[4,128]{0,1:T(8,128)S(1)} collective-permute-done((f32[4,128]{0,1:T(8,128)S(1)}, f32[4,128]{0,1:T(8,128)S(1)}, u32[]{:S(2)}, u32[]{:S(2)}) %collective-permute-start.16) | collective-permute-done | bytes 2080 | tf_op jit(solution)/shard_map/ppermute | solution.py:191
  140.9 4.6 %collective-permute-done.17 = f32[4,64]{0,1:T(8,128)S(1)} collective-permute-done((f32[4,64]{0,1:T(8,128)S(1)}, f32[4,64]{0,1:T(8,128)S(1)}, u32[]{:S(2)}, u32[]{:S(2)}) %collective-permute-start.17) | collective-permute-done | bytes 1056 | tf_op jit(solution)/shard_map/ppermute | solution.py:191
  145.5 1.7 %collective-permute-start.18 = (f32[4,32]{0,1:T(8,128)S(1)}, f32[4,32]{0,1:T(8,128)S(1)}, u32[]{:S(2)}, u32[]{:S(2)}) collective-permute-start(f32[4,32]{0,1:T(8,128)S(1)} %slice_select_fusion.2), channel_id=1, source_target_pairs={{0,32},{16,48},{32,0},{48,16},{64,96},{80,112},{96,64},{112,80},{1... | collective-permute-start | bytes 1544 | tf_op jit(solution)/shard_map/ppermute | solution.py:191
  147.2 1.1 collective-permute-done.18
  148.3 7.2 %collective-permute-start.19 = (f32[4,16]{0,1:T(8,128)S(1)}, f32[4,16]{0,1:T(8,128)S(1)}, u32[]{:S(2)}, u32[]{:S(2)}) collective-permute-start(f32[4,16]{0,1:T(8,128)S(1)} %slice_select_fusion.3), channel_id=1, source_target_pairs={{0,16},{16,0},{32,48},{48,32},{64,80},{80,64},{96,112},{112,96},{1... | collective-permute-start | bytes 776 | tf_op jit(solution)/shard_map/ppermute | solution.py:191
  156.4 1.6 collective-permute-start.20
  158.0 1.0 copy.54
  159.0 1.4 collective-permute-done.20
  160.5 1.0 copy.55
  161.5 1.4 collective-permute-done.21
  163.0 3.3 %collective-permute-done.22 = f32[4,2]{0,1:T(2,128)S(1)} collective-permute-done((f32[4,2]{0,1:T(2,128)S(1)}, f32[4,2]{0,1:T(2,128)S(1)}, u32[]{:S(2)}, u32[]{:S(2)}) %collective-permute-start.22) | collective-permute-done | bytes 64 | tf_op jit(solution)/shard_map/ppermute | solution.py:191
  166.5 2.4 %collective-permute-done.23 = f32[4,1]{0,1:T(1,128)S(1)} collective-permute-done((f32[4,1]{0,1:T(1,128)S(1)}, f32[4,1]{0,1:T(1,128)S(1)}, u32[]{:S(2)}, u32[]{:S(2)}) %collective-permute-start.23) | collective-permute-done | bytes 48 | tf_op jit(solution)/shard_map/ppermute | solution.py:191
  (213 shorter events, 36.1 us)
Async XLA Ops:
  0.6 22.1 %copy-start = (f32[256,128]{1,0:T(8,128)S(1)}, f32[256,128]{1,0:T(8,128)}, u32[]{:S(2)}) copy-start(f32[256,128]{1,0:T(8,128)} %param.12) | copy-start | bytes 393220
  1.4 3.7 %copy-start.18 = (f32[4,256,128]{2,1,0:T(8,128)S(1)}, f32[4,256,128]{2,1,0:T(8,128)}, u32[]{:S(2)}) copy-start(f32[4,256,128]{2,1,0:T(8,128)} %param.15) | copy-start | bytes 1572868
  1.4 25.1 %collective-permute-start.4 = (f32[4,1]{1,0:T(4,128)S(1)}, f32[4,1]{1,0:T(4,128)S(1)}, u32[]{:S(2)}, u32[]{:S(2)}) collective-permute-start(f32[4,1]{1,0:T(4,128)S(1)} %copy.40), channel_id=1, source_target_pairs={{0,1},{1,0},{2,3},{3,2},{4,5},{5,4},{6,7},{7,6},{8,9},{9,8},{10,11... | collective-permute-start | bytes 56 | tf_op jit(solution)/shard_map/ppermute | solution.py:171
  5.1 0.9 copy-start.2
  8.1 63.7 %collective-permute-start = (f32[8,32,128]{2,1,0:T(8,128)}, f32[8,32,128]{2,1,0:T(8,128)}, u32[]{:S(2)}, u32[]{:S(2)}) collective-permute-start(f32[8,32,128]{2,1,0:T(8,128)} %get-tuple-element.22), channel_id=1, source_target_pairs={{0,16},{16,32},{32,48},{48,64},{64,80},{80,96},{96,112},{112,128},... | collective-permute-start | bytes 393224 | tf_op jit(solution)/shard_map/ppermute | solution.py:15
  12.2 65.6 %collective-permute-start.1 = (f32[8,32,128]{2,1,0:T(8,128)}, f32[8,32,128]{2,1,0:T(8,128)}, u32[]{:S(2)}, u32[]{:S(2)}) collective-permute-start(f32[8,32,128]{2,1,0:T(8,128)} %get-tuple-element.21), channel_id=1, source_target_pairs={{16,0},{32,16},{48,32},{64,48},{80,64},{96,80},{112,96},{128,112},... | collective-permute-start | bytes 393224 | tf_op jit(solution)/shard_map/ppermute | solution.py:15
  14.1 69.7 %collective-permute-start.2 = (f32[8,32,128]{2,1,0:T(8,128)}, f32[8,32,128]{2,1,0:T(8,128)S(1)}, u32[]{:S(2)}, u32[]{:S(2)}) collective-permute-start(f32[8,32,128]{2,1,0:T(8,128)} %get-tuple-element.20), channel_id=1, source_target_pairs={{0,1},{1,2},{2,3},{3,4},{4,5},{5,6},{6,7},{7,8},{8,9},{9,10},{10,1... | collective-permute-start | bytes 393224 | tf_op jit(solution)/shard_map/ppermute | solution.py:21
  14.5 74.2 %collective-permute-start.3 = (f32[8,32,128]{2,1,0:T(8,128)}, f32[8,32,128]{2,1,0:T(8,128)}, u32[]{:S(2)}, u32[]{:S(2)}) collective-permute-start(f32[8,32,128]{2,1,0:T(8,128)} %get-tuple-element.19), channel_id=1, source_target_pairs={{0,15},{1,0},{2,1},{3,2},{4,3},{5,4},{6,5},{7,6},{8,7},{9,8},{10,9... | collective-permute-start | bytes 393224 | tf_op jit(solution)/shard_map/ppermute | solution.py:21
  20.8 2.0 %copy-start.20 = (f32[256,64]{1,0:T(8,128)S(1)}, f32[256,64]{1,0:T(8,128)}, u32[]{:S(2)}) copy-start(f32[256,64]{1,0:T(8,128)} %constant.217) | copy-start | bytes 196612
  22.7 2.6 %copy-start.29 = (f32[128]{0:T(128)}, f32[128]{0:T(128)S(1)}, u32[]{:S(2)}) copy-start(f32[128]{0:T(128)S(1)} %get-tuple-element.40) | copy-start | bytes 1540
  22.8 1.0 copy-start.25
  23.8 1.0 copy-start.49
  23.8 1.7 %copy-start.15 = (f32[256,256,1]{1,0,2:T(8,128)S(1)}, f32[256,256,1]{1,0,2:T(8,128)}, u32[]{:S(2)}) copy-start(f32[256,256,1]{1,0,2:T(8,128)} %constant.218) | copy-start | bytes 786436
  25.5 1.0 copy-start.7
  26.6 3.4 %collective-permute-start.5 = (f32[4,2]{1,0:T(4,128)S(1)}, f32[4,2]{1,0:T(4,128)S(1)}, u32[]{:S(2)}, u32[]{:S(2)}) collective-permute-start(f32[4,2]{1,0:T(4,128)S(1)} %maximum_select_fusion), channel_id=1, source_target_pairs={{0,2},{1,3},{2,0},{3,1},{4,6},{5,7},{6,4},{7,5},{8,10},{9,11},{10,... | collective-permute-start | bytes 104 | tf_op jit(solution)/shard_map/ppermute | solution.py:171
  30.1 2.5 %collective-permute-start.6 = (f32[4,4]{1,0:T(4,128)S(1)}, f32[4,4]{1,0:T(4,128)S(1)}, u32[]{:S(2)}, u32[]{:S(2)}) collective-permute-start(f32[4,4]{1,0:T(4,128)S(1)} %maximum_select_fusion.1), channel_id=1, source_target_pairs={{0,4},{1,5},{2,6},{3,7},{4,0},{5,1},{6,2},{7,3},{8,12},{9,13},{10,... | collective-permute-start | bytes 200 | tf_op jit(solution)/shard_map/ppermute | solution.py:171
  32.6 4.0 %collective-permute-start.7 = (f32[4,8]{1,0:T(4,128)S(1)}, f32[4,8]{1,0:T(4,128)S(1)}, u32[]{:S(2)}, u32[]{:S(2)}) collective-permute-start(f32[4,8]{1,0:T(4,128)S(1)} %maximum_select_fusion.2), channel_id=1, source_target_pairs={{0,8},{1,9},{2,10},{3,11},{4,12},{5,13},{6,14},{7,15},{8,0},{9,1},... | collective-permute-start | bytes 392 | tf_op jit(solution)/shard_map/ppermute | solution.py:171
  36.6 3.3 %collective-permute-start.8 = (f32[4,16]{1,0:T(4,128)S(1)}, f32[4,16]{1,0:T(4,128)S(1)}, u32[]{:S(2)}, u32[]{:S(2)}) collective-permute-start(f32[4,16]{1,0:T(4,128)S(1)} %maximum_select_fusion.3), channel_id=1, source_target_pairs={{0,16},{16,0},{32,48},{48,32},{64,80},{80,64},{96,112},{112,96},{1... | collective-permute-start | bytes 776 | tf_op jit(solution)/shard_map/ppermute | solution.py:171
  40.0 4.4 %collective-permute-start.9 = (f32[4,32]{1,0:T(4,128)S(1)}, f32[4,32]{1,0:T(4,128)S(1)}, u32[]{:S(2)}, u32[]{:S(2)}) collective-permute-start(f32[4,32]{1,0:T(4,128)S(1)} %maximum_select_fusion.4), channel_id=1, source_target_pairs={{0,32},{16,48},{32,0},{48,16},{64,96},{80,112},{96,64},{112,80},{1... | collective-permute-start | bytes 1544 | tf_op jit(solution)/shard_map/ppermute | solution.py:171
  44.5 4.1 %collective-permute-start.10 = (f32[4,64]{1,0:T(4,128)S(1)}, f32[4,64]{1,0:T(4,128)S(1)}, u32[]{:S(2)}, u32[]{:S(2)}) collective-permute-start(f32[4,64]{1,0:T(4,128)S(1)} %maximum_select_fusion.5), channel_id=1, source_target_pairs={{0,64},{16,80},{32,96},{48,112},{64,0},{80,16},{96,32},{112,48},{1... | collective-permute-start | bytes 3080 | tf_op jit(solution)/shard_map/ppermute | solution.py:171
  48.6 15.9 %collective-permute-start.11 = (f32[4,128]{1,0:T(4,128)S(1)}, f32[4,128]{1,0:T(4,128)S(1)}, u32[]{:S(2)}, u32[]{:S(2)}) collective-permute-start(f32[4,128]{1,0:T(4,128)S(1)} %maximum_select_fusion.6), channel_id=1, source_target_pairs={{0,128},{16,144},{32,160},{48,176},{64,192},{80,208},{96,224},{112... | collective-permute-start | bytes 6152 | tf_op jit(solution)/shard_map/ppermute | solution.py:171
  61.5 0.8 copy-start.28
  62.3 0.8 copy-start.27
  63.0 0.8 slice-start
  68.3 1.7 copy-start.51
  70.1 0.8 copy-start.24
  89.8 2.4 %copy-start.17 = (f32[8,192,128]{2,1,0:T(8,128)S(1)}, f32[8,192,128]{2,1,0:T(8,128)}, u32[]{:S(2)}) copy-start(f32[8,192,128]{2,1,0:T(8,128)} %multiply_dynamic-update-slice_fusion.18) | copy-start | bytes 2359300
  92.2 0.9 copy-start.10
  93.2 0.9 copy-start.9
  94.1 0.9 copy-start.3
  94.1 1.0 copy-start.5
  97.0 1.3 copy-start.8
  97.0 1.3 copy-start.16
  101.1 9.7 %collective-permute-start.15 = (f32[8,32,128]{2,1,0:T(8,128)S(1)}, f32[8,32,128]{2,1,0:T(8,128)}, u32[]{:S(2)}, u32[]{:S(2)}) collective-permute-start(f32[8,32,128]{2,1,0:T(8,128)S(1)} %get-tuple-element.13), channel_id=1, source_target_pairs={{0,15},{1,0},{2,1},{3,2},{4,3},{5,4},{6,5},{7,6},{8,7},{9,8},{10,9... | collective-permute-start | bytes 393224 | tf_op jit(solution)/shard_map/ppermute | solution.py:21
  101.1 13.1 %collective-permute-start.14 = (f32[8,32,128]{2,1,0:T(8,128)}, f32[8,32,128]{2,1,0:T(8,128)}, u32[]{:S(2)}, u32[]{:S(2)}) collective-permute-start(f32[8,32,128]{2,1,0:T(8,128)} %get-tuple-element.14), channel_id=1, source_target_pairs={{0,1},{1,2},{2,3},{3,4},{4,5},{5,6},{6,7},{7,8},{8,9},{9,10},{10,1... | collective-permute-start | bytes 393224 | tf_op jit(solution)/shard_map/ppermute | solution.py:21
  102.5 15.8 %collective-permute-start.12 = (f32[8,32,128]{2,1,0:T(8,128)}, f32[8,32,128]{2,1,0:T(8,128)}, u32[]{:S(2)}, u32[]{:S(2)}) collective-permute-start(f32[8,32,128]{2,1,0:T(8,128)} %get-tuple-element.16), channel_id=1, source_target_pairs={{0,16},{16,32},{32,48},{48,64},{64,80},{80,96},{96,112},{112,128},... | collective-permute-start | bytes 393224 | tf_op jit(solution)/shard_map/ppermute | solution.py:15
  107.5 14.2 %collective-permute-start.13 = (f32[8,32,128]{2,1,0:T(8,128)}, f32[8,32,128]{2,1,0:T(8,128)}, u32[]{:S(2)}, u32[]{:S(2)}) collective-permute-start(f32[8,32,128]{2,1,0:T(8,128)} %get-tuple-element.15), channel_id=1, source_target_pairs={{16,0},{32,16},{48,32},{64,48},{80,64},{96,80},{112,96},{128,112},... | collective-permute-start | bytes 393224 | tf_op jit(solution)/shard_map/ppermute | solution.py:15
  112.4 1.0 copy-start.36
  115.8 1.1 copy-start.22
  115.8 1.1 copy-start.35
  115.8 1.1 copy-start.37
  115.8 1.1 copy-start.47
  121.0 0.7 copy-start.13
  123.4 1.0 copy-start.33
  123.4 1.1 copy-start.41
  124.4 0.9 copy-start.14
  124.4 1.0 copy-start.21
  124.4 1.0 copy-start.39
  125.6 0.9 copy-start.12
  125.7 1.0 copy-start.11
  125.7 1.3 copy-start.1
  126.8 1.0 copy-start.4
  126.8 1.1 copy-start.6
  127.9 2.0 %copy-start.23 = (f32[64,128]{0,1:T(8,128)S(1)}, f32[64,128]{0,1:T(8,128)}, u32[]{:S(2)}) copy-start(f32[64,128]{0,1:T(8,128)} %copy.53) | copy-start | bytes 98308
  127.9 2.0 %copy-start.26 = (f32[256,64,1]{1,0,2:T(8,128)S(1)}, f32[256,64,1]{1,0,2:T(8,128)}, u32[]{:S(2)}) copy-start(f32[256,64,1]{1,0,2:T(8,128)} %constant.220) | copy-start | bytes 196612
  127.9 2.0 %copy-start.30 = (f32[128]{0:T(128)S(1)}, f32[128]{0:T(128)}, u32[]{:S(2)}) copy-start(f32[128]{0:T(128)} %copy-done.29) | copy-start | bytes 1540
  133.0 7.8 %collective-permute-start.16 = (f32[4,128]{0,1:T(8,128)S(1)}, f32[4,128]{0,1:T(8,128)S(1)}, u32[]{:S(2)}, u32[]{:S(2)}) collective-permute-start(f32[4,128]{0,1:T(8,128)S(1)} %slice_select_fusion), channel_id=1, source_target_pairs={{0,128},{16,144},{32,160},{48,176},{64,192},{80,208},{96,224},{112... | collective-permute-start | bytes 6152 | tf_op jit(solution)/shard_map/ppermute | solution.py:191
  140.8 4.7 %collective-permute-start.17 = (f32[4,64]{0,1:T(8,128)S(1)}, f32[4,64]{0,1:T(8,128)S(1)}, u32[]{:S(2)}, u32[]{:S(2)}) collective-permute-start(f32[4,64]{0,1:T(8,128)S(1)} %slice_select_fusion.1), channel_id=1, source_target_pairs={{0,64},{16,80},{32,96},{48,112},{64,0},{80,16},{96,32},{112,48},{1... | collective-permute-start | bytes 3080 | tf_op jit(solution)/shard_map/ppermute | solution.py:191
  145.5 2.8 %collective-permute-start.18 = (f32[4,32]{0,1:T(8,128)S(1)}, f32[4,32]{0,1:T(8,128)S(1)}, u32[]{:S(2)}, u32[]{:S(2)}) collective-permute-start(f32[4,32]{0,1:T(8,128)S(1)} %slice_select_fusion.2), channel_id=1, source_target_pairs={{0,32},{16,48},{32,0},{48,16},{64,96},{80,112},{96,64},{112,80},{1... | collective-permute-start | bytes 1544 | tf_op jit(solution)/shard_map/ppermute | solution.py:191
  148.3 8.0 %collective-permute-start.19 = (f32[4,16]{0,1:T(8,128)S(1)}, f32[4,16]{0,1:T(8,128)S(1)}, u32[]{:S(2)}, u32[]{:S(2)}) collective-permute-start(f32[4,16]{0,1:T(8,128)S(1)} %slice_select_fusion.3), channel_id=1, source_target_pairs={{0,16},{16,0},{32,48},{48,32},{64,80},{80,64},{96,112},{112,96},{1... | collective-permute-start | bytes 776 | tf_op jit(solution)/shard_map/ppermute | solution.py:191
  156.4 4.0 %collective-permute-start.20 = (f32[4,8]{0,1:T(8,128)S(1)}, f32[4,8]{0,1:T(8,128)S(1)}, u32[]{:S(2)}, u32[]{:S(2)}) collective-permute-start(f32[4,8]{0,1:T(8,128)S(1)} %slice_select_fusion.4), channel_id=1, source_target_pairs={{0,8},{1,9},{2,10},{3,11},{4,12},{5,13},{6,14},{7,15},{8,0},{9,1},... | collective-permute-start | bytes 392 | tf_op jit(solution)/shard_map/ppermute | solution.py:191
  160.4 2.5 %collective-permute-start.21 = (f32[4,4]{0,1:T(4,128)S(1)}, f32[4,4]{0,1:T(4,128)S(1)}, u32[]{:S(2)}, u32[]{:S(2)}) collective-permute-start(f32[4,4]{0,1:T(4,128)S(1)} %slice_select_fusion.5), channel_id=1, source_target_pairs={{0,4},{1,5},{2,6},{3,7},{4,0},{5,1},{6,2},{7,3},{8,12},{9,13},{10,... | collective-permute-start | bytes 200 | tf_op jit(solution)/shard_map/ppermute | solution.py:191
  162.9 3.4 %collective-permute-start.22 = (f32[4,2]{0,1:T(2,128)S(1)}, f32[4,2]{0,1:T(2,128)S(1)}, u32[]{:S(2)}, u32[]{:S(2)}) collective-permute-start(f32[4,2]{0,1:T(2,128)S(1)} %broadcast_select_fusion.10), channel_id=1, source_target_pairs={{0,2},{1,3},{2,0},{3,1},{4,6},{5,7},{6,4},{7,5},{8,10},{9,11},{10,... | collective-permute-start | bytes 104 | tf_op jit(solution)/shard_map/ppermute | solution.py:191
  166.4 2.5 %collective-permute-start.23 = (f32[4,1]{0,1:T(1,128)S(1)}, f32[4,1]{0,1:T(1,128)S(1)}, u32[]{:S(2)}, u32[]{:S(2)}) collective-permute-start(f32[4,1]{0,1:T(1,128)S(1)} %broadcast_select_fusion.11), channel_id=1, source_target_pairs={{0,1},{1,0},{2,3},{3,2},{4,5},{5,4},{6,7},{7,6},{8,9},{9,8},{10,11... | collective-permute-start | bytes 56 | tf_op jit(solution)/shard_map/ppermute | solution.py:191
  (16 other events, 10.3 us)

commit v2 on v0

--- a/solution.py
+++ b/solution.py
@@ -149,11 +149,27 @@
 
 
 def reorient(neighbour, codes_face, orient):
-    result = jnp.zeros_like(neighbour)
-    for code in range(8):
-        permuted = neighbour[:, orient[code], :]
-        result = result + jnp.where((codes_face == code)[None, None, :], permuted, 0.0)
+    choices = np.zeros((orient.shape[0], 32, 32), np.float32)
+    for code in range(orient.shape[0]):
+        choices[code, np.arange(32), orient[code]] = 1.0
+    candidates = jnp.einsum(
+        "qkj,sjr->qskr", jnp.asarray(choices), neighbour, precision=lax.Precision.HIGHEST
+    )
+    result = candidates[0]
+    for code in range(1, orient.shape[0]):
+        result = jnp.where((codes_face == code)[None, None, :], candidates[code], result)
     return result
+
+
+def gather_blocks(block):
+    count = lax.axis_size(("lat", "lon"))
+    spread = jnp.broadcast_to(block.T, (count, block.shape[0]))
+    return lax.all_to_all(spread, ("lat", "lon"), 0, 0, tiled=True).T
+
+
+def scatter_sums(partial):
+    pieces = lax.all_to_all(partial.T, ("lat", "lon"), 0, 0, tiled=True)
+    return jnp.sum(pieces, 0)[:, None]
 
 
 def shift_lat(rim, offset):
@@ -188,7 +204,7 @@
     probe_dirs,
 ):
     coupling, selects, orient, quadrature = node_tables()
-    whole_dirs = lax.all_gather(probe_dirs, ("lat", "lon"), axis=1, tiled=True)
+    whole_dirs = gather_blocks(probe_dirs)
     perturb = jnp.take(whole_dirs, block_map, axis=1)
     forward_div = divergence(forward_state, coupling, inverse_size)
     adjoint_div = divergence(adjoint_state, coupling, inverse_size)
@@ -215,7 +231,7 @@
     partial_sums = jax.ops.segment_sum(
         element_terms.T, block_map, num_segments=whole_dirs.shape[1]
     ).T
-    hess_vec = lax.psum_scatter(partial_sums, ("lat", "lon"), scatter_dimension=1, tiled=True)
+    hess_vec = scatter_sums(partial_sums)
     return (new_forward, new_adjoint, hess_vec)
 
 

time: 864 us -> 125 us (0.14)
  blocking collectives: 682 us -> 0 us
  local copies, waits for them, and re-layouts: 107 us -> 19.9 us
  matrix products: 9.57 us -> 22.5 us
  waiting for transfers between devices: 0.02 us -> 12.2 us
    all_gather x1 -> x0, blocking collectives: 597 us -> none  [body(): whole_dirs = lax.all_gather(probe_dirs, ('lat', 'lon'), axis=1, tiled=True)]
    unnamed x1 -> x0, blocking collectives: 85.2 us -> none
    gather x64 -> x0, local copies, waits for them, and re-layouts: 78.6 us -> none  [reorient(): permuted = neighbour[:, orient[code], :]]
    all_to_all x0 -> x2, starting transfers between devices: none -> 33 us  [the longest x1 17.2 us: gather_blocks(): return lax.all_to_all(spread, ('lat', 'lon'), 0, 0, tiled=True).T]
    ppermute x4, starting transfers between devices: 41.9 us -> 12.4 us  [shifted(): return lax.ppermute(block, axis, route)]
    dot_general x0 -> x8, matrix products: none -> 11.3 us  [reorient(): jnp.einsum('qkj,sjr->qskr', jnp.asarray(choices), neighbour, precision=la...]
    all_to_all x0 -> x2, waiting for transfers between devices: none -> 11.1 us  [the longest x1 10.9 us: scatter_sums(): pieces = lax.all_to_all(partial.T, ('lat', 'lon'), 0, 0, tiled=True)]
  transfers between devices with their start and end apart: 8 -> 10, of which waited for: 0 -> 3; matrix products, arithmetic and copies ran while one was open for 8% -> 24% of each run, Pallas kernels for 0% -> 0%
where the time goes in v2:
time: 125 us; the launch traced here: 124 us
  starting transfers between devices  57.7 us (46%)
  matrix products  22.5 us (18%)
  local copies, waits for them, and re-layouts  19.9 us (16%)
  waiting for transfers between devices  12.2 us (10%)
  other arithmetic  9.8 us (8%)
  between operations  1.64 us (1%)
    all_to_all x1, starting transfers between devices, gather_blocks(): return lax.all_to_all(spread, ('lat', 'lon'), 0, 0, tiled=True).T  17.2 us
    all_to_all x1, starting transfers between devices, scatter_sums(): pieces = lax.all_to_all(partial.T, ('lat', 'lon'), 0, 0, tiled=True)  15.8 us
    ppermute x4, starting transfers between devices, shifted(): return lax.ppermute(block, axis, route)  12.4 us
    ppermute x4, starting transfers between devices, from_behind(): return lax.ppermute(value, axis, pairs)  12.3 us
    dot_general x8, matrix products, reorient(): jnp.einsum('qkj,sjr->qskr', jnp.asarray(choices), neighbour, precision=la...  11.3 us
    all_to_all x1, waiting for transfers between devices, scatter_sums(): pieces = lax.all_to_all(partial.T, ('lat', 'lon'), 0, 0, tiled=True)  10.9 us
    unnamed x96, local copies, waits for them, and re-layouts  9.21 us
    dot_general x2, matrix products, rate_of(): jnp.einsum('ck,skr->scr', selects, face_rates, precision=lax.Precision.HI...  3.78 us
  transfers between devices with their start and end apart: 10, of which 3 were waited for; matrix products, arithmetic and copies ran while one was open for 24% of the time, Pallas kernels for 0%

profile of v2, /device:TPU:1, one launch (start us, length us, event | category | flops | bytes accessed | tf_op | source)
XLA Modules:
  0.0 123.7 jit_solution(16656923500129133092)
XLA Ops:
  0.7 1.3 %copy.41 = f32[4,256,128]{1,2,0:T(8,128)S(1)} copy(f32[4,256,128]{2,1,0:T(8,128)} %param.22) | data formatting | bytes 1048576 | tf_op args[2]
  2.0 0.2 copy.42
  2.2 0.7 copy-done.2
  2.9 1.2 convolution_bitcast_fusion.13
  4.1 0.8 fusion.105
  4.9 4.6 %collective-permute-start = (f32[8,32,128]{2,1,0:T(8,128)}, f32[8,32,128]{2,1,0:T(8,128)}, u32[]{:S(2)}, u32[]{:S(2)}) collective-permute-start(f32[8,32,128]{2,1,0:T(8,128)} %get-tuple-element.22), channel_id=1, source_target_pairs={{0,16},{16,32},{32,48},{48,64},{64,80},{80,96},{96,112},{112,128},... | collective-permute-start | bytes 393224 | tf_op jit(solution)/shard_map/ppermute | solution.py:15
  9.5 2.5 %collective-permute-start.1 = (f32[8,32,128]{2,1,0:T(8,128)}, f32[8,32,128]{2,1,0:T(8,128)}, u32[]{:S(2)}, u32[]{:S(2)}) collective-permute-start(f32[8,32,128]{2,1,0:T(8,128)} %get-tuple-element.21), channel_id=1, source_target_pairs={{16,0},{32,16},{48,32},{64,48},{80,64},{96,80},{112,96},{128,112},... | collective-permute-start | bytes 393224 | tf_op jit(solution)/shard_map/ppermute | solution.py:15
  12.0 1.2 collective-permute-start.2
  13.1 5.0 %collective-permute-start.3 = (f32[8,32,128]{2,1,0:T(8,128)}, f32[8,32,128]{2,1,0:T(8,128)}, u32[]{:S(2)}, u32[]{:S(2)}) collective-permute-start(f32[8,32,128]{2,1,0:T(8,128)} %get-tuple-element.19), channel_id=1, source_target_pairs={{0,15},{1,0},{2,1},{3,2},{4,3},{5,4},{6,5},{7,6},{8,7},{9,8},{10,9... | collective-permute-start | bytes 393224 | tf_op jit(solution)/shard_map/ppermute | solution.py:21
  18.2 0.7 broadcast_in_dim.418
  18.9 17.2 %all-to-all-start = ((f32[256,1,4]{2,1,0:T(1,128)}), f32[256,1,4]{2,1,0:T(1,128)}, u32[]{:S(2)}, u32[]{:S(2)}) async-start(f32[256,1,4]{2,1,0:T(1,128)} %broadcast_in_dim.418), calls=%async_computation | async-start | bytes 262144 | tf_op jit(solution)/shard_map/all_to_all | solution.py:167
  36.1 0.7 compare_bitcast_fusion.6
  36.8 0.6 compare_bitcast_fusion.5
  37.4 0.7 fusion.104
  38.1 0.6 copy-done.45
  38.7 0.5 compare_and_fusion
  39.2 0.1 copy-done.43
  39.4 0.5 fusion.94
  39.9 1.0 convolution_multiply_fusion.2
  40.9 1.0 convolution_multiply_fusion.1
  42.0 1.0 fusion.7
  43.0 0.6 pad_clamp_fusion
  43.6 0.6 slice.570
  44.2 0.8 copy.49
  45.0 1.5 %copy.50 = f32[64,128]{0,1:T(8,128)} copy(f32[64,128]{1,0:T(8,128)} %convolution_multiply_fusion.1) | data formatting | bytes 65536 | tf_op jit(solution)/shard_map/mul | solution.py:126
  46.5 1.5 %copy.56 = f32[64,128]{0,1:T(8,128)} copy(f32[64,128]{1,0:T(8,128)} %slice.570) | data formatting | bytes 65536 | tf_op jit(solution)/shard_map/slice | solution.py:145
  48.0 0.2 all-to-all-done
  48.2 2.3 %gather_fusion = f32[128,4]{1,0:T(8,128)} fusion(f32[4,256]{0,1:T(8,128)} %bitcast.78, s32[1024]{0:T(1024)} %pad_clamp_fusion), kind=kCustom, calls=%fused_computation | custom fusion | bytes 4608 | tf_op jit(solution)/shard_map/jit(_take)/gather | solution.py:208
  50.5 1.5 %select_bitcast_fusion = f32[4,128]{0,1:T(8,128)} fusion(f32[128,4]{1,0:T(8,128)} %gather_fusion, pred[128]{0:T(512)(128)(4,1)} %compare_and_fusion), kind=kLoop, calls=%fused_computation.207 | loop fusion | flops 512 | bytes 4224 | tf_op jit(solution)/shard_map/jit(_take)/select_n | solution.py:208
  52.0 1.5 %copy.48 = f32[4,128]{1,0:T(4,128)} copy(f32[4,128]{0,1:T(8,128)} %select_bitcast_fusion) | data formatting | bytes 4096 | tf_op jit(solution)/shard_map/jit(_take)/select_n | solution.py:208
  53.5 1.0 broadcast_multiply_fusion.1
  54.6 1.9 %convolution_bitcast_fusion.10 = f32[8,8,32,128]{3,2,1,0:T(8,128)S(1)} fusion(f32[8,32,32,1]{2,1,3,0:T(8,128)S(1)} %copy-done.1, f32[8,32,128]{2,1,0:T(8,128)} %collective-permute-done), kind=kOutput, calls=%fused_computation.19 | convolution fusion | flops 100663296 | bytes 1212416 | tf_op jit(solution)/shard_map/qkj,sjr->qskr/dot_general | solution.py:155
  56.6 0.6 copy-done.25
  57.4 1.9 %convolution_bitcast_fusion.9 = f32[8,8,32,128]{3,2,1,0:T(8,128)S(1)} fusion(f32[8,32,32,1]{2,1,3,0:T(8,128)S(1)} %copy-done.1, f32[8,32,128]{2,1,0:T(8,128)} %collective-permute-done.1), kind=kOutput, calls=%fused_computation.18 | convolution fusion | flops 100663296 | bytes 1212416 | tf_op jit(solution)/shard_map/qkj,sjr->qskr/dot_general | solution.py:155
  59.3 0.6 copy-done.19
  60.2 1.9 %convolution_bitcast_fusion.8 = f32[8,8,32,128]{3,2,1,0:T(8,128)S(1)} fusion(f32[8,32,32,1]{2,1,3,0:T(8,128)S(1)} %copy-done.1, f32[8,32,128]{2,1,0:T(8,128)} %collective-permute-done.2), kind=kOutput, calls=%fused_computation.17 | convolution fusion | flops 100663296 | bytes 1212416 | tf_op jit(solution)/shard_map/qkj,sjr->qskr/dot_general | solution.py:155
  62.1 0.6 copy-done.13
  62.9 1.9 %convolution_bitcast_fusion.7 = f32[8,8,32,128]{3,2,1,0:T(8,128)S(1)} fusion(f32[8,32,32,1]{2,1,3,0:T(8,128)S(1)} %copy-done.1, f32[8,32,128]{2,1,0:T(8,128)} %collective-permute-done.3), kind=kOutput, calls=%fused_computation.16 | convolution fusion | flops 100663296 | bytes 1212416 | tf_op jit(solution)/shard_map/qkj,sjr->qskr/dot_general | solution.py:155
  64.9 0.5 copy-done.12
  65.6 0.9 copy-done.3
  66.6 0.1 multiply_dynamic-update-slice_fusion.14
  66.8 1.9 %fusion.6 = f32[8,256,128]{1,2,0:T(8,128)S(1)} fusion(f32[8,256,128]{1,2,0:T(8,128)S(1)} %fusion.7, f32[8,192,128]{2,1,0:T(8,128)S(1)} %multiply_dynamic-update-slice_fusion.12, f32[256,192,1]{0,1,2:T(8,128)S(1)} %copy-done.2, f32[4,64,128]{1,2,0:T(8,128)S(1)} %get-tuple-element.24, f32[4,64,128]{1,2,0:T(8,128)S(1)} %get-tuple-element.23), kind=kOutput, calls=%fused_computation.15 | convolution fusion | flops 605552640 | bytes 3342336 | tf_op jit(solution)/shard_map/ck,skr->scr/dot_general | solution.py:117
  68.7 1.3 %convolution_bitcast_fusion.12 = f32[8,192,128]{2,1,0:T(8,128)S(1)} fusion(f32[256,192,1]{0,1,2:T(8,128)S(1)} %copy-done.2, f32[8,256,128]{1,2,0:T(8,128)S(1)} %fusion.6, f32[4,256,128]{1,2,0:T(8,128)S(1)} %copy.42, f32[4,256,128]{1,2,0:T(8,128)S(1)} %copy.41), kind=kOutput, calls=%fused_computation.23 | convolution fusion | flops 604766208 | bytes 3080192 | tf_op jit(solution)/shard_map/ck,scr->skr/dot_general | solution.py:107
  70.0 1.0 fusion.8
  71.1 3.3 %collective-permute-start.4 = (f32[8,32,128]{2,1,0:T(8,128)S(1)}, f32[8,32,128]{2,1,0:T(8,128)S(1)}, u32[]{:S(2)}, u32[]{:S(2)}) collective-permute-start(f32[8,32,128]{2,1,0:T(8,128)S(1)} %get-tuple-element.16), channel_id=1, source_target_pairs={{0,16},{16,32},{32,48},{48,64},{64,80},{80,96},{96,112},{112,128},... | collective-permute-start | bytes 393224 | tf_op jit(solution)/shard_map/ppermute | solution.py:15
  74.4 2.1 %collective-permute-start.5 = (f32[8,32,128]{2,1,0:T(8,128)S(1)}, f32[8,32,128]{2,1,0:T(8,128)S(1)}, u32[]{:S(2)}, u32[]{:S(2)}) collective-permute-start(f32[8,32,128]{2,1,0:T(8,128)S(1)} %get-tuple-element.15), channel_id=1, source_target_pairs={{16,0},{32,16},{48,32},{64,48},{80,64},{96,80},{112,96},{128,112},... | collective-permute-start | bytes 393224 | tf_op jit(solution)/shard_map/ppermute | solution.py:15
  76.4 1.3 %collective-permute-start.6 = (f32[8,32,128]{2,1,0:T(8,128)S(1)}, f32[8,32,128]{2,1,0:T(8,128)S(1)}, u32[]{:S(2)}, u32[]{:S(2)}) collective-permute-start(f32[8,32,128]{2,1,0:T(8,128)S(1)} %get-tuple-element.14), channel_id=1, source_target_pairs={{0,1},{1,2},{2,3},{3,4},{4,5},{5,6},{6,7},{7,8},{8,9},{9,10},{10,1... | collective-permute-start | bytes 393224 | tf_op jit(solution)/shard_map/ppermute | solution.py:21
  77.8 4.8 %collective-permute-start.7 = (f32[8,32,128]{2,1,0:T(8,128)S(1)}, f32[8,32,128]{2,1,0:T(8,128)S(1)}, u32[]{:S(2)}, u32[]{:S(2)}) collective-permute-start(f32[8,32,128]{2,1,0:T(8,128)S(1)} %get-tuple-element.13), channel_id=1, source_target_pairs={{0,15},{1,0},{2,1},{3,2},{4,3},{5,4},{6,5},{7,6},{8,7},{9,8},{10,9... | collective-permute-start | bytes 393224 | tf_op jit(solution)/shard_map/ppermute | solution.py:21
  82.7 1.0 convolution_bitcast_fusion.4
  83.8 1.0 convolution_bitcast_fusion.3
  85.0 1.1 collective-permute-done.6
  86.1 1.0 convolution_bitcast_fusion.2
  87.2 1.0 convolution_bitcast_fusion.1
  88.7 1.9 %fusion.4 = f32[8,256,128]{1,2,0:T(8,128)S(1)} fusion(f32[8,256,128]{1,2,0:T(8,128)S(1)} %fusion.6, f32[8,256,128]{1,2,0:T(8,128)S(1)} %fusion.8, f32[8,192,128]{2,1,0:T(8,128)S(1)} %multiply_dynamic-update-slice_fusion, f32[256,192,1]{0,1,2:T(8,128)S(1)} %copy-done.2, f32[4,64,128]{1,2,0:T(8,128)S(1)} %get-tuple-element.24, ...), kind=kOutput, calls=%fused_computation.7 | convolution fusion | flops 606601216 | bytes 5439488 | tf_op jit(solution)/shard_map/ck,skr->scr/dot_general | solution.py:117
  90.6 0.6 fusion.11
  91.3 0.3 fusion.106
  91.6 0.1 copy.71
  91.7 0.7 copy-done.40
  92.4 1.8 %scatter_custom_fusion = f32[256,4]{1,0:T(8,128)} fusion(s32[128]{0:T(128)} %param.27, f32[1,4,128]{1,2,0:T(8,128)S(1)} %copy.71, f32[]{:T(128)} %constant.15.clone.1, f32[128]{0:T(128)S(1)} %copy-done.40), kind=kCustom, calls=%fused_computation.204 | custom fusion | flops 1024 | bytes 7168 | tf_op jit(solution)/shard_map/scatter-add | solution.py:231
  94.2 15.8 %all-to-all-start.1 = ((f32[256,1,4]{2,1,0:T(1,128)}), f32[256,1,4]{2,1,0:T(1,128)S(1)}, u32[]{:S(2)}, u32[]{:S(2)}) async-start(f32[256,1,4]{2,1,0:T(1,128)} %bitcast.129), calls=%async_computation.1 | async-start | bytes 262144 | tf_op jit(solution)/shard_map/all_to_all | solution.py:171
  110.1 1.0 copy.58
  111.1 1.0 copy.59
  112.1 10.9 %all-to-all-done.1 = f32[256,1,4]{2,1,0:T(1,128)S(1)} async-done(((f32[256,1,4]{2,1,0:T(1,128)}), f32[256,1,4]{2,1,0:T(1,128)S(1)}, u32[]{:S(2)}, u32[]{:S(2)}) %all-to-all-start.1) | async-done | bytes 4128 | tf_op jit(solution)/shard_map/all_to_all | solution.py:171
  122.9 0.8 reduce_sum.9
  (127 shorter events, 2.2 us)
Async XLA Ops:
  0.6 39.3 %copy-start = (f32[256,128]{1,0:T(8,128)S(1)}, f32[256,128]{1,0:T(8,128)}, u32[]{:S(2)}) copy-start(f32[256,128]{1,0:T(8,128)} %param.20) | copy-start | bytes 393220
  0.6 1.3 %copy-start.6 = (f32[4,256,128]{2,1,0:T(8,128)S(1)}, f32[4,256,128]{2,1,0:T(8,128)}, u32[]{:S(2)}) copy-start(f32[4,256,128]{2,1,0:T(8,128)} %param.23) | copy-start | bytes 1572868
  2.0 0.9 copy-start.2
  4.9 49.6 %collective-permute-start = (f32[8,32,128]{2,1,0:T(8,128)}, f32[8,32,128]{2,1,0:T(8,128)}, u32[]{:S(2)}, u32[]{:S(2)}) collective-permute-start(f32[8,32,128]{2,1,0:T(8,128)} %get-tuple-element.22), channel_id=1, source_target_pairs={{0,16},{16,32},{32,48},{48,64},{64,80},{80,96},{96,112},{112,128},... | collective-permute-start | bytes 393224 | tf_op jit(solution)/shard_map/ppermute | solution.py:15
  9.5 47.8 %collective-permute-start.1 = (f32[8,32,128]{2,1,0:T(8,128)}, f32[8,32,128]{2,1,0:T(8,128)}, u32[]{:S(2)}, u32[]{:S(2)}) collective-permute-start(f32[8,32,128]{2,1,0:T(8,128)} %get-tuple-element.21), channel_id=1, source_target_pairs={{16,0},{32,16},{48,32},{64,48},{80,64},{96,80},{112,96},{128,112},... | collective-permute-start | bytes 393224 | tf_op jit(solution)/shard_map/ppermute | solution.py:15
  12.0 48.1 %collective-permute-start.2 = (f32[8,32,128]{2,1,0:T(8,128)}, f32[8,32,128]{2,1,0:T(8,128)}, u32[]{:S(2)}, u32[]{:S(2)}) collective-permute-start(f32[8,32,128]{2,1,0:T(8,128)} %get-tuple-element.20), channel_id=1, source_target_pairs={{0,1},{1,2},{2,3},{3,4},{4,5},{5,6},{6,7},{7,8},{8,9},{9,10},{10,1... | collective-permute-start | bytes 393224 | tf_op jit(solution)/shard_map/ppermute | solution.py:21
  13.1 5.0 %copy-start.41 = (f32[4,1]{0,1:T(1,128)S(1)}, f32[4,1]{0,1:T(1,128)}, u32[]{:S(2)}) copy-start(f32[4,1]{0,1:T(1,128)} %param.28) | copy-start | bytes 52
  13.1 49.7 %collective-permute-start.3 = (f32[8,32,128]{2,1,0:T(8,128)}, f32[8,32,128]{2,1,0:T(8,128)}, u32[]{:S(2)}, u32[]{:S(2)}) collective-permute-start(f32[8,32,128]{2,1,0:T(8,128)} %get-tuple-element.19), channel_id=1, source_target_pairs={{0,15},{1,0},{2,1},{3,2},{4,3},{5,4},{6,5},{7,6},{8,7},{9,8},{10,9... | collective-permute-start | bytes 393224 | tf_op jit(solution)/shard_map/ppermute | solution.py:21
  18.9 17.2 %copy-start.11 = (s32[4,128]{1,0:T(4,128)S(1)}, s32[4,128]{1,0:T(4,128)}, u32[]{:S(2)}) copy-start(s32[4,128]{1,0:T(4,128)} %param.26) | copy-start | bytes 6148
  18.9 29.3 %all-to-all-start = ((f32[256,1,4]{2,1,0:T(1,128)}), f32[256,1,4]{2,1,0:T(1,128)}, u32[]{:S(2)}, u32[]{:S(2)}) async-start(f32[256,1,4]{2,1,0:T(1,128)} %broadcast_in_dim.418), calls=%async_computation | async-start | bytes 262144 | tf_op jit(solution)/shard_map/all_to_all | solution.py:167
  37.4 2.5 %copy-start.7 = (f32[256,64]{1,0:T(8,128)S(1)}, f32[256,64]{1,0:T(8,128)}, u32[]{:S(2)}) copy-start(f32[256,64]{1,0:T(8,128)} %constant.83) | copy-start | bytes 196612
  38.1 0.7 copy-start.45
  38.7 0.7 copy-start.43
  38.7 0.7 copy-start.44
  39.9 1.0 copy-start.9
  40.9 1.1 copy-start.4
  53.5 1.0 copy-start.1
  54.6 1.9 %copy-start.28 = (pred[128]{0:T(512)(128)(4,1)S(1)}, pred[128]{0:T(512)(128)(4,1)}, u32[]{:S(2)}) copy-start(pred[128]{0:T(512)(128)(4,1)} %get-tuple-element.29) | copy-start | bytes 388
  54.6 1.9 %copy-start.29 = (pred[128]{0:T(512)(128)(4,1)S(1)}, pred[128]{0:T(512)(128)(4,1)}, u32[]{:S(2)}) copy-start(pred[128]{0:T(512)(128)(4,1)} %get-tuple-element.30) | copy-start | bytes 388
  54.6 1.9 %copy-start.30 = (pred[128]{0:T(512)(128)(4,1)S(1)}, pred[128]{0:T(512)(128)(4,1)}, u32[]{:S(2)}) copy-start(pred[128]{0:T(512)(128)(4,1)} %get-tuple-element.31) | copy-start | bytes 388
  54.6 1.9 %copy-start.39 = (pred[128]{0:T(512)(128)(4,1)S(1)}, pred[128]{0:T(512)(128)(4,1)}, u32[]{:S(2)}) copy-start(pred[128]{0:T(512)(128)(4,1)} %get-tuple-element.51) | copy-start | bytes 388
  56.5 0.7 copy-start.25
  56.5 0.7 copy-start.26
  56.5 0.7 copy-start.27
  57.3 1.9 %copy-start.22 = (pred[128]{0:T(512)(128)(4,1)S(1)}, pred[128]{0:T(512)(128)(4,1)}, u32[]{:S(2)}) copy-start(pred[128]{0:T(512)(128)(4,1)} %get-tuple-element.35) | copy-start | bytes 388
  57.4 1.9 %copy-start.23 = (pred[128]{0:T(512)(128)(4,1)S(1)}, pred[128]{0:T(512)(128)(4,1)}, u32[]{:S(2)}) copy-start(pred[128]{0:T(512)(128)(4,1)} %get-tuple-element.36) | copy-start | bytes 388
  57.4 1.9 %copy-start.24 = (pred[128]{0:T(512)(128)(4,1)S(1)}, pred[128]{0:T(512)(128)(4,1)}, u32[]{:S(2)}) copy-start(pred[128]{0:T(512)(128)(4,1)} %get-tuple-element.37) | copy-start | bytes 388
  57.4 1.9 %copy-start.38 = (pred[128]{0:T(512)(128)(4,1)S(1)}, pred[128]{0:T(512)(128)(4,1)}, u32[]{:S(2)}) copy-start(pred[128]{0:T(512)(128)(4,1)} %get-tuple-element.50) | copy-start | bytes 388
  59.3 0.7 copy-start.19
  59.3 0.7 copy-start.20
  59.3 0.7 copy-start.21
  60.1 1.9 %copy-start.16 = (pred[128]{0:T(512)(128)(4,1)S(1)}, pred[128]{0:T(512)(128)(4,1)}, u32[]{:S(2)}) copy-start(pred[128]{0:T(512)(128)(4,1)} %get-tuple-element.41) | copy-start | bytes 388
  60.1 1.9 %copy-start.17 = (pred[128]{0:T(512)(128)(4,1)S(1)}, pred[128]{0:T(512)(128)(4,1)}, u32[]{:S(2)}) copy-start(pred[128]{0:T(512)(128)(4,1)} %get-tuple-element.42) | copy-start | bytes 388
  60.1 1.9 %copy-start.18 = (pred[128]{0:T(512)(128)(4,1)S(1)}, pred[128]{0:T(512)(128)(4,1)}, u32[]{:S(2)}) copy-start(pred[128]{0:T(512)(128)(4,1)} %get-tuple-element.43) | copy-start | bytes 388
  60.1 1.9 %copy-start.37 = (pred[128]{0:T(512)(128)(4,1)S(1)}, pred[128]{0:T(512)(128)(4,1)}, u32[]{:S(2)}) copy-start(pred[128]{0:T(512)(128)(4,1)} %get-tuple-element.52) | copy-start | bytes 388
  62.0 0.7 copy-start.13
  62.0 0.7 copy-start.14
  62.1 0.7 copy-start.15
  62.9 1.9 %copy-start.33 = (pred[128]{0:T(512)(128)(4,1)S(1)}, pred[128]{0:T(512)(128)(4,1)}, u32[]{:S(2)}) copy-start(pred[128]{0:T(512)(128)(4,1)} %get-tuple-element.46) | copy-start | bytes 388
  62.9 1.9 %copy-start.34 = (pred[128]{0:T(512)(128)(4,1)S(1)}, pred[128]{0:T(512)(128)(4,1)}, u32[]{:S(2)}) copy-start(pred[128]{0:T(512)(128)(4,1)} %get-tuple-element.47) | copy-start | bytes 388
  62.9 1.9 %copy-start.35 = (pred[128]{0:T(512)(128)(4,1)S(1)}, pred[128]{0:T(512)(128)(4,1)}, u32[]{:S(2)}) copy-start(pred[128]{0:T(512)(128)(4,1)} %get-tuple-element.48) | copy-start | bytes 388
  62.9 1.9 %copy-start.36 = (pred[128]{0:T(512)(128)(4,1)S(1)}, pred[128]{0:T(512)(128)(4,1)}, u32[]{:S(2)}) copy-start(pred[128]{0:T(512)(128)(4,1)} %get-tuple-element.49) | copy-start | bytes 388
  64.8 0.6 copy-start.12
  64.8 0.6 copy-start.31
  64.8 0.6 copy-start.32
  65.6 0.9 copy-start.3
  68.6 1.3 %copy-start.5 = (f32[256,256,1]{1,0,2:T(8,128)S(1)}, f32[256,256,1]{1,0,2:T(8,128)}, u32[]{:S(2)}) copy-start(f32[256,256,1]{1,0,2:T(8,128)} %constant.84) | copy-start | bytes 786436
  71.1 11.6 %collective-permute-start.4 = (f32[8,32,128]{2,1,0:T(8,128)S(1)}, f32[8,32,128]{2,1,0:T(8,128)S(1)}, u32[]{:S(2)}, u32[]{:S(2)}) collective-permute-start(f32[8,32,128]{2,1,0:T(8,128)S(1)} %get-tuple-element.16), channel_id=1, source_target_pairs={{0,16},{16,32},{32,48},{48,64},{64,80},{80,96},{96,112},{112,128},... | collective-permute-start | bytes 393224 | tf_op jit(solution)/shard_map/ppermute | solution.py:15
  74.4 9.4 %collective-permute-start.5 = (f32[8,32,128]{2,1,0:T(8,128)S(1)}, f32[8,32,128]{2,1,0:T(8,128)S(1)}, u32[]{:S(2)}, u32[]{:S(2)}) collective-permute-start(f32[8,32,128]{2,1,0:T(8,128)S(1)} %get-tuple-element.15), channel_id=1, source_target_pairs={{16,0},{32,16},{48,32},{64,48},{80,64},{96,80},{112,96},{128,112},... | collective-permute-start | bytes 393224 | tf_op jit(solution)/shard_map/ppermute | solution.py:15
  76.4 9.6 %collective-permute-start.6 = (f32[8,32,128]{2,1,0:T(8,128)S(1)}, f32[8,32,128]{2,1,0:T(8,128)S(1)}, u32[]{:S(2)}, u32[]{:S(2)}) collective-permute-start(f32[8,32,128]{2,1,0:T(8,128)S(1)} %get-tuple-element.14), channel_id=1, source_target_pairs={{0,1},{1,2},{2,3},{3,4},{4,5},{5,6},{6,7},{7,8},{8,9},{9,10},{10,1... | collective-permute-start | bytes 393224 | tf_op jit(solution)/shard_map/ppermute | solution.py:21
  77.8 9.4 %collective-permute-start.7 = (f32[8,32,128]{2,1,0:T(8,128)S(1)}, f32[8,32,128]{2,1,0:T(8,128)S(1)}, u32[]{:S(2)}, u32[]{:S(2)}) collective-permute-start(f32[8,32,128]{2,1,0:T(8,128)S(1)} %get-tuple-element.13), channel_id=1, source_target_pairs={{0,15},{1,0},{2,1},{3,2},{4,3},{5,4},{6,5},{7,6},{8,7},{9,8},{10,9... | collective-permute-start | bytes 393224 | tf_op jit(solution)/shard_map/ppermute | solution.py:21
  88.6 2.0 %copy-start.8 = (f32[64,128]{0,1:T(8,128)S(1)}, f32[64,128]{0,1:T(8,128)}, u32[]{:S(2)}) copy-start(f32[64,128]{0,1:T(8,128)} %copy.56) | copy-start | bytes 98308
  88.6 2.0 %copy-start.10 = (f32[256,64,1]{1,0,2:T(8,128)S(1)}, f32[256,64,1]{1,0,2:T(8,128)}, u32[]{:S(2)}) copy-start(f32[256,64,1]{1,0,2:T(8,128)} %constant.87) | copy-start | bytes 196612
  90.6 0.7 copy-start.42
  91.7 0.7 copy-start.40
  94.2 28.7 %all-to-all-start.1 = ((f32[256,1,4]{2,1,0:T(1,128)}), f32[256,1,4]{2,1,0:T(1,128)S(1)}, u32[]{:S(2)}, u32[]{:S(2)}) async-start(f32[256,1,4]{2,1,0:T(1,128)} %bitcast.129), calls=%async_computation.1 | async-start | bytes 262144 | tf_op jit(solution)/shard_map/all_to_all | solution.py:171

commit v3 on v2

--- a/solution.py
+++ b/solution.py
@@ -148,17 +148,18 @@
     )
 
 
-def reorient(neighbour, codes_face, orient):
+def reorient(sides, codes, orient):
     choices = np.zeros((orient.shape[0], 32, 32), np.float32)
     for code in range(orient.shape[0]):
         choices[code, np.arange(32), orient[code]] = 1.0
     candidates = jnp.einsum(
-        "qkj,sjr->qskr", jnp.asarray(choices), neighbour, precision=lax.Precision.HIGHEST
+        "qkj,fsjr->qfskr", jnp.asarray(choices), jnp.stack(sides, 0),
+        precision=lax.Precision.HIGHEST,
     )
     result = candidates[0]
     for code in range(1, orient.shape[0]):
-        result = jnp.where((codes_face == code)[None, None, :], candidates[code], result)
-    return result
+        result = jnp.where((codes == code)[:, None, None, :], candidates[code], result)
+    return [result[f] for f in range(len(sides))]
 
 
 def gather_blocks(block):
@@ -205,7 +206,10 @@
 ):
     coupling, selects, orient, quadrature = node_tables()
     whole_dirs = gather_blocks(probe_dirs)
-    perturb = jnp.take(whole_dirs, block_map, axis=1)
+    owners = block_map[None, :] == jnp.arange(whole_dirs.shape[1])[:, None]
+    perturb = jnp.einsum(
+        "qb,be->qe", whole_dirs, owners.astype(jnp.float32), precision=lax.Precision.HIGHEST
+    )
     forward_div = divergence(forward_state, coupling, inverse_size)
     adjoint_div = divergence(adjoint_state, coupling, inverse_size)
 
@@ -213,7 +217,7 @@
         from_south, from_north = rims_lat(traces[0], traces[1])
         from_west, from_east = rims_lon(traces[2], traces[3])
         sides = [from_south, from_north, from_west, from_east]
-        horizontal = [reorient(sides[f], face_codes[f], orient) for f in range(4)]
+        horizontal = reorient(sides, face_codes, orient)
         below_trace, above_trace = radial_neighbours(traces[4], traces[5])
         return horizontal + [below_trace, above_trace]
 

time: 125 us -> 113 us (0.904)
  local copies, waits for them, and re-layouts: 19.9 us -> 9.74 us
  waiting for transfers between devices: 12.2 us -> 19.6 us
  starting transfers between devices: 57.7 us -> 53.6 us
  other arithmetic: 9.8 us -> 6.79 us
  matrix products: 22.5 us -> 21.2 us
    all_to_all x1, waiting for transfers between devices: 0.24 us -> 5.09 us  [gather_blocks(): return lax.all_to_all(spread, ('lat', 'lon'), 0, 0, tiled=True).T]
    unnamed x96 -> x44, local copies, waits for them, and re-layouts: 9.21 us -> 4.71 us
    ppermute x4, waiting for transfers between devices: 1.12 us -> 3.69 us  [from_behind(): return lax.ppermute(value, axis, pairs)]
    all_to_all x1, starting transfers between devices: 15.8 us -> 13.3 us  [scatter_sums(): pieces = lax.all_to_all(partial.T, ('lat', 'lon'), 0, 0, tiled=True)]
    gather x1 -> x0, local copies, waits for them, and re-layouts: 2.25 us -> none  [body(): perturb = jnp.take(whole_dirs, block_map, axis=1)]
    dot_general x8 -> x3, matrix products: 11.3 us -> 9.21 us  [the longest x2 8.04 us: reorient(): jnp.einsum('qkj,fsjr->qfskr', jnp.asarray(choices), jnp.stack(sides, 0),...]
    mul x2, local copies, waits for them, and re-layouts: 2.33 us -> 0.81 us  [divergence(): -inverse_size]
    select_n x1 -> x0, local copies, waits for them, and re-layouts: 1.51 us -> none  [body(): perturb = jnp.take(whole_dirs, block_map, axis=1)]
  transfers between devices with their start and end apart: 10 -> 10, of which waited for: 3 -> 3; matrix products, arithmetic and copies ran while one was open for 24% -> 11% of each run, Pallas kernels for 0% -> 0%
where the time goes in v3:
time: 113 us; the launch traced here: 112 us
  starting transfers between devices  53.6 us (47%)
  matrix products  21.2 us (19%)
  waiting for transfers between devices  19.6 us (17%)
  local copies, waits for them, and re-layouts  9.74 us (9%)
  other arithmetic  6.79 us (6%)
  between operations  1.32 us (1%)
    all_to_all x1, starting transfers between devices, gather_blocks(): return lax.all_to_all(spread, ('lat', 'lon'), 0, 0, tiled=True).T  17.2 us
    all_to_all x1, starting transfers between devices, scatter_sums(): pieces = lax.all_to_all(partial.T, ('lat', 'lon'), 0, 0, tiled=True)  13.3 us
    ppermute x4, starting transfers between devices, from_behind(): return lax.ppermute(value, axis, pairs)  11.6 us
    ppermute x4, starting transfers between devices, shifted(): return lax.ppermute(block, axis, route)  11.5 us
    all_to_all x1, waiting for transfers between devices, scatter_sums(): pieces = lax.all_to_all(partial.T, ('lat', 'lon'), 0, 0, tiled=True)  10.8 us
    dot_general x2, matrix products, reorient(): jnp.einsum('qkj,fsjr->qfskr', jnp.asarray(choices), jnp.stack(sides, 0),...  8.04 us
    all_to_all x1, waiting for transfers between devices, gather_blocks(): return lax.all_to_all(spread, ('lat', 'lon'), 0, 0, tiled=True).T  5.09 us
    unnamed x44, local copies, waits for them, and re-layouts  4.71 us
  transfers between devices with their start and end apart: 10, of which 3 were waited for; matrix products, arithmetic and copies ran while one was open for 11% of the time, Pallas kernels for 0%

profile of v3, /device:TPU:1, one launch (start us, length us, event | category | flops | bytes accessed | tf_op | source)
XLA Modules:
  0.0 112.2 jit_solution(10495657736123342183)
XLA Ops:
  0.6 0.0 copy-start
  0.6 0.0 copy-start.4
  0.7 0.0 copy-start.5
  0.7 1.4 %copy.28 = f32[4,256,128]{1,2,0:T(8,128)S(1)} copy(f32[4,256,128]{2,1,0:T(8,128)} %param.16) | data formatting | bytes 1048576 | tf_op args[2]
  2.1 0.0 copy-start.15
  2.1 1.2 %copy.29 = f32[4,256,128]{1,2,0:T(8,128)S(1)} copy(f32[4,256,128]{2,1,0:T(8,128)} %param.17) | data formatting | bytes 1048576 | tf_op args[3]
  3.3 2.2 %convolution_bitcast_fusion.7 = f32[8,192,128]{2,1,0:T(8,128)S(1)} fusion(f32[256,192,1]{0,1,2:T(8,128)} %constant.69, f32[4,256,128]{1,2,0:T(8,128)S(1)} %copy.29, f32[4,256,128]{1,2,0:T(8,128)S(1)} %copy.28), kind=kOutput, calls=%fused_computation.17 | convolution fusion | flops 604241920 | bytes 2031616 | tf_op jit(solution)/shard_map/ck,scr->skr/dot_general | solution.py:107
  5.5 0.8 fusion.70
  6.3 4.6 %collective-permute-start = (f32[8,32,128]{2,1,0:T(8,128)}, f32[8,32,128]{2,1,0:T(8,128)}, u32[]{:S(2)}, u32[]{:S(2)}) collective-permute-start(f32[8,32,128]{2,1,0:T(8,128)} %get-tuple-element.19), channel_id=1, source_target_pairs={{0,16},{16,32},{32,48},{48,64},{64,80},{80,96},{96,112},{112,128},... | collective-permute-start | bytes 393224 | tf_op jit(solution)/shard_map/ppermute | solution.py:15
  10.9 2.5 %collective-permute-start.1 = (f32[8,32,128]{2,1,0:T(8,128)}, f32[8,32,128]{2,1,0:T(8,128)}, u32[]{:S(2)}, u32[]{:S(2)}) collective-permute-start(f32[8,32,128]{2,1,0:T(8,128)} %get-tuple-element.22), channel_id=1, source_target_pairs={{16,0},{32,16},{48,32},{64,48},{80,64},{96,80},{112,96},{128,112},... | collective-permute-start | bytes 393224 | tf_op jit(solution)/shard_map/ppermute | solution.py:15
  13.3 1.2 %collective-permute-start.2 = (f32[8,32,128]{2,1,0:T(8,128)}, f32[8,32,128]{2,1,0:T(8,128)}, u32[]{:S(2)}, u32[]{:S(2)}) collective-permute-start(f32[8,32,128]{2,1,0:T(8,128)} %get-tuple-element.21), channel_id=1, source_target_pairs={{0,1},{1,2},{2,3},{3,4},{4,5},{5,6},{6,7},{7,8},{8,9},{9,10},{10,1... | collective-permute-start | bytes 393224 | tf_op jit(solution)/shard_map/ppermute | solution.py:21
  14.5 5.0 %collective-permute-start.3 = (f32[8,32,128]{2,1,0:T(8,128)}, f32[8,32,128]{2,1,0:T(8,128)}, u32[]{:S(2)}, u32[]{:S(2)}) collective-permute-start(f32[8,32,128]{2,1,0:T(8,128)} %get-tuple-element.20), channel_id=1, source_target_pairs={{0,15},{1,0},{2,1},{3,2},{4,3},{5,4},{6,5},{7,6},{8,7},{9,8},{10,9... | collective-permute-start | bytes 393224 | tf_op jit(solution)/shard_map/ppermute | solution.py:21
  19.5 0.7 broadcast_in_dim.176
  20.2 17.2 %all-to-all-start = ((f32[256,1,4]{2,1,0:T(1,128)}), f32[256,1,4]{2,1,0:T(1,128)}, u32[]{:S(2)}, u32[]{:S(2)}) async-start(f32[256,1,4]{2,1,0:T(1,128)} %broadcast_in_dim.176), calls=%async_computation | async-start | bytes 262144 | tf_op jit(solution)/shard_map/all_to_all | solution.py:168
  37.4 0.1 fusion.69
  37.6 0.5 fusion.57
  38.1 0.4 convolution_multiply_fusion.2
  38.5 0.4 convolution_multiply_fusion.1
  38.9 0.1 broadcast_select_fusion
  39.0 1.9 %fusion.7 = f32[8,256,128]{1,2,0:T(8,128)S(1)} fusion(f32[256,256,1]{1,0,2:T(8,128)} %constant.68, f32[256,128]{0,1:T(8,128)S(1)} %broadcast_select_fusion, f32[4,256,128]{1,2,0:T(8,128)S(1)} %copy.29, f32[4,256,128]{1,2,0:T(8,128)S(1)} %copy.28), kind=kOutput, calls=%fused_computation.14 | convolution fusion | flops 805830656 | bytes 2490368 | tf_op jit(solution)/shard_map/cd,scr->sdr/dot_general | solution.py:78
  40.9 0.6 broadcast_compare_fusion.6
  41.5 1.4 %slice.390 = f32[64,128]{1,0:T(8,128)} slice(f32[256,128]{1,0:T(8,128)} %param.15), slice={[0:64], [0:128]} | slice | bytes 65536 | tf_op jit(solution)/shard_map/slice | solution.py:145
  42.9 0.1 copy.32
  43.0 0.7 copy.33
  43.7 0.8 copy.36
  44.6 5.1 %all-to-all-done = f32[256,1,4]{2,1,0:T(1,128)} async-done(((f32[256,1,4]{2,1,0:T(1,128)}), f32[256,1,4]{2,1,0:T(1,128)}, u32[]{:S(2)}, u32[]{:S(2)}) %all-to-all-start) | async-done | bytes 4128 | tf_op jit(solution)/shard_map/all_to_all | solution.py:168
  49.7 1.2 %convolution_bitcast_fusion.8 = f32[4,128]{1,0:T(4,128)S(1)} fusion(f32[256,4]{1,0:T(8,128)} %bitcast.26, s32[128]{0:T(128)} %param.21), kind=kOutput, calls=%fused_computation.24 | convolution fusion | flops 1605632 | bytes 6656 | tf_op jit(solution)/shard_map/qb,be->qe/dot_general | solution.py:210
  50.9 1.0 broadcast_multiply_fusion.1
  51.9 0.0 collective-permute-done.1
  51.9 0.0 collective-permute-done.2
  51.9 4.6 %convolution_bitcast_fusion.1 = f32[8,4,8,32,128]{4,3,2,1,0:T(8,128)S(1)} fusion(f32[8,32,32,1,1]{2,1,4,3,0:T(8,128)} %constant.70, f32[1,8,32,128]{3,2,1,0:T(8,128)} %bitcast.7, f32[1,8,32,128]{3,2,1,0:T(8,128)} %bitcast.6, f32[1,8,32,128]{3,2,1,0:T(8,128)} %bitcast.5, f32[1,8,32,128]{3,2,1,0:T(8,128)} %bitcast.4), kind=kOutput, calls=%fused_computation.2 | convolution fusion | flops 403046400 | bytes 4751360 | tf_op jit(solution)/shard_map/qkj,fsjr->qfskr/dot_general | solution.py:155
  56.6 0.0 copy-start.1
  56.6 0.5 fusion.25
  57.4 0.0 copy-start.2
  57.4 0.1 multiply_dynamic-update-slice_fusion.15
  57.5 0.1 multiply_dynamic-update-slice_fusion.14
  57.7 1.9 %fusion.6 = f32[8,256,128]{1,2,0:T(8,128)S(1)} fusion(f32[8,256,128]{1,2,0:T(8,128)S(1)} %fusion.7, f32[8,192,128]{2,1,0:T(8,128)S(1)} %multiply_dynamic-update-slice_fusion.12, f32[256,192,1]{0,1,2:T(8,128)S(1)} %copy-done.1, f32[4,64,128]{1,2,0:T(8,128)S(1)} %get-tuple-element.32, f32[4,64,128]{1,2,0:T(8,128)S(1)} %get-tuple-element.31), kind=kOutput, calls=%fused_computation.12 | convolution fusion | flops 605552640 | bytes 3342336 | tf_op jit(solution)/shard_map/ck,skr->scr/dot_general | solution.py:117
  59.6 0.0 copy-start.3
  59.6 1.3 %convolution_bitcast_fusion.6 = f32[8,192,128]{2,1,0:T(8,128)S(1)} fusion(f32[256,192,1]{0,1,2:T(8,128)S(1)} %copy-done.1, f32[8,256,128]{1,2,0:T(8,128)S(1)} %fusion.6, f32[4,256,128]{1,2,0:T(8,128)S(1)} %copy.29, f32[4,256,128]{1,2,0:T(8,128)S(1)} %copy.28), kind=kOutput, calls=%fused_computation.16 | convolution fusion | flops 604766208 | bytes 3080192 | tf_op jit(solution)/shard_map/ck,scr->skr/dot_general | solution.py:107
  61.0 1.0 fusion.8
  62.0 2.6 %collective-permute-start.4 = (f32[8,32,128]{2,1,0:T(8,128)S(1)}, f32[8,32,128]{2,1,0:T(8,128)S(1)}, u32[]{:S(2)}, u32[]{:S(2)}) collective-permute-start(f32[8,32,128]{2,1,0:T(8,128)S(1)} %get-tuple-element.13), channel_id=1, source_target_pairs={{0,16},{16,32},{32,48},{48,64},{64,80},{80,96},{96,112},{112,128},... | collective-permute-start | bytes 393224 | tf_op jit(solution)/shard_map/ppermute | solution.py:15
  64.6 1.9 %collective-permute-start.5 = (f32[8,32,128]{2,1,0:T(8,128)S(1)}, f32[8,32,128]{2,1,0:T(8,128)S(1)}, u32[]{:S(2)}, u32[]{:S(2)}) collective-permute-start(f32[8,32,128]{2,1,0:T(8,128)S(1)} %get-tuple-element.16), channel_id=1, source_target_pairs={{16,0},{32,16},{48,32},{64,48},{80,64},{96,80},{112,96},{128,112},... | collective-permute-start | bytes 393224 | tf_op jit(solution)/shard_map/ppermute | solution.py:15
  66.5 0.8 collective-permute-start.6
  67.3 4.7 %collective-permute-start.7 = (f32[8,32,128]{2,1,0:T(8,128)S(1)}, f32[8,32,128]{2,1,0:T(8,128)S(1)}, u32[]{:S(2)}, u32[]{:S(2)}) collective-permute-start(f32[8,32,128]{2,1,0:T(8,128)S(1)} %get-tuple-element.14), channel_id=1, source_target_pairs={{0,15},{1,0},{2,1},{3,2},{4,3},{5,4},{6,5},{7,6},{8,7},{9,8},{10,9... | collective-permute-start | bytes 393224 | tf_op jit(solution)/shard_map/ppermute | solution.py:21
  72.0 0.1 fusion.67
  72.1 3.7 %collective-permute-done.6 = f32[8,32,128]{2,1,0:T(8,128)S(1)} collective-permute-done((f32[8,32,128]{2,1,0:T(8,128)S(1)}, f32[8,32,128]{2,1,0:T(8,128)S(1)}, u32[]{:S(2)}, u32[]{:S(2)}) %collective-permute-start.6) | collective-permute-done | bytes 131104 | tf_op jit(solution)/shard_map/ppermute | solution.py:21
  75.8 3.4 %convolution_bitcast_fusion = f32[8,4,8,32,128]{4,3,2,1,0:T(8,128)S(1)} fusion(f32[8,32,32,1,1]{2,1,4,3,0:T(8,128)S(1)} %copy-done.3, f32[1,8,32,128]{3,2,1,0:T(8,128)S(1)} %bitcast.203, f32[1,8,32,128]{3,2,1,0:T(8,128)S(1)} %bitcast.202, f32[1,8,32,128]{3,2,1,0:T(8,128)S(1)} %bitcast.201, f32[1,8,32,128]{3,2,1,0:T(8,128)S(1)} %bitcast.200), kind=kOutput, calls=%fused_computation.1 | convolution fusion | flops 403046400 | bytes 4751360 | tf_op jit(solution)/shard_map/qkj,fsjr->qfskr/dot_general | solution.py:155
  79.3 0.5 fusion.18
  79.9 0.0 copy-start.6
  80.0 0.0 copy-start.17
  80.1 0.0 copy-start.14
  80.1 0.1 multiply_dynamic-update-slice_fusion.3
  80.2 0.1 multiply_dynamic-update-slice_fusion.2
  80.4 2.0 %fusion.4 = f32[8,256,128]{1,2,0:T(8,128)S(1)} fusion(f32[8,256,128]{1,2,0:T(8,128)S(1)} %fusion.6, f32[8,256,128]{1,2,0:T(8,128)S(1)} %fusion.8, f32[8,192,128]{2,1,0:T(8,128)S(1)} %multiply_dynamic-update-slice_fusion, f32[256,192,1]{0,1,2:T(8,128)S(1)} %copy-done.1, f32[4,64,128]{1,2,0:T(8,128)S(1)} %get-tuple-element.32, ...), kind=kOutput, calls=%fused_computation.8 | convolution fusion | flops 606601216 | bytes 5439488 | tf_op jit(solution)/shard_map/ck,skr->scr/dot_general | solution.py:117
  82.4 0.6 fusion.11
  83.0 0.3 fusion.71
  83.3 0.1 copy.45
  83.5 1.8 %scatter_custom_fusion = f32[256,4]{1,0:T(8,128)} fusion(s32[128]{0:T(128)} %param.21, f32[1,4,128]{1,2,0:T(8,128)S(1)} %copy.45, f32[]{:T(128)} %constant.11.clone.1, f32[128]{0:T(128)S(1)} %copy-done.14), kind=kCustom, calls=%fused_computation.123 | custom fusion | flops 1024 | bytes 7168 | tf_op jit(solution)/shard_map/scatter-add | solution.py:235
  85.3 13.3 %all-to-all-start.1 = ((f32[256,1,4]{2,1,0:T(1,128)}), f32[256,1,4]{2,1,0:T(1,128)S(1)}, u32[]{:S(2)}, u32[]{:S(2)}) async-start(f32[256,1,4]{2,1,0:T(1,128)} %bitcast.56), calls=%async_computation.1 | async-start | bytes 262144 | tf_op jit(solution)/shard_map/all_to_all | solution.py:172
  98.5 0.1 fusion.66
  98.6 1.0 copy.38
  99.6 1.0 copy.39
  100.6 10.8 %all-to-all-done.1 = f32[256,1,4]{2,1,0:T(1,128)S(1)} async-done(((f32[256,1,4]{2,1,0:T(1,128)}), f32[256,1,4]{2,1,0:T(1,128)S(1)}, u32[]{:S(2)}, u32[]{:S(2)}) %all-to-all-start.1) | async-done | bytes 4128 | tf_op jit(solution)/shard_map/all_to_all | solution.py:172
  111.4 0.8 reduce_sum.9
  (59 shorter events, 0.7 us)
Async XLA Ops:
  0.6 37.5 %copy-start = (f32[256,128]{1,0:T(8,128)S(1)}, f32[256,128]{1,0:T(8,128)}, u32[]{:S(2)}) copy-start(f32[256,128]{1,0:T(8,128)} %param.14) | copy-start | bytes 393220
  0.6 37.4 %copy-start.4 = (f32[256,64]{1,0:T(8,128)S(1)}, f32[256,64]{1,0:T(8,128)}, u32[]{:S(2)}) copy-start(f32[256,64]{1,0:T(8,128)} %constant.67) | copy-start | bytes 196612
  0.7 18.9 %copy-start.16 = (f32[4,1]{0,1:T(1,128)S(1)}, f32[4,1]{0,1:T(1,128)}, u32[]{:S(2)}) copy-start(f32[4,1]{0,1:T(1,128)} %param.22) | copy-start | bytes 52
  0.7 36.9 %copy-start.19 = (f32[128]{0:T(128)S(1)}, f32[128]{0:T(128)}, u32[]{:S(2)}) copy-start(f32[128]{0:T(128)} %param.18) | copy-start | bytes 1540
  0.7 36.9 %copy-start.18 = (f32[128]{0:T(128)S(1)}, f32[128]{0:T(128)}, u32[]{:S(2)}) copy-start(f32[128]{0:T(128)} %param.19) | copy-start | bytes 1540
  0.7 37.8 %copy-start.5 = (f32[256,128]{1,0:T(8,128)S(1)}, f32[256,128]{1,0:T(8,128)}, u32[]{:S(2)}) copy-start(f32[256,128]{1,0:T(8,128)} %param.15) | copy-start | bytes 393220
  2.1 38.8 %copy-start.15 = (s32[4,128]{1,0:T(4,128)S(1)}, s32[4,128]{1,0:T(4,128)}, u32[]{:S(2)}) copy-start(s32[4,128]{1,0:T(4,128)} %param.20) | copy-start | bytes 6148
  6.3 45.6 %collective-permute-start = (f32[8,32,128]{2,1,0:T(8,128)}, f32[8,32,128]{2,1,0:T(8,128)}, u32[]{:S(2)}, u32[]{:S(2)}) collective-permute-start(f32[8,32,128]{2,1,0:T(8,128)} %get-tuple-element.19), channel_id=1, source_target_pairs={{0,16},{16,32},{32,48},{48,64},{64,80},{80,96},{96,112},{112,128},... | collective-permute-start | bytes 393224 | tf_op jit(solution)/shard_map/ppermute | solution.py:15
  10.9 41.0 %collective-permute-start.1 = (f32[8,32,128]{2,1,0:T(8,128)}, f32[8,32,128]{2,1,0:T(8,128)}, u32[]{:S(2)}, u32[]{:S(2)}) collective-permute-start(f32[8,32,128]{2,1,0:T(8,128)} %get-tuple-element.22), channel_id=1, source_target_pairs={{16,0},{32,16},{48,32},{64,48},{80,64},{96,80},{112,96},{128,112},... | collective-permute-start | bytes 393224 | tf_op jit(solution)/shard_map/ppermute | solution.py:15
  13.3 38.5 %collective-permute-start.2 = (f32[8,32,128]{2,1,0:T(8,128)}, f32[8,32,128]{2,1,0:T(8,128)}, u32[]{:S(2)}, u32[]{:S(2)}) collective-permute-start(f32[8,32,128]{2,1,0:T(8,128)} %get-tuple-element.21), channel_id=1, source_target_pairs={{0,1},{1,2},{2,3},{3,4},{4,5},{5,6},{6,7},{7,8},{8,9},{9,10},{10,1... | collective-permute-start | bytes 393224 | tf_op jit(solution)/shard_map/ppermute | solution.py:21
  14.5 37.4 %collective-permute-start.3 = (f32[8,32,128]{2,1,0:T(8,128)}, f32[8,32,128]{2,1,0:T(8,128)}, u32[]{:S(2)}, u32[]{:S(2)}) collective-permute-start(f32[8,32,128]{2,1,0:T(8,128)} %get-tuple-element.20), channel_id=1, source_target_pairs={{0,15},{1,0},{2,1},{3,2},{4,3},{5,4},{6,5},{7,6},{8,7},{9,8},{10,9... | collective-permute-start | bytes 393224 | tf_op jit(solution)/shard_map/ppermute | solution.py:21
  20.2 29.4 %all-to-all-start = ((f32[256,1,4]{2,1,0:T(1,128)}), f32[256,1,4]{2,1,0:T(1,128)}, u32[]{:S(2)}, u32[]{:S(2)}) async-start(f32[256,1,4]{2,1,0:T(1,128)} %broadcast_in_dim.176), calls=%async_computation | async-start | bytes 262144 | tf_op jit(solution)/shard_map/all_to_all | solution.py:168
  49.7 6.8 %copy-start.7 = (pred[4,128]{1,0:T(4,128)(4,1)S(1)}, pred[4,128]{1,0:T(4,128)(4,1)}, u32[]{:S(2)}) copy-start(pred[4,128]{1,0:T(4,128)(4,1)} %get-tuple-element.33) | copy-start | bytes 1540
  49.7 6.9 %copy-start.8 = (pred[4,128]{1,0:T(4,128)(4,1)S(1)}, pred[4,128]{1,0:T(4,128)(4,1)}, u32[]{:S(2)}) copy-start(pred[4,128]{1,0:T(4,128)(4,1)} %get-tuple-element.34) | copy-start | bytes 1540
  49.7 6.9 %copy-start.9 = (pred[4,128]{1,0:T(4,128)(4,1)S(1)}, pred[4,128]{1,0:T(4,128)(4,1)}, u32[]{:S(2)}) copy-start(pred[4,128]{1,0:T(4,128)(4,1)} %get-tuple-element.35) | copy-start | bytes 1540
  49.7 6.9 %copy-start.10 = (pred[4,128]{1,0:T(4,128)(4,1)S(1)}, pred[4,128]{1,0:T(4,128)(4,1)}, u32[]{:S(2)}) copy-start(pred[4,128]{1,0:T(4,128)(4,1)} %get-tuple-element.36) | copy-start | bytes 1540
  49.7 6.9 %copy-start.11 = (pred[4,128]{1,0:T(4,128)(4,1)S(1)}, pred[4,128]{1,0:T(4,128)(4,1)}, u32[]{:S(2)}) copy-start(pred[4,128]{1,0:T(4,128)(4,1)} %get-tuple-element.37) | copy-start | bytes 1540
  49.7 6.9 %copy-start.12 = (pred[4,128]{1,0:T(4,128)(4,1)S(1)}, pred[4,128]{1,0:T(4,128)(4,1)}, u32[]{:S(2)}) copy-start(pred[4,128]{1,0:T(4,128)(4,1)} %get-tuple-element.38) | copy-start | bytes 1540
  49.7 6.9 %copy-start.13 = (pred[4,128]{1,0:T(4,128)(4,1)S(1)}, pred[4,128]{1,0:T(4,128)(4,1)}, u32[]{:S(2)}) copy-start(pred[4,128]{1,0:T(4,128)(4,1)} %get-tuple-element.39) | copy-start | bytes 1540
  56.6 1.1 %copy-start.1 = (f32[256,192,1]{0,1,2:T(8,128)S(1)}, f32[256,192,1]{0,1,2:T(8,128)}, u32[]{:S(2)}) copy-start(f32[256,192,1]{0,1,2:T(8,128)} %constant.69) | copy-start | bytes 589828
  57.4 3.6 %copy-start.2 = (f32[256,256,1]{1,0,2:T(8,128)S(1)}, f32[256,256,1]{1,0,2:T(8,128)}, u32[]{:S(2)}) copy-start(f32[256,256,1]{1,0,2:T(8,128)} %constant.68) | copy-start | bytes 786436
  59.6 16.2 %copy-start.3 = (f32[8,32,32,1,1]{2,1,4,3,0:T(8,128)S(1)}, f32[8,32,32,1,1]{2,1,4,3,0:T(8,128)}, u32[]{:S(2)}) copy-start(f32[8,32,32,1,1]{2,1,4,3,0:T(8,128)} %constant.70) | copy-start | bytes 98308
  62.0 10.1 %collective-permute-start.4 = (f32[8,32,128]{2,1,0:T(8,128)S(1)}, f32[8,32,128]{2,1,0:T(8,128)S(1)}, u32[]{:S(2)}, u32[]{:S(2)}) collective-permute-start(f32[8,32,128]{2,1,0:T(8,128)S(1)} %get-tuple-element.13), channel_id=1, source_target_pairs={{0,16},{16,32},{32,48},{48,64},{64,80},{80,96},{96,112},{112,128},... | collective-permute-start | bytes 393224 | tf_op jit(solution)/shard_map/ppermute | solution.py:15
  64.6 7.5 %collective-permute-start.5 = (f32[8,32,128]{2,1,0:T(8,128)S(1)}, f32[8,32,128]{2,1,0:T(8,128)S(1)}, u32[]{:S(2)}, u32[]{:S(2)}) collective-permute-start(f32[8,32,128]{2,1,0:T(8,128)S(1)} %get-tuple-element.16), channel_id=1, source_target_pairs={{16,0},{32,16},{48,32},{64,48},{80,64},{96,80},{112,96},{128,112},... | collective-permute-start | bytes 393224 | tf_op jit(solution)/shard_map/ppermute | solution.py:15
  66.5 9.3 %collective-permute-start.6 = (f32[8,32,128]{2,1,0:T(8,128)S(1)}, f32[8,32,128]{2,1,0:T(8,128)S(1)}, u32[]{:S(2)}, u32[]{:S(2)}) collective-permute-start(f32[8,32,128]{2,1,0:T(8,128)S(1)} %get-tuple-element.15), channel_id=1, source_target_pairs={{0,1},{1,2},{2,3},{3,4},{4,5},{5,6},{6,7},{7,8},{8,9},{9,10},{10,1... | collective-permute-start | bytes 393224 | tf_op jit(solution)/shard_map/ppermute | solution.py:21
  67.3 8.5 %collective-permute-start.7 = (f32[8,32,128]{2,1,0:T(8,128)S(1)}, f32[8,32,128]{2,1,0:T(8,128)S(1)}, u32[]{:S(2)}, u32[]{:S(2)}) collective-permute-start(f32[8,32,128]{2,1,0:T(8,128)S(1)} %get-tuple-element.14), channel_id=1, source_target_pairs={{0,15},{1,0},{2,1},{3,2},{4,3},{5,4},{6,5},{7,6},{8,7},{9,8},{10,9... | collective-permute-start | bytes 393224 | tf_op jit(solution)/shard_map/ppermute | solution.py:21
  79.9 2.4 %copy-start.6 = (f32[256,64,1]{1,0,2:T(8,128)S(1)}, f32[256,64,1]{1,0,2:T(8,128)}, u32[]{:S(2)}) copy-start(f32[256,64,1]{1,0,2:T(8,128)} %constant.71) | copy-start | bytes 196612
  80.0 2.9 %copy-start.17 = (f32[64,1,1]{0,1,2:T(1,128)S(1)}, f32[64,1,1]{0,1,2:T(1,128)}, u32[]{:S(2)}) copy-start(f32[64,1,1]{0,1,2:T(1,128)} %constant.72) | copy-start | bytes 772
  80.1 3.4 %copy-start.14 = (f32[128]{0:T(128)S(1)}, f32[128]{0:T(128)}, u32[]{:S(2)}) copy-start(f32[128]{0:T(128)} %get-tuple-element.40) | copy-start | bytes 1540
  85.3 26.2 %all-to-all-start.1 = ((f32[256,1,4]{2,1,0:T(1,128)}), f32[256,1,4]{2,1,0:T(1,128)S(1)}, u32[]{:S(2)}, u32[]{:S(2)}) async-start(f32[256,1,4]{2,1,0:T(1,128)} %bitcast.56), calls=%async_computation.1 | async-start | bytes 262144 | tf_op jit(solution)/shard_map/all_to_all | solution.py:172

commit v4 on v3

--- a/solution.py
+++ b/solution.py
@@ -148,18 +148,24 @@
     )
 
 
+def face_map(kind):
+    picks = np.zeros((32, 32), np.float32)
+    for part in range(2):
+        for u in range(4):
+            for v in range(4):
+                su, sv = {"v": (u, 3 - v), "u": (3 - u, v), "t": (v, u)}[kind]
+                picks[16 * part + 4 * u + v, 16 * part + 4 * su + sv] = 1.0
+    return jnp.asarray(picks)
+
+
 def reorient(sides, codes, orient):
-    choices = np.zeros((orient.shape[0], 32, 32), np.float32)
-    for code in range(orient.shape[0]):
-        choices[code, np.arange(32), orient[code]] = 1.0
-    candidates = jnp.einsum(
-        "qkj,fsjr->qfskr", jnp.asarray(choices), jnp.stack(sides, 0),
-        precision=lax.Precision.HIGHEST,
-    )
-    result = candidates[0]
-    for code in range(1, orient.shape[0]):
-        result = jnp.where((codes == code)[:, None, None, :], candidates[code], result)
-    return [result[f] for f in range(len(sides))]
+    stacked = jnp.stack(sides, 0)
+    for bit, kind in ((2, "v"), (1, "u"), (0, "t")):
+        moved = jnp.einsum(
+            "kj,fsjr->fskr", face_map(kind), stacked, precision=lax.Precision.HIGHEST
+        )
+        stacked = jnp.where(((codes & (1 << bit)) != 0)[:, None, None, :], moved, stacked)
+    return [stacked[f] for f in range(len(sides))]
 
 
 def gather_blocks(block):
@@ -232,9 +238,9 @@
     element_terms = sensitivity(
         new_forward, new_adjoint, forward_div, adjoint_state, inverse_size, coupling, quadrature
     )
-    partial_sums = jax.ops.segment_sum(
-        element_terms.T, block_map, num_segments=whole_dirs.shape[1]
-    ).T
+    partial_sums = jnp.einsum(
+        "qe,be->qb", element_terms, owners.astype(jnp.float32), precision=lax.Precision.HIGHEST
+    )
     hess_vec = scatter_sums(partial_sums)
     return (new_forward, new_adjoint, hess_vec)
 

time: 113 us -> 112 us (level)
  local copies, waits for them, and re-layouts: 9.74 us -> 15.9 us
  other arithmetic: 6.79 us -> 3.02 us
  matrix products: 21.2 us -> 18 us
  waiting for transfers between devices: 19.6 us -> 16.7 us
  starting transfers between devices: 53.6 us -> 56.4 us
    unnamed x44 -> x52, local copies, waits for them, and re-layouts: 4.71 us -> 9.05 us
    all_to_all x1, waiting for transfers between devices: 5.09 us -> 2.18 us  [gather_blocks(): return lax.all_to_all(spread, ('lat', 'lon'), 0, 0, tiled=True).T]
    all_to_all x1, starting transfers between devices: 13.3 us -> 16 us  [scatter_sums(): pieces = lax.all_to_all(partial.T, ('lat', 'lon'), 0, 0, tiled=True)]
    dot_general x2 -> x7, matrix products: 8.04 us -> 5.56 us  [the longest x6 4.71 us: reorient(): jnp.einsum('kj,fsjr->fskr', face_map(kind), stacked, precision=lax.Precis...]
    scatter-add x1 -> x0, other arithmetic: 1.82 us -> none  [body(): jax.ops.segment_sum(element_terms.T, block_map, num_segments=whole_dirs.s...]
    mul x2, local copies, waits for them, and re-layouts: 0.81 us -> 2.33 us  [divergence(): -inverse_size]
    dot_general x3, matrix products: 1.34 us -> 2.55 us  [divergence(): jnp.einsum('cn,...cr->...nr', coupling[:, :64], field_state, precision=la...]
  transfers between devices with their start and end apart: 10 -> 10, of which waited for: 3 -> 3; matrix products, arithmetic and copies ran while one was open for 11% -> 12% of each run, Pallas kernels for 0% -> 0%
where the time goes in v4:
time: 112 us; the launch traced here: 111 us
  starting transfers between devices  56.4 us (50%)
  matrix products  18 us (16%)
  waiting for transfers between devices  16.7 us (15%)
  local copies, waits for them, and re-layouts  15.9 us (14%)
  other arithmetic  3.02 us (3%)
  between operations  1.24 us (1%)
    all_to_all x1, starting transfers between devices, gather_blocks(): return lax.all_to_all(spread, ('lat', 'lon'), 0, 0, tiled=True).T  17.2 us
    all_to_all x1, starting transfers between devices, scatter_sums(): pieces = lax.all_to_all(partial.T, ('lat', 'lon'), 0, 0, tiled=True)  16 us
    ppermute x4, starting transfers between devices, from_behind(): return lax.ppermute(value, axis, pairs)  11.6 us
    ppermute x4, starting transfers between devices, shifted(): return lax.ppermute(block, axis, route)  11.5 us
    all_to_all x1, waiting for transfers between devices, scatter_sums(): pieces = lax.all_to_all(partial.T, ('lat', 'lon'), 0, 0, tiled=True)  10.8 us
    unnamed x52, local copies, waits for them, and re-layouts  9.05 us
    dot_general x6, matrix products, reorient(): jnp.einsum('kj,fsjr->fskr', face_map(kind), stacked, precision=lax.Precis...  4.71 us
    dot_general x2, matrix products, rate_of(): jnp.einsum('ck,skr->scr', selects, face_rates, precision=lax.Precision.HI...  3.81 us
  transfers between devices with their start and end apart: 10, of which 3 were waited for; matrix products, arithmetic and copies ran while one was open for 12% of the time, Pallas kernels for 0%

profile of v4, /device:TPU:1, one launch (start us, length us, event | category | flops | bytes accessed | tf_op | source)
XLA Modules:
  0.0 111.2 jit_solution(276214103886783353)
XLA Ops:
  0.7 1.3 %copy.30 = f32[4,256,128]{1,2,0:T(8,128)S(1)} copy(f32[4,256,128]{2,1,0:T(8,128)} %param.20) | data formatting | bytes 1048576 | tf_op args[2]
  2.0 0.2 copy.31
  2.2 0.7 copy-done.1
  2.9 1.2 %convolution_bitcast_fusion.5 = f32[8,192,128]{2,1,0:T(8,128)S(1)} fusion(f32[256,192,1]{0,1,2:T(8,128)S(1)} %copy-done.1, f32[4,256,128]{1,2,0:T(8,128)S(1)} %copy.31, f32[4,256,128]{1,2,0:T(8,128)S(1)} %copy.30), kind=kOutput, calls=%fused_computation.14 | convolution fusion | flops 604241920 | bytes 2031616 | tf_op jit(solution)/shard_map/ck,scr->skr/dot_general | solution.py:107
  4.1 0.8 fusion.64
  4.9 4.6 %collective-permute-start = (f32[8,32,128]{2,1,0:T(8,128)}, f32[8,32,128]{2,1,0:T(8,128)}, u32[]{:S(2)}, u32[]{:S(2)}) collective-permute-start(f32[8,32,128]{2,1,0:T(8,128)} %get-tuple-element.19), channel_id=1, source_target_pairs={{0,16},{16,32},{32,48},{48,64},{64,80},{80,96},{96,112},{112,128},... | collective-permute-start | bytes 393224 | tf_op jit(solution)/shard_map/ppermute | solution.py:15
  9.5 2.5 %collective-permute-start.1 = (f32[8,32,128]{2,1,0:T(8,128)}, f32[8,32,128]{2,1,0:T(8,128)}, u32[]{:S(2)}, u32[]{:S(2)}) collective-permute-start(f32[8,32,128]{2,1,0:T(8,128)} %get-tuple-element.22), channel_id=1, source_target_pairs={{16,0},{32,16},{48,32},{64,48},{80,64},{96,80},{112,96},{128,112},... | collective-permute-start | bytes 393224 | tf_op jit(solution)/shard_map/ppermute | solution.py:15
  12.0 1.2 %collective-permute-start.2 = (f32[8,32,128]{2,1,0:T(8,128)}, f32[8,32,128]{2,1,0:T(8,128)}, u32[]{:S(2)}, u32[]{:S(2)}) collective-permute-start(f32[8,32,128]{2,1,0:T(8,128)} %get-tuple-element.21), channel_id=1, source_target_pairs={{0,1},{1,2},{2,3},{3,4},{4,5},{5,6},{6,7},{7,8},{8,9},{9,10},{10,1... | collective-permute-start | bytes 393224 | tf_op jit(solution)/shard_map/ppermute | solution.py:21
  13.2 5.0 %collective-permute-start.3 = (f32[8,32,128]{2,1,0:T(8,128)}, f32[8,32,128]{2,1,0:T(8,128)}, u32[]{:S(2)}, u32[]{:S(2)}) collective-permute-start(f32[8,32,128]{2,1,0:T(8,128)} %get-tuple-element.20), channel_id=1, source_target_pairs={{0,15},{1,0},{2,1},{3,2},{4,3},{5,4},{6,5},{7,6},{8,7},{9,8},{10,9... | collective-permute-start | bytes 393224 | tf_op jit(solution)/shard_map/ppermute | solution.py:21
  18.2 0.7 broadcast_in_dim.73
  18.9 17.2 %all-to-all-start = ((f32[256,1,4]{2,1,0:T(1,128)}), f32[256,1,4]{2,1,0:T(1,128)}, u32[]{:S(2)}, u32[]{:S(2)}) async-start(f32[256,1,4]{2,1,0:T(1,128)} %broadcast_in_dim.73), calls=%async_computation | async-start | bytes 262144 | tf_op jit(solution)/shard_map/all_to_all | solution.py:174
  36.1 0.7 fusion.63
  36.8 0.6 copy-done.21
  37.4 0.5 fusion.51
  38.0 1.0 convolution_multiply_fusion.2
  38.9 1.0 convolution_multiply_fusion.1
  39.9 0.1 broadcast_select_fusion
  40.0 1.0 fusion.7
  41.1 0.6 and_compare_fusion.2
  41.7 0.6 slice.326
  42.3 0.8 copy.33
  43.1 1.5 %copy.34 = f32[64,128]{0,1:T(8,128)} copy(f32[64,128]{1,0:T(8,128)} %convolution_multiply_fusion.1) | data formatting | bytes 65536 | tf_op jit(solution)/shard_map/mul | solution.py:126
  44.6 1.5 %copy.36 = f32[64,128]{0,1:T(8,128)} copy(f32[64,128]{1,0:T(8,128)} %slice.326) | data formatting | bytes 65536 | tf_op jit(solution)/shard_map/slice | solution.py:145
  46.1 2.2 %all-to-all-done = f32[256,1,4]{2,1,0:T(1,128)} async-done(((f32[256,1,4]{2,1,0:T(1,128)}), f32[256,1,4]{2,1,0:T(1,128)}, u32[]{:S(2)}, u32[]{:S(2)}) %all-to-all-start) | async-done | bytes 4128 | tf_op jit(solution)/shard_map/all_to_all | solution.py:174
  48.2 0.7 copy-done.15
  48.9 1.2 %convolution_bitcast_fusion.12 = f32[4,128]{1,0:T(4,128)S(1)} fusion(f32[256,4]{1,0:T(8,128)} %bitcast.23, s32[128]{0:T(128)S(1)} %copy-done.15), kind=kOutput, calls=%fused_computation.33 | convolution fusion | flops 1605632 | bytes 6656 | tf_op jit(solution)/shard_map/qb,be->qe/dot_general | solution.py:216
  50.1 0.1 broadcast_multiply_fusion.1
  50.3 0.5 copy-done.23
  50.8 0.1 copy-done.20
  50.9 1.9 %fusion.14 = f32[4,8,32,128]{3,2,1,0:T(8,128)S(1)} fusion(f32[32,32,1,1]{1,0,3,2:T(8,128)S(1)} %copy-done.23, f32[1,8,32,128]{3,2,1,0:T(8,128)} %bitcast.7, f32[1,8,32,128]{3,2,1,0:T(8,128)} %bitcast.6, f32[1,8,32,128]{3,2,1,0:T(8,128)} %bitcast.5, f32[1,8,32,128]{3,2,1,0:T(8,128)} %bitcast.4, pred[4,128]{1,0:T(4,128)(4,1)S(1)} %copy-done.20), kind=kOutput, calls=%fused_computation.26 | convolution fusion | flops 51249152 | bytes 1053184 | tf_op jit(solution)/shard_map/kj,fsjr->fskr/dot_general | solution.py:164
  52.8 0.6 copy-done.14
  53.4 0.6 fusion.13
  54.0 0.1 copy-done.11
  54.1 0.5 copy-done.13
  54.6 0.6 fusion.12
  55.5 0.9 copy-done.2
  56.4 0.1 multiply_dynamic-update-slice_fusion.15
  56.5 0.1 multiply_dynamic-update-slice_fusion.14
  56.6 1.9 %fusion.6 = f32[8,256,128]{1,2,0:T(8,128)S(1)} fusion(f32[8,256,128]{1,2,0:T(8,128)S(1)} %fusion.7, f32[8,192,128]{2,1,0:T(8,128)S(1)} %multiply_dynamic-update-slice_fusion.12, f32[256,192,1]{0,1,2:T(8,128)S(1)} %copy-done.1, f32[4,64,128]{1,2,0:T(8,128)S(1)} %get-tuple-element.32, f32[4,64,128]{1,2,0:T(8,128)S(1)} %get-tuple-element.31), kind=kOutput, calls=%fused_computation.9 | convolution fusion | flops 605552640 | bytes 3342336 | tf_op jit(solution)/shard_map/ck,skr->scr/dot_general | solution.py:117
  58.5 1.3 %convolution_bitcast_fusion.4 = f32[8,192,128]{2,1,0:T(8,128)S(1)} fusion(f32[256,192,1]{0,1,2:T(8,128)S(1)} %copy-done.1, f32[8,256,128]{1,2,0:T(8,128)S(1)} %fusion.6, f32[4,256,128]{1,2,0:T(8,128)S(1)} %copy.31, f32[4,256,128]{1,2,0:T(8,128)S(1)} %copy.30), kind=kOutput, calls=%fused_computation.13 | convolution fusion | flops 604766208 | bytes 3080192 | tf_op jit(solution)/shard_map/ck,scr->skr/dot_general | solution.py:107
  59.9 1.0 fusion.8
  61.0 2.6 %collective-permute-start.4 = (f32[8,32,128]{2,1,0:T(8,128)S(1)}, f32[8,32,128]{2,1,0:T(8,128)S(1)}, u32[]{:S(2)}, u32[]{:S(2)}) collective-permute-start(f32[8,32,128]{2,1,0:T(8,128)S(1)} %get-tuple-element.13), channel_id=1, source_target_pairs={{0,16},{16,32},{32,48},{48,64},{64,80},{80,96},{96,112},{112,128},... | collective-permute-start | bytes 393224 | tf_op jit(solution)/shard_map/ppermute | solution.py:15
  63.5 1.9 %collective-permute-start.5 = (f32[8,32,128]{2,1,0:T(8,128)S(1)}, f32[8,32,128]{2,1,0:T(8,128)S(1)}, u32[]{:S(2)}, u32[]{:S(2)}) collective-permute-start(f32[8,32,128]{2,1,0:T(8,128)S(1)} %get-tuple-element.16), channel_id=1, source_target_pairs={{16,0},{32,16},{48,32},{64,48},{80,64},{96,80},{112,96},{128,112},... | collective-permute-start | bytes 393224 | tf_op jit(solution)/shard_map/ppermute | solution.py:15
  65.5 0.9 collective-permute-start.6
  66.3 4.6 %collective-permute-start.7 = (f32[8,32,128]{2,1,0:T(8,128)S(1)}, f32[8,32,128]{2,1,0:T(8,128)S(1)}, u32[]{:S(2)}, u32[]{:S(2)}) collective-permute-start(f32[8,32,128]{2,1,0:T(8,128)S(1)} %get-tuple-element.14), channel_id=1, source_target_pairs={{0,15},{1,0},{2,1},{3,2},{4,3},{5,4},{6,5},{7,6},{8,7},{9,8},{10,9... | collective-permute-start | bytes 393224 | tf_op jit(solution)/shard_map/ppermute | solution.py:21
  70.9 0.1 fusion.61
  71.0 3.7 %collective-permute-done.6 = f32[8,32,128]{2,1,0:T(8,128)S(1)} collective-permute-done((f32[8,32,128]{2,1,0:T(8,128)S(1)}, f32[8,32,128]{2,1,0:T(8,128)S(1)}, u32[]{:S(2)}, u32[]{:S(2)}) %collective-permute-start.6) | collective-permute-done | bytes 131104 | tf_op jit(solution)/shard_map/ppermute | solution.py:21
  74.7 0.6 fusion.11
  75.3 0.6 fusion.10
  75.9 0.6 fusion.9
  76.7 0.1 multiply_dynamic-update-slice_fusion.3
  76.9 0.1 multiply_dynamic-update-slice_fusion.2
  77.1 1.9 %fusion.4 = f32[8,256,128]{1,2,0:T(8,128)S(1)} fusion(f32[8,256,128]{1,2,0:T(8,128)S(1)} %fusion.6, f32[8,256,128]{1,2,0:T(8,128)S(1)} %fusion.8, f32[8,192,128]{2,1,0:T(8,128)S(1)} %multiply_dynamic-update-slice_fusion, f32[256,192,1]{0,1,2:T(8,128)S(1)} %copy-done.1, f32[4,64,128]{1,2,0:T(8,128)S(1)} %get-tuple-element.32, ...), kind=kOutput, calls=%fused_computation.5 | convolution fusion | flops 606601216 | bytes 5439488 | tf_op jit(solution)/shard_map/ck,skr->scr/dot_general | solution.py:117
  79.0 0.6 fusion.17
  79.6 0.1 copy-done.19
  79.7 0.3 fusion.65
  80.0 0.7 copy-done.16
  80.7 0.8 fusion.32
  81.5 16.0 %all-to-all-start.1 = ((f32[256,1,4]{2,1,0:T(1,128)}), f32[256,1,4]{2,1,0:T(1,128)S(1)}, u32[]{:S(2)}, u32[]{:S(2)}) async-start(f32[256,1,4]{2,1,0:T(1,128)} %bitcast.49), calls=%async_computation.1 | async-start | bytes 262144 | tf_op jit(solution)/shard_map/all_to_all | solution.py:178
  97.5 0.1 fusion.60
  97.6 1.0 copy.38
  98.6 1.0 copy.39
  99.6 10.8 %all-to-all-done.1 = f32[256,1,4]{2,1,0:T(1,128)S(1)} async-done(((f32[256,1,4]{2,1,0:T(1,128)}), f32[256,1,4]{2,1,0:T(1,128)S(1)}, u32[]{:S(2)}, u32[]{:S(2)}) %all-to-all-start.1) | async-done | bytes 4128 | tf_op jit(solution)/shard_map/all_to_all | solution.py:178
  110.4 0.8 reduce_sum.9
  (68 shorter events, 0.7 us)
Async XLA Ops:
  0.6 37.3 %copy-start = (f32[256,128]{1,0:T(8,128)S(1)}, f32[256,128]{1,0:T(8,128)}, u32[]{:S(2)}) copy-start(f32[256,128]{1,0:T(8,128)} %param.18) | copy-start | bytes 393220
  0.6 1.3 %copy-start.5 = (f32[4,256,128]{2,1,0:T(8,128)S(1)}, f32[4,256,128]{2,1,0:T(8,128)}, u32[]{:S(2)}) copy-start(f32[4,256,128]{2,1,0:T(8,128)} %param.21) | copy-start | bytes 1572868
  2.0 0.9 copy-start.1
  4.9 45.3 %collective-permute-start = (f32[8,32,128]{2,1,0:T(8,128)}, f32[8,32,128]{2,1,0:T(8,128)}, u32[]{:S(2)}, u32[]{:S(2)}) collective-permute-start(f32[8,32,128]{2,1,0:T(8,128)} %get-tuple-element.19), channel_id=1, source_target_pairs={{0,16},{16,32},{32,48},{48,64},{64,80},{80,96},{96,112},{112,128},... | collective-permute-start | bytes 393224 | tf_op jit(solution)/shard_map/ppermute | solution.py:15
  9.5 40.7 %collective-permute-start.1 = (f32[8,32,128]{2,1,0:T(8,128)}, f32[8,32,128]{2,1,0:T(8,128)}, u32[]{:S(2)}, u32[]{:S(2)}) collective-permute-start(f32[8,32,128]{2,1,0:T(8,128)} %get-tuple-element.22), channel_id=1, source_target_pairs={{16,0},{32,16},{48,32},{64,48},{80,64},{96,80},{112,96},{128,112},... | collective-permute-start | bytes 393224 | tf_op jit(solution)/shard_map/ppermute | solution.py:15
  12.0 38.3 %collective-permute-start.2 = (f32[8,32,128]{2,1,0:T(8,128)}, f32[8,32,128]{2,1,0:T(8,128)}, u32[]{:S(2)}, u32[]{:S(2)}) collective-permute-start(f32[8,32,128]{2,1,0:T(8,128)} %get-tuple-element.21), channel_id=1, source_target_pairs={{0,1},{1,2},{2,3},{3,4},{4,5},{5,6},{6,7},{7,8},{8,9},{9,10},{10,1... | collective-permute-start | bytes 393224 | tf_op jit(solution)/shard_map/ppermute | solution.py:21
  13.2 5.0 %copy-start.18 = (f32[4,1]{0,1:T(1,128)S(1)}, f32[4,1]{0,1:T(1,128)}, u32[]{:S(2)}) copy-start(f32[4,1]{0,1:T(1,128)} %param.26) | copy-start | bytes 52
  13.2 37.1 %collective-permute-start.3 = (f32[8,32,128]{2,1,0:T(8,128)}, f32[8,32,128]{2,1,0:T(8,128)}, u32[]{:S(2)}, u32[]{:S(2)}) collective-permute-start(f32[8,32,128]{2,1,0:T(8,128)} %get-tuple-element.20), channel_id=1, source_target_pairs={{0,15},{1,0},{2,1},{3,2},{4,3},{5,4},{6,5},{7,6},{8,7},{9,8},{10,9... | collective-permute-start | bytes 393224 | tf_op jit(solution)/shard_map/ppermute | solution.py:21
  18.9 29.4 %all-to-all-start = ((f32[256,1,4]{2,1,0:T(1,128)}), f32[256,1,4]{2,1,0:T(1,128)}, u32[]{:S(2)}, u32[]{:S(2)}) async-start(f32[256,1,4]{2,1,0:T(1,128)} %broadcast_in_dim.73), calls=%async_computation | async-start | bytes 262144 | tf_op jit(solution)/shard_map/all_to_all | solution.py:174
  36.1 1.9 %copy-start.6 = (f32[256,64]{1,0:T(8,128)S(1)}, f32[256,64]{1,0:T(8,128)}, u32[]{:S(2)}) copy-start(f32[256,64]{1,0:T(8,128)} %constant.66) | copy-start | bytes 196612
  36.8 0.7 copy-start.21
  36.8 0.7 copy-start.22
  37.9 1.0 copy-start.9
  38.9 1.1 copy-start.3
  40.0 1.0 copy-start.17
  48.2 0.7 copy-start.15
  48.9 1.2 %copy-start.8 = (f32[64,128]{0,1:T(8,128)S(1)}, f32[64,128]{0,1:T(8,128)}, u32[]{:S(2)}) copy-start(f32[64,128]{0,1:T(8,128)} %copy.34) | copy-start | bytes 98308
  50.1 0.7 copy-start.23
  50.3 0.6 copy-start.20
  50.9 1.9 %copy-start.12 = (f32[32,32,1,1]{1,0,3,2:T(8,128)S(1)}, f32[32,32,1,1]{1,0,3,2:T(8,128)}, u32[]{:S(2)}) copy-start(f32[32,32,1,1]{1,0,3,2:T(8,128)} %constant.70) | copy-start | bytes 12292
  52.8 0.6 copy-start.14
  53.4 0.7 copy-start.11
  53.9 0.7 copy-start.13
  55.4 0.9 copy-start.2
  58.5 1.3 %copy-start.4 = (f32[256,256,1]{1,0,2:T(8,128)S(1)}, f32[256,256,1]{1,0,2:T(8,128)}, u32[]{:S(2)}) copy-start(f32[256,256,1]{1,0,2:T(8,128)} %constant.67) | copy-start | bytes 786436
  61.0 10.1 %collective-permute-start.4 = (f32[8,32,128]{2,1,0:T(8,128)S(1)}, f32[8,32,128]{2,1,0:T(8,128)S(1)}, u32[]{:S(2)}, u32[]{:S(2)}) collective-permute-start(f32[8,32,128]{2,1,0:T(8,128)S(1)} %get-tuple-element.13), channel_id=1, source_target_pairs={{0,16},{16,32},{32,48},{48,64},{64,80},{80,96},{96,112},{112,128},... | collective-permute-start | bytes 393224 | tf_op jit(solution)/shard_map/ppermute | solution.py:15
  63.5 7.5 %collective-permute-start.5 = (f32[8,32,128]{2,1,0:T(8,128)S(1)}, f32[8,32,128]{2,1,0:T(8,128)S(1)}, u32[]{:S(2)}, u32[]{:S(2)}) collective-permute-start(f32[8,32,128]{2,1,0:T(8,128)S(1)} %get-tuple-element.16), channel_id=1, source_target_pairs={{16,0},{32,16},{48,32},{64,48},{80,64},{96,80},{112,96},{128,112},... | collective-permute-start | bytes 393224 | tf_op jit(solution)/shard_map/ppermute | solution.py:15
  65.5 9.3 %collective-permute-start.6 = (f32[8,32,128]{2,1,0:T(8,128)S(1)}, f32[8,32,128]{2,1,0:T(8,128)S(1)}, u32[]{:S(2)}, u32[]{:S(2)}) collective-permute-start(f32[8,32,128]{2,1,0:T(8,128)S(1)} %get-tuple-element.15), channel_id=1, source_target_pairs={{0,1},{1,2},{2,3},{3,4},{4,5},{5,6},{6,7},{7,8},{8,9},{9,10},{10,1... | collective-permute-start | bytes 393224 | tf_op jit(solution)/shard_map/ppermute | solution.py:21
  66.3 8.4 %collective-permute-start.7 = (f32[8,32,128]{2,1,0:T(8,128)S(1)}, f32[8,32,128]{2,1,0:T(8,128)S(1)}, u32[]{:S(2)}, u32[]{:S(2)}) collective-permute-start(f32[8,32,128]{2,1,0:T(8,128)S(1)} %get-tuple-element.14), channel_id=1, source_target_pairs={{0,15},{1,0},{2,1},{3,2},{4,3},{5,4},{6,5},{7,6},{8,7},{9,8},{10,9... | collective-permute-start | bytes 393224 | tf_op jit(solution)/shard_map/ppermute | solution.py:21
  77.0 2.0 %copy-start.7 = (f32[64,128]{0,1:T(8,128)S(1)}, f32[64,128]{0,1:T(8,128)}, u32[]{:S(2)}) copy-start(f32[64,128]{0,1:T(8,128)} %copy.36) | copy-start | bytes 98308
  77.0 2.0 %copy-start.10 = (f32[256,64,1]{1,0,2:T(8,128)S(1)}, f32[256,64,1]{1,0,2:T(8,128)}, u32[]{:S(2)}) copy-start(f32[256,64,1]{1,0,2:T(8,128)} %constant.72) | copy-start | bytes 196612
  79.0 0.7 copy-start.19
  80.0 0.7 copy-start.16
  81.5 28.9 %all-to-all-start.1 = ((f32[256,1,4]{2,1,0:T(1,128)}), f32[256,1,4]{2,1,0:T(1,128)S(1)}, u32[]{:S(2)}, u32[]{:S(2)}) async-start(f32[256,1,4]{2,1,0:T(1,128)} %bitcast.49), calls=%async_computation.1 | async-start | bytes 262144 | tf_op jit(solution)/shard_map/all_to_all | solution.py:178

commit v5 on v4

--- a/solution.py
+++ b/solution.py
@@ -74,8 +74,9 @@
     )
 
 
-def volume_rate(states, coupling, bulk_modulus, inverse_size):
-    mixed = jnp.einsum("cd,scr->sdr", coupling, states, precision=lax.Precision.HIGHEST)
+def volume_rate(states, coupling, bulk_modulus, inverse_size, mixed=None):
+    if mixed is None:
+        mixed = jnp.einsum("cd,scr->sdr", coupling, states, precision=lax.Precision.HIGHEST)
     channel = lax.broadcasted_iota(jnp.int32, (256, 1), 0)
     factor = jnp.where(
         channel < 64, -(bulk_modulus * inverse_size)[None, :], -inverse_size[None, :]
@@ -101,9 +102,11 @@
     return (below_trace, above_trace)
 
 
-def heun_step(states, sources, neighbour_fn, bulk_modulus, inverse_size, coupling, selects):
-
-    def rate_of(field_now):
+def heun_step(
+    states, sources, neighbour_fn, bulk_modulus, inverse_size, coupling, selects, mixed
+):
+
+    def rate_of(field_now, mixed=None):
         traces_all = jnp.einsum("ck,scr->skr", selects, field_now, precision=lax.Precision.HIGHEST)
         traces = [traces_all[:, 32 * f : 32 * f + 32] for f in range(6)]
         neighbours = neighbour_fn(traces)
@@ -115,9 +118,10 @@
             1,
         )
         lifted = jnp.einsum("ck,skr->scr", selects, face_rates, precision=lax.Precision.HIGHEST)
-        return volume_rate(field_now, coupling, bulk_modulus, inverse_size) + lifted + sources
-
-    first_rate = rate_of(states)
+        volume = volume_rate(field_now, coupling, bulk_modulus, inverse_size, mixed)
+        return volume + lifted + sources
+
+    first_rate = rate_of(states, mixed)
     second_rate = rate_of(states + TIME_STEP * first_rate)
     return states + 0.5 * TIME_STEP * (first_rate + second_rate)
 
@@ -142,7 +146,7 @@
     new_forward, new_adjoint, forward_div, adjoint_state, inverse_size, coupling, quadrature
 ):
     new_div = divergence(new_forward, coupling, inverse_size)
-    integrand = new_adjoint[:, :64] * forward_div[None] + adjoint_state[None, :64] * new_div
+    integrand = new_adjoint[:, :64] * forward_div[None] + adjoint_state[:64][None] * new_div
     return jnp.einsum("n,pnr->pr", quadrature, integrand, precision=lax.Precision.HIGHEST) / (
         64.0 * inverse_size**3
     )
@@ -216,8 +220,13 @@
     perturb = jnp.einsum(
         "qb,be->qe", whole_dirs, owners.astype(jnp.float32), precision=lax.Precision.HIGHEST
     )
-    forward_div = divergence(forward_state, coupling, inverse_size)
-    adjoint_div = divergence(adjoint_state, coupling, inverse_size)
+    probe_count = inc_forward.shape[0]
+    batch = jnp.concatenate(
+        [inc_forward, inc_adjoint, forward_state[None], adjoint_state[None]], 0
+    )
+    mixed = jnp.einsum("cd,scr->sdr", coupling, batch, precision=lax.Precision.HIGHEST)
+    forward_div = -inverse_size * mixed[2 * probe_count, :64]
+    adjoint_div = -inverse_size * mixed[2 * probe_count + 1, :64]
 
     def neighbour_fn(traces):
         from_south, from_north = rims_lat(traces[0], traces[1])
@@ -227,16 +236,17 @@
         below_trace, above_trace = radial_neighbours(traces[4], traces[5])
         return horizontal + [below_trace, above_trace]
 
-    probe_count = inc_forward.shape[0]
-    states = jnp.concatenate([inc_forward, inc_adjoint], 0)
+    states = batch[: 2 * probe_count]
     sources = pressure_source(perturb, forward_div, adjoint_div)
     updated = heun_step(
-        states, sources, neighbour_fn, bulk_modulus, inverse_size, coupling, selects
+        states, sources, neighbour_fn, bulk_modulus, inverse_size, coupling, selects,
+        mixed[: 2 * probe_count],
     )
     new_forward = updated[:probe_count]
     new_adjoint = updated[probe_count:]
     element_terms = sensitivity(
-        new_forward, new_adjoint, forward_div, adjoint_state, inverse_size, coupling, quadrature
+        new_forward, new_adjoint, forward_div, batch[2 * probe_count + 1], inverse_size,
+        coupling, quadrature,
     )
     partial_sums = jnp.einsum(
         "qe,be->qb", element_terms, owners.astype(jnp.float32), precision=lax.Precision.HIGHEST

time: 112 us -> 108 us (0.964)
  local copies, waits for them, and re-layouts: 15.9 us -> 10.5 us
  other arithmetic: 3.02 us -> 5.15 us
    unnamed x52, local copies, waits for them, and re-layouts: 9.05 us -> 5.13 us
    mul x2 -> x0, local copies, waits for them, and re-layouts: 2.33 us -> none  [divergence(): -inverse_size]
    dot_general x0 -> x1, matrix products: none -> 2.22 us  [body(): jnp.einsum('cd,scr->sdr', coupling, batch, precision=lax.Precision.HIGHEST)]
    dot_general x3 -> x1, matrix products: 2.55 us -> 0.58 us  [divergence(): jnp.einsum('cn,...cr->...nr', coupling[:, :64], field_state, precision=la...]
    mul x1 -> x2, other arithmetic: 0.14 us -> 1.7 us  [pressure_source(): perturb[:, None, :] * forward_div[None]]
  transfers between devices with their start and end apart: 10 -> 10, of which waited for: 3 -> 3; matrix products, arithmetic and copies ran while one was open for 12% -> 13% of each run, Pallas kernels for 0% -> 0%
where the time goes in v5:
time: 108 us; the launch traced here: 107 us
  starting transfers between devices  55.6 us (51%)
  waiting for transfers between devices  17.5 us (16%)
  matrix products  17.3 us (16%)
  local copies, waits for them, and re-layouts  10.5 us (10%)
  other arithmetic  5.15 us (5%)
  between operations  1.34 us (1%)
    all_to_all x1, starting transfers between devices, gather_blocks(): return lax.all_to_all(spread, ('lat', 'lon'), 0, 0, tiled=True).T  17.2 us
    all_to_all x1, starting transfers between devices, scatter_sums(): pieces = lax.all_to_all(partial.T, ('lat', 'lon'), 0, 0, tiled=True)  15.2 us
    ppermute x4, starting transfers between devices, from_behind(): return lax.ppermute(value, axis, pairs)  11.6 us
    ppermute x4, starting transfers between devices, shifted(): return lax.ppermute(block, axis, route)  11.5 us
    all_to_all x1, waiting for transfers between devices, scatter_sums(): pieces = lax.all_to_all(partial.T, ('lat', 'lon'), 0, 0, tiled=True)  10.8 us
    unnamed x52, local copies, waits for them, and re-layouts  5.13 us
    dot_general x6, matrix products, reorient(): jnp.einsum('kj,fsjr->fskr', face_map(kind), stacked, precision=lax.Precis...  4.74 us
    dot_general x2, matrix products, rate_of(): jnp.einsum('ck,skr->scr', selects, face_rates, precision=lax.Precision.HI...  3.84 us
  transfers between devices with their start and end apart: 10, of which 3 were waited for; matrix products, arithmetic and copies ran while one was open for 13% of the time, Pallas kernels for 0%

profile of v5, /device:TPU:1, one launch (start us, length us, event | category | flops | bytes accessed | tf_op | source)
XLA Modules:
  0.0 107.3 jit_solution(3062386287678405567)
XLA Ops:
  0.6 0.0 copy-start
  0.7 1.3 %copy.32 = f32[4,256,128]{1,2,0:T(8,128)S(1)} copy(f32[4,256,128]{2,1,0:T(8,128)} %param.20) | data formatting | bytes 1048576 | tf_op args[2]
  2.0 0.2 copy.33
  2.2 0.0 copy-start.16
  2.2 1.2 %convolution_bitcast_fusion.5 = f32[8,192,128]{2,1,0:T(8,128)S(1)} fusion(f32[256,192,1]{0,1,2:T(8,128)S(1)} %copy-done, f32[4,256,128]{1,2,0:T(8,128)S(1)} %copy.33, f32[4,256,128]{1,2,0:T(8,128)S(1)} %copy.32), kind=kOutput, calls=%fused_computation.20 | convolution fusion | flops 604241920 | bytes 2031616 | tf_op jit(solution)/shard_map/ck,scr->skr/dot_general | solution.py:110
  3.4 0.0 copy-start.8
  3.5 0.0 copy-start.6
  3.5 0.8 fusion.72
  4.3 4.6 %collective-permute-start = (f32[8,32,128]{2,1,0:T(8,128)}, f32[8,32,128]{2,1,0:T(8,128)}, u32[]{:S(2)}, u32[]{:S(2)}) collective-permute-start(f32[8,32,128]{2,1,0:T(8,128)} %get-tuple-element.21), channel_id=1, source_target_pairs={{0,16},{16,32},{32,48},{48,64},{64,80},{80,96},{96,112},{112,128},... | collective-permute-start | bytes 393224 | tf_op jit(solution)/shard_map/ppermute | solution.py:15
  8.9 2.5 %collective-permute-start.1 = (f32[8,32,128]{2,1,0:T(8,128)}, f32[8,32,128]{2,1,0:T(8,128)}, u32[]{:S(2)}, u32[]{:S(2)}) collective-permute-start(f32[8,32,128]{2,1,0:T(8,128)} %get-tuple-element.24), channel_id=1, source_target_pairs={{16,0},{32,16},{48,32},{64,48},{80,64},{96,80},{112,96},{128,112},... | collective-permute-start | bytes 393224 | tf_op jit(solution)/shard_map/ppermute | solution.py:15
  11.3 1.2 %collective-permute-start.2 = (f32[8,32,128]{2,1,0:T(8,128)}, f32[8,32,128]{2,1,0:T(8,128)}, u32[]{:S(2)}, u32[]{:S(2)}) collective-permute-start(f32[8,32,128]{2,1,0:T(8,128)} %get-tuple-element.23), channel_id=1, source_target_pairs={{0,1},{1,2},{2,3},{3,4},{4,5},{5,6},{6,7},{7,8},{8,9},{9,10},{10,1... | collective-permute-start | bytes 393224 | tf_op jit(solution)/shard_map/ppermute | solution.py:21
  12.5 5.0 %collective-permute-start.3 = (f32[8,32,128]{2,1,0:T(8,128)}, f32[8,32,128]{2,1,0:T(8,128)}, u32[]{:S(2)}, u32[]{:S(2)}) collective-permute-start(f32[8,32,128]{2,1,0:T(8,128)} %get-tuple-element.22), channel_id=1, source_target_pairs={{0,15},{1,0},{2,1},{3,2},{4,3},{5,4},{6,5},{7,6},{8,7},{9,8},{10,9... | collective-permute-start | bytes 393224 | tf_op jit(solution)/shard_map/ppermute | solution.py:21
  17.5 0.7 broadcast_in_dim.134
  18.2 17.2 %all-to-all-start = ((f32[256,1,4]{2,1,0:T(1,128)}), f32[256,1,4]{2,1,0:T(1,128)}, u32[]{:S(2)}, u32[]{:S(2)}) async-start(f32[256,1,4]{2,1,0:T(1,128)} %broadcast_in_dim.134), calls=%async_computation | async-start | bytes 262144 | tf_op jit(solution)/shard_map/all_to_all | solution.py:178
  35.4 0.8 fusion.71
  36.2 0.6 iota_compare_fusion.4
  36.7 0.1 copy.34
  36.8 0.8 copy.35
  37.6 0.5 fusion.59
  38.1 2.2 %convolution_bitcast_fusion = f32[10,256,128]{1,2,0:T(8,128)S(1)} fusion(f32[256,256,1]{1,0,2:T(8,128)} %constant.67, f32[1,256,128]{1,2,0:T(8,128)} %bitcast.134, f32[1,256,128]{1,2,0:T(8,128)S(1)} %bitcast.133, f32[4,256,128]{1,2,0:T(8,128)S(1)} %copy.33, f32[4,256,128]{1,2,0:T(8,128)S(1)} %copy.32), kind=kOutput, calls=%fused_computation | convolution fusion | flops 1007616000 | bytes 2883584 | tf_op jit(solution)/shard_map/cd,scr->sdr/dot_general | solution.py:227
  40.4 0.7 fusion.52
  41.1 0.1 broadcast_select_fusion
  41.2 0.6 and_compare_fusion.2
  41.8 1.4 %slice.337 = f32[64,128]{1,0:T(8,128)} slice(f32[256,128]{1,0:T(8,128)} %param.19), slice={[0:64], [0:128]} | slice | bytes 65536 | tf_op jit(solution)/shard_map/slice | solution.py:149
  43.1 1.5 %copy.40 = f32[64,128]{0,1:T(8,128)} copy(f32[64,128]{1,0:T(8,128)} %slice.337) | data formatting | bytes 65536 | tf_op jit(solution)/shard_map/slice | solution.py:149
  44.6 3.0 %all-to-all-done = f32[256,1,4]{2,1,0:T(1,128)} async-done(((f32[256,1,4]{2,1,0:T(1,128)}), f32[256,1,4]{2,1,0:T(1,128)}, u32[]{:S(2)}, u32[]{:S(2)}) %all-to-all-start) | async-done | bytes 4128 | tf_op jit(solution)/shard_map/all_to_all | solution.py:178
  47.6 1.2 %convolution_bitcast_fusion.12 = f32[4,128]{1,0:T(4,128)S(1)} fusion(f32[256,4]{1,0:T(8,128)} %bitcast.25, s32[128]{0:T(128)} %param.25), kind=kOutput, calls=%fused_computation.37 | convolution fusion | flops 1605632 | bytes 6656 | tf_op jit(solution)/shard_map/qb,be->qe/dot_general | solution.py:220
  48.8 1.0 broadcast_multiply_fusion.1
  49.8 0.0 copy-start.9
  49.8 1.9 %fusion.20 = f32[4,8,32,128]{3,2,1,0:T(8,128)S(1)} fusion(f32[32,32,1,1]{1,0,3,2:T(8,128)} %constant.69, f32[1,8,32,128]{3,2,1,0:T(8,128)} %bitcast.9, f32[1,8,32,128]{3,2,1,0:T(8,128)} %bitcast.8, f32[1,8,32,128]{3,2,1,0:T(8,128)} %bitcast.7, f32[1,8,32,128]{3,2,1,0:T(8,128)} %bitcast.6, pred[4,128]{1,0:T(4,128)(4,1)} %get-tuple-element.36), kind=kOutput, calls=%fused_computation.32 | convolution fusion | flops 51249152 | bytes 1053184 | tf_op jit(solution)/shard_map/kj,fsjr->fskr/dot_general | solution.py:168
  51.7 0.6 fusion.19
  52.3 0.6 fusion.18
  53.2 0.7 copy-done.2
  53.9 0.1 multiply_dynamic-update-slice_fusion.15
  54.0 0.1 multiply_dynamic-update-slice_fusion.14
  54.2 1.9 %fusion.6 = f32[8,256,128]{1,2,0:T(8,128)S(1)} fusion(f32[8,192,128]{2,1,0:T(8,128)S(1)} %multiply_dynamic-update-slice_fusion.12, f32[256,192,1]{0,1,2:T(8,128)S(1)} %copy-done, f32[10,256,128]{1,2,0:T(8,128)S(1)} %convolution_bitcast_fusion, f32[4,64,128]{1,2,0:T(8,128)S(1)} %get-tuple-element.34, f32[4,64,128]{1,2,0:T(8,128)S(1)} %get-tuple-element.33, ...), kind=kOutput, calls=%fused_computation.10 | convolution fusion | flops 605814784 | bytes 3473408 | tf_op jit(solution)/shard_map/ck,skr->scr/dot_general | solution.py:120
  56.1 0.0 copy-start.3
  56.1 1.3 %convolution_bitcast_fusion.4 = f32[8,192,128]{2,1,0:T(8,128)S(1)} fusion(f32[256,192,1]{0,1,2:T(8,128)S(1)} %copy-done, f32[8,256,128]{1,2,0:T(8,128)S(1)} %fusion.6, f32[4,256,128]{1,2,0:T(8,128)S(1)} %copy.33, f32[4,256,128]{1,2,0:T(8,128)S(1)} %copy.32), kind=kOutput, calls=%fused_computation.19 | convolution fusion | flops 604766208 | bytes 3080192 | tf_op jit(solution)/shard_map/ck,scr->skr/dot_general | solution.py:110
  57.4 1.0 fusion.7
  58.5 0.0 copy-start.22
  58.5 2.6 %collective-permute-start.4 = (f32[8,32,128]{2,1,0:T(8,128)S(1)}, f32[8,32,128]{2,1,0:T(8,128)S(1)}, u32[]{:S(2)}, u32[]{:S(2)}) collective-permute-start(f32[8,32,128]{2,1,0:T(8,128)S(1)} %get-tuple-element.15), channel_id=1, source_target_pairs={{0,16},{16,32},{32,48},{48,64},{64,80},{80,96},{96,112},{112,128},... | collective-permute-start | bytes 393224 | tf_op jit(solution)/shard_map/ppermute | solution.py:15
  61.1 1.9 %collective-permute-start.5 = (f32[8,32,128]{2,1,0:T(8,128)S(1)}, f32[8,32,128]{2,1,0:T(8,128)S(1)}, u32[]{:S(2)}, u32[]{:S(2)}) collective-permute-start(f32[8,32,128]{2,1,0:T(8,128)S(1)} %get-tuple-element.18), channel_id=1, source_target_pairs={{16,0},{32,16},{48,32},{64,48},{80,64},{96,80},{112,96},{128,112},... | collective-permute-start | bytes 393224 | tf_op jit(solution)/shard_map/ppermute | solution.py:15
  63.1 0.8 collective-permute-start.6
  63.9 4.6 %collective-permute-start.7 = (f32[8,32,128]{2,1,0:T(8,128)S(1)}, f32[8,32,128]{2,1,0:T(8,128)S(1)}, u32[]{:S(2)}, u32[]{:S(2)}) collective-permute-start(f32[8,32,128]{2,1,0:T(8,128)S(1)} %get-tuple-element.16), channel_id=1, source_target_pairs={{0,15},{1,0},{2,1},{3,2},{4,3},{5,4},{6,5},{7,6},{8,7},{9,8},{10,9... | collective-permute-start | bytes 393224 | tf_op jit(solution)/shard_map/ppermute | solution.py:21
  68.5 0.1 fusion.69
  68.6 3.7 %collective-permute-done.6 = f32[8,32,128]{2,1,0:T(8,128)S(1)} collective-permute-done((f32[8,32,128]{2,1,0:T(8,128)S(1)}, f32[8,32,128]{2,1,0:T(8,128)S(1)}, u32[]{:S(2)}, u32[]{:S(2)}) %collective-permute-start.6) | collective-permute-done | bytes 131104 | tf_op jit(solution)/shard_map/ppermute | solution.py:21
  72.3 0.6 fusion.17
  72.9 0.6 fusion.16
  73.5 0.6 fusion.15
  74.3 0.1 multiply_dynamic-update-slice_fusion.3
  74.4 0.1 multiply_dynamic-update-slice_fusion.2
  74.6 0.0 copy-start.7
  74.6 0.0 copy-start.17
  74.7 1.9 %fusion.4 = f32[8,256,128]{1,2,0:T(8,128)S(1)} fusion(f32[8,256,128]{1,2,0:T(8,128)S(1)} %fusion.6, f32[8,256,128]{1,2,0:T(8,128)S(1)} %fusion.7, f32[8,192,128]{2,1,0:T(8,128)S(1)} %multiply_dynamic-update-slice_fusion, f32[256,192,1]{0,1,2:T(8,128)S(1)} %copy-done, f32[4,64,128]{1,2,0:T(8,128)S(1)} %get-tuple-element.34, ...), kind=kOutput, calls=%fused_computation.6 | convolution fusion | flops 606601216 | bytes 5439488 | tf_op jit(solution)/shard_map/ck,skr->scr/dot_general | solution.py:120
  76.6 0.6 fusion.23
  77.2 0.3 fusion.73
  77.6 0.0 copy-done.14
  77.6 0.8 fusion.38
  78.4 15.2 %all-to-all-start.1 = ((f32[256,1,4]{2,1,0:T(1,128)}), f32[256,1,4]{2,1,0:T(1,128)S(1)}, u32[]{:S(2)}, u32[]{:S(2)}) async-start(f32[256,1,4]{2,1,0:T(1,128)} %bitcast.53), calls=%async_computation.1 | async-start | bytes 262144 | tf_op jit(solution)/shard_map/all_to_all | solution.py:182
  93.6 0.1 fusion.68
  93.7 1.0 copy.42
  94.7 1.0 copy.43
  95.7 10.8 %all-to-all-done.1 = f32[256,1,4]{2,1,0:T(1,128)S(1)} async-done(((f32[256,1,4]{2,1,0:T(1,128)}), f32[256,1,4]{2,1,0:T(1,128)S(1)}, u32[]{:S(2)}, u32[]{:S(2)}) %all-to-all-start.1) | async-done | bytes 4128 | tf_op jit(solution)/shard_map/all_to_all | solution.py:182
  106.5 0.8 reduce_sum.9
  (65 shorter events, 0.7 us)
Async XLA Ops:
  0.6 1.6 %copy-start = (f32[256,192,1]{0,1,2:T(8,128)S(1)}, f32[256,192,1]{0,1,2:T(8,128)}, u32[]{:S(2)}) copy-start(f32[256,192,1]{0,1,2:T(8,128)} %constant.68) | copy-start | bytes 589828
  0.6 1.3 %copy-start.4 = (f32[4,256,128]{2,1,0:T(8,128)S(1)}, f32[4,256,128]{2,1,0:T(8,128)}, u32[]{:S(2)}) copy-start(f32[4,256,128]{2,1,0:T(8,128)} %param.21) | copy-start | bytes 1572868
  2.2 15.3 %copy-start.16 = (f32[4,1]{0,1:T(1,128)S(1)}, f32[4,1]{0,1:T(1,128)}, u32[]{:S(2)}) copy-start(f32[4,1]{0,1:T(1,128)} %param.26) | copy-start | bytes 52
  3.4 33.3 %copy-start.8 = (f32[256,128]{1,0:T(8,128)S(1)}, f32[256,128]{1,0:T(8,128)}, u32[]{:S(2)}) copy-start(f32[256,128]{1,0:T(8,128)} %param.18) | copy-start | bytes 393220
  3.5 33.4 %copy-start.6 = (f32[256,128]{1,0:T(8,128)S(1)}, f32[256,128]{1,0:T(8,128)}, u32[]{:S(2)}) copy-start(f32[256,128]{1,0:T(8,128)} %param.19) | copy-start | bytes 393220
  3.5 34.1 %copy-start.20 = (f32[128]{0:T(128)S(1)}, f32[128]{0:T(128)}, u32[]{:S(2)}) copy-start(f32[128]{0:T(128)} %param.23) | copy-start | bytes 1540
  3.5 34.1 %copy-start.21 = (f32[128]{0:T(128)S(1)}, f32[128]{0:T(128)}, u32[]{:S(2)}) copy-start(f32[128]{0:T(128)} %param.22) | copy-start | bytes 1540
  4.3 45.5 %collective-permute-start = (f32[8,32,128]{2,1,0:T(8,128)}, f32[8,32,128]{2,1,0:T(8,128)}, u32[]{:S(2)}, u32[]{:S(2)}) collective-permute-start(f32[8,32,128]{2,1,0:T(8,128)} %get-tuple-element.21), channel_id=1, source_target_pairs={{0,16},{16,32},{32,48},{48,64},{64,80},{80,96},{96,112},{112,128},... | collective-permute-start | bytes 393224 | tf_op jit(solution)/shard_map/ppermute | solution.py:15
  8.9 40.9 %collective-permute-start.1 = (f32[8,32,128]{2,1,0:T(8,128)}, f32[8,32,128]{2,1,0:T(8,128)}, u32[]{:S(2)}, u32[]{:S(2)}) collective-permute-start(f32[8,32,128]{2,1,0:T(8,128)} %get-tuple-element.24), channel_id=1, source_target_pairs={{16,0},{32,16},{48,32},{64,48},{80,64},{96,80},{112,96},{128,112},... | collective-permute-start | bytes 393224 | tf_op jit(solution)/shard_map/ppermute | solution.py:15
  11.3 38.5 %collective-permute-start.2 = (f32[8,32,128]{2,1,0:T(8,128)}, f32[8,32,128]{2,1,0:T(8,128)}, u32[]{:S(2)}, u32[]{:S(2)}) collective-permute-start(f32[8,32,128]{2,1,0:T(8,128)} %get-tuple-element.23), channel_id=1, source_target_pairs={{0,1},{1,2},{2,3},{3,4},{4,5},{5,6},{6,7},{7,8},{8,9},{9,10},{10,1... | collective-permute-start | bytes 393224 | tf_op jit(solution)/shard_map/ppermute | solution.py:21
  12.5 37.3 %collective-permute-start.3 = (f32[8,32,128]{2,1,0:T(8,128)}, f32[8,32,128]{2,1,0:T(8,128)}, u32[]{:S(2)}, u32[]{:S(2)}) collective-permute-start(f32[8,32,128]{2,1,0:T(8,128)} %get-tuple-element.22), channel_id=1, source_target_pairs={{0,15},{1,0},{2,1},{3,2},{4,3},{5,4},{6,5},{7,6},{8,7},{9,8},{10,9... | collective-permute-start | bytes 393224 | tf_op jit(solution)/shard_map/ppermute | solution.py:21
  18.2 29.4 %all-to-all-start = ((f32[256,1,4]{2,1,0:T(1,128)}), f32[256,1,4]{2,1,0:T(1,128)}, u32[]{:S(2)}, u32[]{:S(2)}) async-start(f32[256,1,4]{2,1,0:T(1,128)} %broadcast_in_dim.134), calls=%async_computation | async-start | bytes 262144 | tf_op jit(solution)/shard_map/all_to_all | solution.py:178
  38.1 2.9 %copy-start.18 = (pred[256]{0:T(512)(128)(4,1)S(1)}, pred[256]{0:T(512)(128)(4,1)}, u32[]{:S(2)}) copy-start(pred[256]{0:T(512)(128)(4,1)} %iota_compare_fusion.4) | copy-start | bytes 772
  38.1 3.0 %copy-start.15 = (s32[4,128]{1,0:T(4,128)S(1)}, s32[4,128]{1,0:T(4,128)}, u32[]{:S(2)}) copy-start(s32[4,128]{1,0:T(4,128)} %param.24) | copy-start | bytes 6148
  48.8 3.0 %copy-start.10 = (f32[32,32,1,1]{1,0,3,2:T(8,128)S(1)}, f32[32,32,1,1]{1,0,3,2:T(8,128)}, u32[]{:S(2)}) copy-start(f32[32,32,1,1]{1,0,3,2:T(8,128)} %constant.70) | copy-start | bytes 12292
  48.8 3.0 %copy-start.12 = (pred[4,128]{1,0:T(4,128)(4,1)S(1)}, pred[4,128]{1,0:T(4,128)(4,1)}, u32[]{:S(2)}) copy-start(pred[4,128]{1,0:T(4,128)(4,1)} %get-tuple-element.37) | copy-start | bytes 1540
  49.8 2.5 %copy-start.9 = (f32[32,32,1,1]{1,0,3,2:T(8,128)S(1)}, f32[32,32,1,1]{1,0,3,2:T(8,128)}, u32[]{:S(2)}) copy-start(f32[32,32,1,1]{1,0,3,2:T(8,128)} %constant.71) | copy-start | bytes 12292
  49.8 2.5 %copy-start.11 = (pred[4,128]{1,0:T(4,128)(4,1)S(1)}, pred[4,128]{1,0:T(4,128)(4,1)}, u32[]{:S(2)}) copy-start(pred[4,128]{1,0:T(4,128)(4,1)} %get-tuple-element.35) | copy-start | bytes 1540
  53.0 0.9 copy-start.2
  53.0 1.1 copy-start.1
  56.1 1.3 %copy-start.3 = (f32[256,256,1]{1,0,2:T(8,128)S(1)}, f32[256,256,1]{1,0,2:T(8,128)}, u32[]{:S(2)}) copy-start(f32[256,256,1]{1,0,2:T(8,128)} %constant.67) | copy-start | bytes 786436
  58.5 13.8 %copy-start.19 = (pred[4,128]{1,0:T(4,128)(4,1)S(1)}, pred[4,128]{1,0:T(4,128)(4,1)}, u32[]{:S(2)}) copy-start(pred[4,128]{1,0:T(4,128)(4,1)} %get-tuple-element.36) | copy-start | bytes 1540
  58.5 13.8 %copy-start.22 = (f32[32,32,1,1]{1,0,3,2:T(8,128)S(1)}, f32[32,32,1,1]{1,0,3,2:T(8,128)}, u32[]{:S(2)}) copy-start(f32[32,32,1,1]{1,0,3,2:T(8,128)} %constant.69) | copy-start | bytes 12292
  58.5 10.1 %collective-permute-start.4 = (f32[8,32,128]{2,1,0:T(8,128)S(1)}, f32[8,32,128]{2,1,0:T(8,128)S(1)}, u32[]{:S(2)}, u32[]{:S(2)}) collective-permute-start(f32[8,32,128]{2,1,0:T(8,128)S(1)} %get-tuple-element.15), channel_id=1, source_target_pairs={{0,16},{16,32},{32,48},{48,64},{64,80},{80,96},{96,112},{112,128},... | collective-permute-start | bytes 393224 | tf_op jit(solution)/shard_map/ppermute | solution.py:15
  61.1 7.5 %collective-permute-start.5 = (f32[8,32,128]{2,1,0:T(8,128)S(1)}, f32[8,32,128]{2,1,0:T(8,128)S(1)}, u32[]{:S(2)}, u32[]{:S(2)}) collective-permute-start(f32[8,32,128]{2,1,0:T(8,128)S(1)} %get-tuple-element.18), channel_id=1, source_target_pairs={{16,0},{32,16},{48,32},{64,48},{80,64},{96,80},{112,96},{128,112},... | collective-permute-start | bytes 393224 | tf_op jit(solution)/shard_map/ppermute | solution.py:15
  63.1 9.3 %collective-permute-start.6 = (f32[8,32,128]{2,1,0:T(8,128)S(1)}, f32[8,32,128]{2,1,0:T(8,128)S(1)}, u32[]{:S(2)}, u32[]{:S(2)}) collective-permute-start(f32[8,32,128]{2,1,0:T(8,128)S(1)} %get-tuple-element.17), channel_id=1, source_target_pairs={{0,1},{1,2},{2,3},{3,4},{4,5},{5,6},{6,7},{7,8},{8,9},{9,10},{10,1... | collective-permute-start | bytes 393224 | tf_op jit(solution)/shard_map/ppermute | solution.py:21
  63.9 8.5 %collective-permute-start.7 = (f32[8,32,128]{2,1,0:T(8,128)S(1)}, f32[8,32,128]{2,1,0:T(8,128)S(1)}, u32[]{:S(2)}, u32[]{:S(2)}) collective-permute-start(f32[8,32,128]{2,1,0:T(8,128)S(1)} %get-tuple-element.16), channel_id=1, source_target_pairs={{0,15},{1,0},{2,1},{3,2},{4,3},{5,4},{6,5},{7,6},{8,7},{9,8},{10,9... | collective-permute-start | bytes 393224 | tf_op jit(solution)/shard_map/ppermute | solution.py:21
  74.6 2.0 %copy-start.5 = (f32[64,128]{0,1:T(8,128)S(1)}, f32[64,128]{0,1:T(8,128)}, u32[]{:S(2)}) copy-start(f32[64,128]{0,1:T(8,128)} %copy.40) | copy-start | bytes 98308
  74.6 2.0 %copy-start.7 = (f32[256,64,1]{1,0,2:T(8,128)S(1)}, f32[256,64,1]{1,0,2:T(8,128)}, u32[]{:S(2)}) copy-start(f32[256,64,1]{1,0,2:T(8,128)} %constant.72) | copy-start | bytes 196612
  74.6 2.6 %copy-start.17 = (f32[64,1,1]{0,1,2:T(1,128)S(1)}, f32[64,1,1]{0,1,2:T(1,128)}, u32[]{:S(2)}) copy-start(f32[64,1,1]{0,1,2:T(1,128)} %constant.73) | copy-start | bytes 772
  76.6 1.0 copy-start.13
  76.6 1.0 copy-start.14
  78.4 28.1 %all-to-all-start.1 = ((f32[256,1,4]{2,1,0:T(1,128)}), f32[256,1,4]{2,1,0:T(1,128)S(1)}, u32[]{:S(2)}, u32[]{:S(2)}) async-start(f32[256,1,4]{2,1,0:T(1,128)} %bitcast.53), calls=%async_computation.1 | async-start | bytes 262144 | tf_op jit(solution)/shard_map/all_to_all | solution.py:182

commit v6 on v5

--- a/solution.py
+++ b/solution.py
@@ -145,11 +145,16 @@
 def sensitivity(
     new_forward, new_adjoint, forward_div, adjoint_state, inverse_size, coupling, quadrature
 ):
-    new_div = divergence(new_forward, coupling, inverse_size)
-    integrand = new_adjoint[:, :64] * forward_div[None] + adjoint_state[:64][None] * new_div
-    return jnp.einsum("n,pnr->pr", quadrature, integrand, precision=lax.Precision.HIGHEST) / (
-        64.0 * inverse_size**3
-    )
+    own = jnp.einsum(
+        "n,pnr->pr", quadrature, new_adjoint[:, :64] * forward_div[None],
+        precision=lax.Precision.HIGHEST,
+    )
+    weighted = coupling[:, :64] * quadrature[None, :]
+    pulled = jnp.einsum(
+        "cn,nr->cr", weighted, adjoint_state[:64], precision=lax.Precision.HIGHEST
+    )
+    crossed = jnp.einsum("pcr,cr->pr", new_forward, pulled, precision=lax.Precision.HIGHEST)
+    return (own - inverse_size * crossed) / (64.0 * inverse_size**3)
 
 
 def face_map(kind):
@@ -245,8 +250,7 @@
     new_forward = updated[:probe_count]
     new_adjoint = updated[probe_count:]
     element_terms = sensitivity(
-        new_forward, new_adjoint, forward_div, batch[2 * probe_count + 1], inverse_size,
-        coupling, quadrature,
+        new_forward, new_adjoint, forward_div, adjoint_state, inverse_size, coupling, quadrature
     )
     partial_sums = jnp.einsum(
         "qe,be->qb", element_terms, owners.astype(jnp.float32), precision=lax.Precision.HIGHEST

time: 108 us -> 106 us (0.981)
  local copies, waits for them, and re-layouts: 10.5 us -> 9.31 us
  starting transfers between devices: 55.6 us -> 54.5 us
    slice x2 -> x0, local copies, waits for them, and re-layouts: 2.84 us -> none  [sensitivity(): adjoint_state[:64][None] * new_div]
    unnamed x52 -> x51, local copies, waits for them, and re-layouts: 5.13 us -> 6.76 us
    ppermute x4, starting transfers between devices: 11.5 us -> 10.3 us  [shifted(): return lax.ppermute(block, axis, route)]
    ppermute x4, starting transfers between devices: 11.6 us -> 12.8 us  [from_behind(): return lax.ppermute(value, axis, pairs)]
where the time goes in v6:
time: 106 us
  starting transfers between devices  54.5 us (51%)
  waiting for transfers between devices  18.5 us (17%)
  matrix products  17.6 us (17%)
  local copies, waits for them, and re-layouts  9.31 us (9%)
  other arithmetic  4.73 us (4%)
  between operations  1.34 us (1%)
    all_to_all x1, starting transfers between devices, gather_blocks(): return lax.all_to_all(spread, ('lat', 'lon'), 0, 0, tiled=True).T  17 us
    all_to_all x1, starting transfers between devices, scatter_sums(): pieces = lax.all_to_all(partial.T, ('lat', 'lon'), 0, 0, tiled=True)  14.4 us
    ppermute x4, starting transfers between devices, from_behind(): return lax.ppermute(value, axis, pairs)  12.8 us
    all_to_all x1, waiting for transfers between devices, scatter_sums(): pieces = lax.all_to_all(partial.T, ('lat', 'lon'), 0, 0, tiled=True)  10.8 us
    ppermute x4, starting transfers between devices, shifted(): return lax.ppermute(block, axis, route)  10.3 us
    unnamed x51, local copies, waits for them, and re-layouts  6.76 us
    dot_general x6, matrix products, reorient(): jnp.einsum('kj,fsjr->fskr', face_map(kind), stacked, precision=lax.Precis...  4.74 us
    all_to_all x1, waiting for transfers between devices, gather_blocks(): return lax.all_to_all(spread, ('lat', 'lon'), 0, 0, tiled=True).T  3.97 us
  transfers between devices with their start and end apart: 10, of which 3 were waited for; matrix products, arithmetic and copies ran while one was open for 13% of the time, Pallas kernels for 0%

profile of v6, /device:TPU:1, one launch (start us, length us, event | category | flops | bytes accessed | tf_op | source)
XLA Modules:
  0.0 106.0 jit_solution(16007088687003003131)
XLA Ops:
  0.6 0.0 copy-start
  0.7 1.3 %copy.31 = f32[4,256,128]{1,2,0:T(8,128)S(1)} copy(f32[4,256,128]{2,1,0:T(8,128)} %param.20) | data formatting | bytes 1048576 | tf_op args[2]
  2.0 0.2 copy.32
  2.2 0.0 copy-start.17
  2.2 1.2 %convolution_bitcast_fusion.5 = f32[8,192,128]{2,1,0:T(8,128)S(1)} fusion(f32[256,192,1]{0,1,2:T(8,128)S(1)} %copy-done, f32[4,256,128]{1,2,0:T(8,128)S(1)} %copy.32, f32[4,256,128]{1,2,0:T(8,128)S(1)} %copy.31), kind=kOutput, calls=%fused_computation.20 | convolution fusion | flops 604241920 | bytes 2031616 | tf_op jit(solution)/shard_map/ck,scr->skr/dot_general | solution.py:110
  3.4 0.0 copy-start.7
  3.5 0.0 copy-start.6
  3.5 0.0 copy-start.8
  3.5 0.0 copy-start.13
  3.5 0.8 fusion.74
  4.3 2.5 %collective-permute-start.2 = (f32[8,32,128]{2,1,0:T(8,128)}, f32[8,32,128]{2,1,0:T(8,128)}, u32[]{:S(2)}, u32[]{:S(2)}) collective-permute-start(f32[8,32,128]{2,1,0:T(8,128)} %get-tuple-element.23), channel_id=1, source_target_pairs={{0,1},{1,2},{2,3},{3,4},{4,5},{5,6},{6,7},{7,8},{8,9},{9,10},{10,1... | collective-permute-start | bytes 393224 | tf_op jit(solution)/shard_map/ppermute | solution.py:21
  6.8 4.9 %collective-permute-start.3 = (f32[8,32,128]{2,1,0:T(8,128)}, f32[8,32,128]{2,1,0:T(8,128)}, u32[]{:S(2)}, u32[]{:S(2)}) collective-permute-start(f32[8,32,128]{2,1,0:T(8,128)} %get-tuple-element.22), channel_id=1, source_target_pairs={{0,15},{1,0},{2,1},{3,2},{4,3},{5,4},{6,5},{7,6},{8,7},{9,8},{10,9... | collective-permute-start | bytes 393224 | tf_op jit(solution)/shard_map/ppermute | solution.py:21
  11.7 4.0 %collective-permute-start = (f32[8,32,128]{2,1,0:T(8,128)}, f32[8,32,128]{2,1,0:T(8,128)}, u32[]{:S(2)}, u32[]{:S(2)}) collective-permute-start(f32[8,32,128]{2,1,0:T(8,128)} %get-tuple-element.21), channel_id=1, source_target_pairs={{0,16},{16,32},{32,48},{48,64},{64,80},{80,96},{96,112},{112,128},... | collective-permute-start | bytes 393224 | tf_op jit(solution)/shard_map/ppermute | solution.py:15
  15.7 1.9 %collective-permute-start.1 = (f32[8,32,128]{2,1,0:T(8,128)}, f32[8,32,128]{2,1,0:T(8,128)}, u32[]{:S(2)}, u32[]{:S(2)}) collective-permute-start(f32[8,32,128]{2,1,0:T(8,128)} %get-tuple-element.24), channel_id=1, source_target_pairs={{16,0},{32,16},{48,32},{64,48},{80,64},{96,80},{112,96},{128,112},... | collective-permute-start | bytes 393224 | tf_op jit(solution)/shard_map/ppermute | solution.py:15
  17.6 0.7 broadcast_in_dim.134
  18.4 17.0 %all-to-all-start = ((f32[256,1,4]{2,1,0:T(1,128)}), f32[256,1,4]{2,1,0:T(1,128)}, u32[]{:S(2)}, u32[]{:S(2)}) async-start(f32[256,1,4]{2,1,0:T(1,128)} %broadcast_in_dim.134), calls=%async_computation | async-start | bytes 262144 | tf_op jit(solution)/shard_map/all_to_all | solution.py:183
  35.4 0.8 fusion.73
  36.1 0.1 copy.33
  36.2 0.8 copy.34
  37.0 0.9 convolution_bitcast_fusion.12
  37.9 0.5 fusion.61
  38.4 2.2 %convolution_bitcast_fusion = f32[10,256,128]{1,2,0:T(8,128)S(1)} fusion(f32[256,256,1]{1,0,2:T(8,128)} %constant.69, f32[1,256,128]{1,2,0:T(8,128)} %bitcast.134, f32[1,256,128]{1,2,0:T(8,128)S(1)} %bitcast.133, f32[4,256,128]{1,2,0:T(8,128)S(1)} %copy.32, f32[4,256,128]{1,2,0:T(8,128)S(1)} %copy.31), kind=kOutput, calls=%fused_computation | convolution fusion | flops 1007616000 | bytes 2883584 | tf_op jit(solution)/shard_map/cd,scr->sdr/dot_general | solution.py:232
  40.7 0.7 fusion.51
  41.4 0.1 broadcast_select_fusion
  41.5 0.6 and_compare_fusion.2
  42.1 1.7 %copy.54 = f32[128,256]{1,0:T(8,128)} copy(f32[128,256]{0,1:T(8,128)} %convolution_bitcast_fusion.12) | data formatting | bytes 262144
  43.7 4.0 %all-to-all-done = f32[256,1,4]{2,1,0:T(1,128)} async-done(((f32[256,1,4]{2,1,0:T(1,128)}), f32[256,1,4]{2,1,0:T(1,128)}, u32[]{:S(2)}, u32[]{:S(2)}) %all-to-all-start) | async-done | bytes 4128 | tf_op jit(solution)/shard_map/all_to_all | solution.py:183
  47.7 1.2 %convolution_bitcast_fusion.13 = f32[4,128]{1,0:T(4,128)S(1)} fusion(f32[256,4]{1,0:T(8,128)} %bitcast.27, s32[128]{0:T(128)} %param.25), kind=kOutput, calls=%fused_computation.34 | convolution fusion | flops 1605632 | bytes 6656 | tf_op jit(solution)/shard_map/qb,be->qe/dot_general | solution.py:225
  48.8 1.0 broadcast_multiply_fusion.1
  49.9 0.0 copy-start.9
  49.9 1.9 %fusion.20 = f32[4,8,32,128]{3,2,1,0:T(8,128)S(1)} fusion(f32[32,32,1,1]{1,0,3,2:T(8,128)} %constant.71, f32[1,8,32,128]{3,2,1,0:T(8,128)} %bitcast.11, f32[1,8,32,128]{3,2,1,0:T(8,128)} %bitcast.10, f32[1,8,32,128]{3,2,1,0:T(8,128)} %bitcast.9, f32[1,8,32,128]{3,2,1,0:T(8,128)} %bitcast.8, pred[4,128]{1,0:T(4,128)(4,1)} %get-tuple-element.36), kind=kOutput, calls=%fused_computation.32 | convolution fusion | flops 51249152 | bytes 1053184 | tf_op jit(solution)/shard_map/kj,fsjr->fskr/dot_general | solution.py:173
  51.8 0.6 fusion.19
  52.4 0.6 fusion.18
  53.3 0.7 copy-done.2
  53.9 0.1 multiply_dynamic-update-slice_fusion.15
  54.0 0.1 multiply_dynamic-update-slice_fusion.14
  54.2 1.9 %fusion.6 = f32[8,256,128]{1,2,0:T(8,128)S(1)} fusion(f32[8,192,128]{2,1,0:T(8,128)S(1)} %multiply_dynamic-update-slice_fusion.12, f32[256,192,1]{0,1,2:T(8,128)S(1)} %copy-done, f32[10,256,128]{1,2,0:T(8,128)S(1)} %convolution_bitcast_fusion, f32[4,64,128]{1,2,0:T(8,128)S(1)} %get-tuple-element.34, f32[4,64,128]{1,2,0:T(8,128)S(1)} %get-tuple-element.33, ...), kind=kOutput, calls=%fused_computation.10 | convolution fusion | flops 605814784 | bytes 3473408 | tf_op jit(solution)/shard_map/ck,skr->scr/dot_general | solution.py:120
  56.1 0.0 copy-start.3
  56.2 1.3 %convolution_bitcast_fusion.4 = f32[8,192,128]{2,1,0:T(8,128)S(1)} fusion(f32[256,192,1]{0,1,2:T(8,128)S(1)} %copy-done, f32[8,256,128]{1,2,0:T(8,128)S(1)} %fusion.6, f32[4,256,128]{1,2,0:T(8,128)S(1)} %copy.32, f32[4,256,128]{1,2,0:T(8,128)S(1)} %copy.31), kind=kOutput, calls=%fused_computation.19 | convolution fusion | flops 604766208 | bytes 3080192 | tf_op jit(solution)/shard_map/ck,scr->skr/dot_general | solution.py:110
  57.5 1.0 fusion.7
  58.5 0.0 copy-start.21
  58.6 2.4 %collective-permute-start.4 = (f32[8,32,128]{2,1,0:T(8,128)S(1)}, f32[8,32,128]{2,1,0:T(8,128)S(1)}, u32[]{:S(2)}, u32[]{:S(2)}) collective-permute-start(f32[8,32,128]{2,1,0:T(8,128)S(1)} %get-tuple-element.15), channel_id=1, source_target_pairs={{0,16},{16,32},{32,48},{48,64},{64,80},{80,96},{96,112},{112,128},... | collective-permute-start | bytes 393224 | tf_op jit(solution)/shard_map/ppermute | solution.py:15
  61.0 2.0 %collective-permute-start.5 = (f32[8,32,128]{2,1,0:T(8,128)S(1)}, f32[8,32,128]{2,1,0:T(8,128)S(1)}, u32[]{:S(2)}, u32[]{:S(2)}) collective-permute-start(f32[8,32,128]{2,1,0:T(8,128)S(1)} %get-tuple-element.18), channel_id=1, source_target_pairs={{16,0},{32,16},{48,32},{64,48},{80,64},{96,80},{112,96},{128,112},... | collective-permute-start | bytes 393224 | tf_op jit(solution)/shard_map/ppermute | solution.py:15
  62.9 1.0 collective-permute-start.6
  64.0 4.4 %collective-permute-start.7 = (f32[8,32,128]{2,1,0:T(8,128)S(1)}, f32[8,32,128]{2,1,0:T(8,128)S(1)}, u32[]{:S(2)}, u32[]{:S(2)}) collective-permute-start(f32[8,32,128]{2,1,0:T(8,128)S(1)} %get-tuple-element.16), channel_id=1, source_target_pairs={{0,15},{1,0},{2,1},{3,2},{4,3},{5,4},{6,5},{7,6},{8,7},{9,8},{10,9... | collective-permute-start | bytes 393224 | tf_op jit(solution)/shard_map/ppermute | solution.py:21
  68.4 0.1 fusion.71
  68.5 3.7 %collective-permute-done.6 = f32[8,32,128]{2,1,0:T(8,128)S(1)} collective-permute-done((f32[8,32,128]{2,1,0:T(8,128)S(1)}, f32[8,32,128]{2,1,0:T(8,128)S(1)}, u32[]{:S(2)}, u32[]{:S(2)}) %collective-permute-start.6) | collective-permute-done | bytes 131104 | tf_op jit(solution)/shard_map/ppermute | solution.py:21
  72.2 0.6 fusion.17
  72.8 0.6 fusion.16
  73.4 0.6 fusion.15
  74.2 0.1 multiply_dynamic-update-slice_fusion.3
  74.3 0.1 multiply_dynamic-update-slice_fusion.2
  74.5 0.0 copy-start.18
  74.5 0.0 copy-start.15
  74.6 1.9 %fusion.4 = f32[8,256,128]{1,2,0:T(8,128)S(1)} fusion(f32[8,256,128]{1,2,0:T(8,128)S(1)} %fusion.6, f32[8,256,128]{1,2,0:T(8,128)S(1)} %fusion.7, f32[8,192,128]{2,1,0:T(8,128)S(1)} %multiply_dynamic-update-slice_fusion, f32[256,192,1]{0,1,2:T(8,128)S(1)} %copy-done, f32[4,64,128]{1,2,0:T(8,128)S(1)} %get-tuple-element.34, ...), kind=kOutput, calls=%fused_computation.6 | convolution fusion | flops 606601216 | bytes 5439488 | tf_op jit(solution)/shard_map/ck,skr->scr/dot_general | solution.py:120
  76.5 0.3 fusion.35
  76.8 0.2 multiply_reduce_fusion
  77.0 0.8 fusion.37
  77.9 14.4 %all-to-all-start.1 = ((f32[256,1,4]{2,1,0:T(1,128)}), f32[256,1,4]{2,1,0:T(1,128)S(1)}, u32[]{:S(2)}, u32[]{:S(2)}) async-start(f32[256,1,4]{2,1,0:T(1,128)} %bitcast.54), calls=%async_computation.1 | async-start | bytes 262144 | tf_op jit(solution)/shard_map/all_to_all | solution.py:187
  92.3 0.1 fusion.70
  92.3 1.0 copy.40
  93.3 1.0 copy.41
  94.3 10.8 %all-to-all-done.1 = f32[256,1,4]{2,1,0:T(1,128)S(1)} async-done(((f32[256,1,4]{2,1,0:T(1,128)}), f32[256,1,4]{2,1,0:T(1,128)S(1)}, u32[]{:S(2)}, u32[]{:S(2)}) %all-to-all-start.1) | async-done | bytes 4128 | tf_op jit(solution)/shard_map/all_to_all | solution.py:187
  105.2 0.8 reduce_sum.9
  (63 shorter events, 0.7 us)
Async XLA Ops:
  0.6 1.6 %copy-start = (f32[256,192,1]{0,1,2:T(8,128)S(1)}, f32[256,192,1]{0,1,2:T(8,128)}, u32[]{:S(2)}) copy-start(f32[256,192,1]{0,1,2:T(8,128)} %constant.70) | copy-start | bytes 589828
  0.6 1.3 %copy-start.5 = (f32[4,256,128]{2,1,0:T(8,128)S(1)}, f32[4,256,128]{2,1,0:T(8,128)}, u32[]{:S(2)}) copy-start(f32[4,256,128]{2,1,0:T(8,128)} %param.21) | copy-start | bytes 1572868
  2.2 15.4 %copy-start.17 = (f32[4,1]{0,1:T(1,128)S(1)}, f32[4,1]{0,1:T(1,128)}, u32[]{:S(2)}) copy-start(f32[4,1]{0,1:T(1,128)} %param.26) | copy-start | bytes 52
  3.4 32.7 %copy-start.7 = (f32[256,128]{1,0:T(8,128)S(1)}, f32[256,128]{1,0:T(8,128)}, u32[]{:S(2)}) copy-start(f32[256,128]{1,0:T(8,128)} %param.18) | copy-start | bytes 393220
  3.5 32.8 %copy-start.6 = (f32[256,128]{1,0:T(8,128)S(1)}, f32[256,128]{1,0:T(8,128)}, u32[]{:S(2)}) copy-start(f32[256,128]{1,0:T(8,128)} %param.19) | copy-start | bytes 393220
  3.5 33.5 %copy-start.8 = (f32[256,64]{1,0:T(8,128)S(1)}, f32[256,64]{1,0:T(8,128)}, u32[]{:S(2)}) copy-start(f32[256,64]{1,0:T(8,128)} %constant.67) | copy-start | bytes 196612
  3.5 34.4 %copy-start.13 = (f32[128]{0:T(128)S(1)}, f32[128]{0:T(128)}, u32[]{:S(2)}) copy-start(f32[128]{0:T(128)} %param.23) | copy-start | bytes 1540
  3.5 34.4 %copy-start.20 = (f32[128]{0:T(128)S(1)}, f32[128]{0:T(128)}, u32[]{:S(2)}) copy-start(f32[128]{0:T(128)} %param.22) | copy-start | bytes 1540
  4.3 45.6 %collective-permute-start.2 = (f32[8,32,128]{2,1,0:T(8,128)}, f32[8,32,128]{2,1,0:T(8,128)}, u32[]{:S(2)}, u32[]{:S(2)}) collective-permute-start(f32[8,32,128]{2,1,0:T(8,128)} %get-tuple-element.23), channel_id=1, source_target_pairs={{0,1},{1,2},{2,3},{3,4},{4,5},{5,6},{6,7},{7,8},{8,9},{9,10},{10,1... | collective-permute-start | bytes 393224 | tf_op jit(solution)/shard_map/ppermute | solution.py:21
  6.8 43.1 %collective-permute-start.3 = (f32[8,32,128]{2,1,0:T(8,128)}, f32[8,32,128]{2,1,0:T(8,128)}, u32[]{:S(2)}, u32[]{:S(2)}) collective-permute-start(f32[8,32,128]{2,1,0:T(8,128)} %get-tuple-element.22), channel_id=1, source_target_pairs={{0,15},{1,0},{2,1},{3,2},{4,3},{5,4},{6,5},{7,6},{8,7},{9,8},{10,9... | collective-permute-start | bytes 393224 | tf_op jit(solution)/shard_map/ppermute | solution.py:21
  11.7 38.2 %collective-permute-start = (f32[8,32,128]{2,1,0:T(8,128)}, f32[8,32,128]{2,1,0:T(8,128)}, u32[]{:S(2)}, u32[]{:S(2)}) collective-permute-start(f32[8,32,128]{2,1,0:T(8,128)} %get-tuple-element.21), channel_id=1, source_target_pairs={{0,16},{16,32},{32,48},{48,64},{64,80},{80,96},{96,112},{112,128},... | collective-permute-start | bytes 393224 | tf_op jit(solution)/shard_map/ppermute | solution.py:15
  15.7 34.2 %collective-permute-start.1 = (f32[8,32,128]{2,1,0:T(8,128)}, f32[8,32,128]{2,1,0:T(8,128)}, u32[]{:S(2)}, u32[]{:S(2)}) collective-permute-start(f32[8,32,128]{2,1,0:T(8,128)} %get-tuple-element.24), channel_id=1, source_target_pairs={{16,0},{32,16},{48,32},{64,48},{80,64},{96,80},{112,96},{128,112},... | collective-permute-start | bytes 393224 | tf_op jit(solution)/shard_map/ppermute | solution.py:15
  18.4 29.3 %all-to-all-start = ((f32[256,1,4]{2,1,0:T(1,128)}), f32[256,1,4]{2,1,0:T(1,128)}, u32[]{:S(2)}, u32[]{:S(2)}) async-start(f32[256,1,4]{2,1,0:T(1,128)} %broadcast_in_dim.134), calls=%async_computation | async-start | bytes 262144 | tf_op jit(solution)/shard_map/all_to_all | solution.py:183
  38.4 3.0 %copy-start.16 = (s32[4,128]{1,0:T(4,128)S(1)}, s32[4,128]{1,0:T(4,128)}, u32[]{:S(2)}) copy-start(s32[4,128]{1,0:T(4,128)} %param.24) | copy-start | bytes 6148
  48.8 3.0 %copy-start.10 = (f32[32,32,1,1]{1,0,3,2:T(8,128)S(1)}, f32[32,32,1,1]{1,0,3,2:T(8,128)}, u32[]{:S(2)}) copy-start(f32[32,32,1,1]{1,0,3,2:T(8,128)} %constant.72) | copy-start | bytes 12292
  48.8 3.0 %copy-start.11 = (pred[4,128]{1,0:T(4,128)(4,1)S(1)}, pred[4,128]{1,0:T(4,128)(4,1)}, u32[]{:S(2)}) copy-start(pred[4,128]{1,0:T(4,128)(4,1)} %get-tuple-element.37) | copy-start | bytes 1540
  49.9 2.5 %copy-start.9 = (f32[32,32,1,1]{1,0,3,2:T(8,128)S(1)}, f32[32,32,1,1]{1,0,3,2:T(8,128)}, u32[]{:S(2)}) copy-start(f32[32,32,1,1]{1,0,3,2:T(8,128)} %constant.73) | copy-start | bytes 12292
  53.0 0.9 copy-start.2
  53.1 1.1 copy-start.1
  56.1 1.3 %copy-start.3 = (f32[256,256,1]{1,0,2:T(8,128)S(1)}, f32[256,256,1]{1,0,2:T(8,128)}, u32[]{:S(2)}) copy-start(f32[256,256,1]{1,0,2:T(8,128)} %constant.69) | copy-start | bytes 786436
  58.5 13.7 %copy-start.19 = (pred[4,128]{1,0:T(4,128)(4,1)S(1)}, pred[4,128]{1,0:T(4,128)(4,1)}, u32[]{:S(2)}) copy-start(pred[4,128]{1,0:T(4,128)(4,1)} %get-tuple-element.36) | copy-start | bytes 1540
  58.5 13.7 %copy-start.21 = (f32[32,32,1,1]{1,0,3,2:T(8,128)S(1)}, f32[32,32,1,1]{1,0,3,2:T(8,128)}, u32[]{:S(2)}) copy-start(f32[32,32,1,1]{1,0,3,2:T(8,128)} %constant.71) | copy-start | bytes 12292
  58.6 9.9 %collective-permute-start.4 = (f32[8,32,128]{2,1,0:T(8,128)S(1)}, f32[8,32,128]{2,1,0:T(8,128)S(1)}, u32[]{:S(2)}, u32[]{:S(2)}) collective-permute-start(f32[8,32,128]{2,1,0:T(8,128)S(1)} %get-tuple-element.15), channel_id=1, source_target_pairs={{0,16},{16,32},{32,48},{48,64},{64,80},{80,96},{96,112},{112,128},... | collective-permute-start | bytes 393224 | tf_op jit(solution)/shard_map/ppermute | solution.py:15
  61.0 7.5 %collective-permute-start.5 = (f32[8,32,128]{2,1,0:T(8,128)S(1)}, f32[8,32,128]{2,1,0:T(8,128)S(1)}, u32[]{:S(2)}, u32[]{:S(2)}) collective-permute-start(f32[8,32,128]{2,1,0:T(8,128)S(1)} %get-tuple-element.18), channel_id=1, source_target_pairs={{16,0},{32,16},{48,32},{64,48},{80,64},{96,80},{112,96},{128,112},... | collective-permute-start | bytes 393224 | tf_op jit(solution)/shard_map/ppermute | solution.py:15
  62.9 9.3 %collective-permute-start.6 = (f32[8,32,128]{2,1,0:T(8,128)S(1)}, f32[8,32,128]{2,1,0:T(8,128)S(1)}, u32[]{:S(2)}, u32[]{:S(2)}) collective-permute-start(f32[8,32,128]{2,1,0:T(8,128)S(1)} %get-tuple-element.17), channel_id=1, source_target_pairs={{0,1},{1,2},{2,3},{3,4},{4,5},{5,6},{6,7},{7,8},{8,9},{9,10},{10,1... | collective-permute-start | bytes 393224 | tf_op jit(solution)/shard_map/ppermute | solution.py:21
  64.0 8.2 %collective-permute-start.7 = (f32[8,32,128]{2,1,0:T(8,128)S(1)}, f32[8,32,128]{2,1,0:T(8,128)S(1)}, u32[]{:S(2)}, u32[]{:S(2)}) collective-permute-start(f32[8,32,128]{2,1,0:T(8,128)S(1)} %get-tuple-element.16), channel_id=1, source_target_pairs={{0,15},{1,0},{2,1},{3,2},{4,3},{5,4},{6,5},{7,6},{8,7},{9,8},{10,9... | collective-permute-start | bytes 393224 | tf_op jit(solution)/shard_map/ppermute | solution.py:21
  74.5 2.0 %copy-start.18 = (f32[64,1,1]{0,1,2:T(1,128)S(1)}, f32[64,1,1]{0,1,2:T(1,128)}, u32[]{:S(2)}) copy-start(f32[64,1,1]{0,1,2:T(1,128)} %constant.74) | copy-start | bytes 772
  74.5 2.3 %copy-start.4 = (f32[128,256]{1,0:T(8,128)S(1)}, f32[128,256]{1,0:T(8,128)}, u32[]{:S(2)}) copy-start(f32[128,256]{1,0:T(8,128)} %copy.54) | copy-start | bytes 393220
  74.5 2.5 %copy-start.12 = (s32[128]{0:T(128)S(1)}, s32[128]{0:T(128)}, u32[]{:S(2)}) copy-start(s32[128]{0:T(128)} %param.25) | copy-start | bytes 1540
  74.5 2.5 %copy-start.14 = (f32[128]{0:T(128)S(1)}, f32[128]{0:T(128)}, u32[]{:S(2)}) copy-start(f32[128]{0:T(128)} %param.23) | copy-start | bytes 1540
  74.5 2.5 %copy-start.15 = (f32[128]{0:T(128)S(1)}, f32[128]{0:T(128)}, u32[]{:S(2)}) copy-start(f32[128]{0:T(128)} %get-tuple-element.38) | copy-start | bytes 1540
  77.9 27.3 %all-to-all-start.1 = ((f32[256,1,4]{2,1,0:T(1,128)}), f32[256,1,4]{2,1,0:T(1,128)S(1)}, u32[]{:S(2)}, u32[]{:S(2)}) async-start(f32[256,1,4]{2,1,0:T(1,128)} %bitcast.54), calls=%async_computation.1 | async-start | bytes 262144 | tf_op jit(solution)/shard_map/all_to_all | solution.py:187

commit v7 on v6

--- a/solution.py
+++ b/solution.py
@@ -118,6 +118,8 @@
             1,
         )
         lifted = jnp.einsum("ck,skr->scr", selects, face_rates, precision=lax.Precision.HIGHEST)
+        if mixed is None:
+            field_now, _ = lax.optimization_barrier((field_now, neighbours[6]))
         volume = volume_rate(field_now, coupling, bulk_modulus, inverse_size, mixed)
         return volume + lifted + sources
 
@@ -239,7 +241,7 @@
         sides = [from_south, from_north, from_west, from_east]
         horizontal = reorient(sides, face_codes, orient)
         below_trace, above_trace = radial_neighbours(traces[4], traces[5])
-        return horizontal + [below_trace, above_trace]
+        return horizontal + [below_trace, above_trace, from_south]
 
     states = batch[: 2 * probe_count]
     sources = pressure_source(perturb, forward_div, adjoint_div)

time: 106 us -> 108 us (1.019)
  starting transfers between devices: 54.5 us -> 57.6 us
  waiting for transfers between devices: 18.5 us -> 16.1 us
    all_to_all x1, starting transfers between devices: 14.4 us -> 18.9 us  [scatter_sums(): pieces = lax.all_to_all(partial.T, ('lat', 'lon'), 0, 0, tiled=True)]
    all_to_all x1, waiting for transfers between devices: 3.97 us -> 0.01 us  [gather_blocks(): return lax.all_to_all(spread, ('lat', 'lon'), 0, 0, tiled=True).T]
    ppermute x4, waiting for transfers between devices: 3.69 us -> 5.31 us  [from_behind(): return lax.ppermute(value, axis, pairs)]
    unnamed x51 -> x49, local copies, waits for them, and re-layouts: 6.76 us -> 6.7 us
  transfers between devices with their start and end apart: 10 -> 10, of which waited for: 3 -> 2; matrix products, arithmetic and copies ran while one was open for 13% -> 16% of each run, Pallas kernels for 0% -> 0%
where the time goes in v7:
time: 108 us; the launch traced here: 107 us
  starting transfers between devices  57.6 us (53%)
  matrix products  17.6 us (16%)
  waiting for transfers between devices  16.1 us (15%)
  local copies, waits for them, and re-layouts  9.98 us (9%)
  other arithmetic  4.75 us (4%)
  between operations  1.3 us (1%)
    all_to_all x1, starting transfers between devices, scatter_sums(): pieces = lax.all_to_all(partial.T, ('lat', 'lon'), 0, 0, tiled=True)  18.9 us
    all_to_all x1, starting transfers between devices, gather_blocks(): return lax.all_to_all(spread, ('lat', 'lon'), 0, 0, tiled=True).T  16.6 us
    ppermute x4, starting transfers between devices, from_behind(): return lax.ppermute(value, axis, pairs)  11.9 us
    all_to_all x1, waiting for transfers between devices, scatter_sums(): pieces = lax.all_to_all(partial.T, ('lat', 'lon'), 0, 0, tiled=True)  10.8 us
    ppermute x4, starting transfers between devices, shifted(): return lax.ppermute(block, axis, route)  10.2 us
    unnamed x49, local copies, waits for them, and re-layouts  6.7 us
    ppermute x4, waiting for transfers between devices, from_behind(): return lax.ppermute(value, axis, pairs)  5.31 us
    dot_general x6, matrix products, reorient(): jnp.einsum('kj,fsjr->fskr', face_map(kind), stacked, precision=lax.Precis...  4.74 us
  transfers between devices with their start and end apart: 10, of which 2 were waited for; matrix products, arithmetic and copies ran while one was open for 16% of the time, Pallas kernels for 0%

profile of v7, /device:TPU:1, one launch (start us, length us, event | category | flops | bytes accessed | tf_op | source)
XLA Modules:
  0.0 107.4 jit_solution(8026331155958271063)
XLA Ops:
  0.6 0.0 copy-start
  0.7 1.4 %broadcast_in_dim.134 = f32[256,1,4]{2,1,0:T(1,128)} broadcast(f32[4]{0:T(128)} %bitcast.138), dimensions={2} | broadcast | bytes 4112 | tf_op jit(solution)/shard_map/broadcast_in_dim | solution.py:184
  2.1 16.6 %all-to-all-start = ((f32[256,1,4]{2,1,0:T(1,128)}), f32[256,1,4]{2,1,0:T(1,128)}, u32[]{:S(2)}, u32[]{:S(2)}) async-start(f32[256,1,4]{2,1,0:T(1,128)} %broadcast_in_dim.134), calls=%async_computation | async-start | bytes 262144 | tf_op jit(solution)/shard_map/all_to_all | solution.py:185
  18.8 1.2 %copy.32 = f32[4,256,128]{1,2,0:T(8,128)S(1)} copy(f32[4,256,128]{2,1,0:T(8,128)} %param.21) | data formatting | bytes 1048576 | tf_op args[3]
  20.0 0.2 copy.31
  20.2 0.0 copy-start.6
  20.2 1.2 %convolution_bitcast_fusion.5 = f32[8,192,128]{2,1,0:T(8,128)S(1)} fusion(f32[256,192,1]{0,1,2:T(8,128)S(1)} %copy-done, f32[4,256,128]{1,2,0:T(8,128)S(1)} %copy.32, f32[4,256,128]{1,2,0:T(8,128)S(1)} %copy.31), kind=kOutput, calls=%fused_computation.20 | convolution fusion | flops 604241920 | bytes 2031616 | tf_op jit(solution)/shard_map/ck,scr->skr/dot_general | solution.py:110
  21.5 0.0 copy-start.7
  21.5 0.0 copy-start.8
  21.5 0.0 copy-start.13
  21.5 0.0 copy-start.19
  21.5 0.8 fusion.70
  22.3 6.0 %collective-permute-start.3 = (f32[8,32,128]{2,1,0:T(8,128)}, f32[8,32,128]{2,1,0:T(8,128)}, u32[]{:S(2)}, u32[]{:S(2)}) collective-permute-start(f32[8,32,128]{2,1,0:T(8,128)} %get-tuple-element.24), channel_id=1, source_target_pairs={{0,15},{1,0},{2,1},{3,2},{4,3},{5,4},{6,5},{7,6},{8,7},{9,8},{10,9... | collective-permute-start | bytes 393224 | tf_op jit(solution)/shard_map/ppermute | solution.py:21
  28.3 2.6 %collective-permute-start.1 = (f32[8,32,128]{2,1,0:T(8,128)}, f32[8,32,128]{2,1,0:T(8,128)}, u32[]{:S(2)}, u32[]{:S(2)}) collective-permute-start(f32[8,32,128]{2,1,0:T(8,128)} %get-tuple-element.26), channel_id=1, source_target_pairs={{16,0},{32,16},{48,32},{64,48},{80,64},{96,80},{112,96},{128,112},... | collective-permute-start | bytes 393224 | tf_op jit(solution)/shard_map/ppermute | solution.py:15
  30.9 3.1 %collective-permute-start = (f32[8,32,128]{2,1,0:T(8,128)}, f32[8,32,128]{2,1,0:T(8,128)}, u32[]{:S(2)}, u32[]{:S(2)}) collective-permute-start(f32[8,32,128]{2,1,0:T(8,128)} %get-tuple-element.23), channel_id=1, source_target_pairs={{0,16},{16,32},{32,48},{48,64},{64,80},{80,96},{96,112},{112,128},... | collective-permute-start | bytes 393224 | tf_op jit(solution)/shard_map/ppermute | solution.py:15
  34.0 0.7 fusion.69
  34.7 0.1 copy.34
  34.8 0.8 copy.33
  35.6 0.9 convolution_bitcast_fusion.12
  36.5 0.5 fusion.61
  37.0 2.2 %convolution_bitcast_fusion = f32[10,256,128]{1,2,0:T(8,128)S(1)} fusion(f32[256,256,1]{1,0,2:T(8,128)} %constant.69, f32[1,256,128]{1,2,0:T(8,128)S(1)} %bitcast.135, f32[1,256,128]{1,2,0:T(8,128)} %bitcast.136, f32[4,256,128]{1,2,0:T(8,128)S(1)} %copy.32, f32[4,256,128]{1,2,0:T(8,128)S(1)} %copy.31), kind=kOutput, calls=%fused_computation | convolution fusion | flops 1007616000 | bytes 2883584 | tf_op jit(solution)/shard_map/cd,scr->sdr/dot_general | solution.py:234
  39.2 0.7 fusion.51
  39.9 0.1 broadcast_select_fusion
  40.0 0.6 and_compare_fusion.2
  40.6 1.7 %copy.54 = f32[128,256]{1,0:T(8,128)} copy(f32[128,256]{0,1:T(8,128)} %convolution_bitcast_fusion.12) | data formatting | bytes 262144
  42.3 1.2 %convolution_bitcast_fusion.13 = f32[4,128]{1,0:T(4,128)S(1)} fusion(f32[256,4]{1,0:T(8,128)} %bitcast.27, s32[128]{0:T(128)} %param.25), kind=kOutput, calls=%fused_computation.34 | convolution fusion | flops 1605632 | bytes 6656 | tf_op jit(solution)/shard_map/qb,be->qe/dot_general | solution.py:227
  43.5 1.0 broadcast_multiply_fusion.1
  44.5 0.0 copy-start.9
  44.5 1.9 %fusion.20 = f32[4,8,32,128]{3,2,1,0:T(8,128)S(1)} fusion(f32[32,32,1,1]{1,0,3,2:T(8,128)} %constant.71, f32[1,8,32,128]{3,2,1,0:T(8,128)} %bitcast.11, f32[1,8,32,128]{3,2,1,0:T(8,128)} %bitcast.10, f32[1,8,32,128]{3,2,1,0:T(8,128)} %bitcast.9, f32[1,8,32,128]{3,2,1,0:T(8,128)} %bitcast.8, pred[4,128]{1,0:T(4,128)(4,1)} %get-tuple-element.38), kind=kOutput, calls=%fused_computation.32 | convolution fusion | flops 51249152 | bytes 1053184 | tf_op jit(solution)/shard_map/kj,fsjr->fskr/dot_general | solution.py:175
  46.4 0.6 fusion.19
  47.0 0.6 fusion.18
  47.9 0.7 copy-done.2
  48.5 0.1 multiply_dynamic-update-slice_fusion.15
  48.7 0.1 multiply_dynamic-update-slice_fusion.14
  48.8 2.0 %multiply_add_fusion = (f32[8,256,128]{1,2,0:T(8,128)S(1)}, f32[8,256,128]{1,2,0:T(8,128)S(1)}) fusion(f32[4,256,128]{1,2,0:T(8,128)S(1)} %copy.32, f32[4,256,128]{1,2,0:T(8,128)S(1)} %copy.31, f32[4,64,128]{1,2,0:T(8,128)S(1)} %get-tuple-element.36, f32[4,64,128]{1,2,0:T(8,128)S(1)} %get-tuple-element.35, ...), kind=kOutput, calls=%fused_computation.39 | convolution fusion | flops 606601216 | bytes 5570560 | tf_op jit(solution)/shard_map/ck,skr->scr/dot_general | solution.py:120
  50.8 0.0 copy-start.3
  50.8 1.2 %convolution_bitcast_fusion.4 = f32[8,192,128]{2,1,0:T(8,128)S(1)} fusion(f32[8,256,128]{1,2,0:T(8,128)S(1)} %get-tuple-element.4, f32[256,192,1]{0,1,2:T(8,128)S(1)} %copy-done), kind=kOutput, calls=%fused_computation.19 | convolution fusion | flops 603979776 | bytes 2031616 | tf_op jit(solution)/shard_map/ck,scr->skr/dot_general | solution.py:110
  52.1 2.4 %collective-permute-start.4 = (f32[8,32,128]{2,1,0:T(8,128)S(1)}, f32[8,32,128]{2,1,0:T(8,128)S(1)}, u32[]{:S(2)}, u32[]{:S(2)}) collective-permute-start(f32[8,32,128]{2,1,0:T(8,128)S(1)} %get-tuple-element.20), channel_id=1, source_target_pairs={{0,16},{16,32},{32,48},{48,64},{64,80},{80,96},{96,112},{112,128},... | collective-permute-start | bytes 393224 | tf_op jit(solution)/shard_map/ppermute | solution.py:15
  54.5 5.9 %collective-permute-start.7 = (f32[8,32,128]{2,1,0:T(8,128)S(1)}, f32[8,32,128]{2,1,0:T(8,128)S(1)}, u32[]{:S(2)}, u32[]{:S(2)}) collective-permute-start(f32[8,32,128]{2,1,0:T(8,128)S(1)} %get-tuple-element.18), channel_id=1, source_target_pairs={{0,15},{1,0},{2,1},{3,2},{4,3},{5,4},{6,5},{7,6},{8,7},{9,8},{10,9... | collective-permute-start | bytes 393224 | tf_op jit(solution)/shard_map/ppermute | solution.py:21
  60.4 2.2 %collective-permute-start.5 = (f32[8,32,128]{2,1,0:T(8,128)S(1)}, f32[8,32,128]{2,1,0:T(8,128)S(1)}, u32[]{:S(2)}, u32[]{:S(2)}) collective-permute-start(f32[8,32,128]{2,1,0:T(8,128)S(1)} %get-tuple-element.17), channel_id=1, source_target_pairs={{16,0},{32,16},{48,32},{64,48},{80,64},{96,80},{112,96},{128,112},... | collective-permute-start | bytes 393224 | tf_op jit(solution)/shard_map/ppermute | solution.py:15
  62.6 0.1 fusion.67
  62.8 0.0 copy-start.20
  62.8 1.0 fusion.7
  63.8 5.3 %collective-permute-done.6 = f32[8,32,128]{2,1,0:T(8,128)S(1)} collective-permute-done((f32[8,32,128]{2,1,0:T(8,128)S(1)}, f32[8,32,128]{2,1,0:T(8,128)S(1)}, u32[]{:S(2)}, u32[]{:S(2)}) %collective-permute-start.6) | collective-permute-done | bytes 131104 | tf_op jit(solution)/shard_map/ppermute | solution.py:21
  69.1 0.6 fusion.17
  69.7 0.6 fusion.16
  70.3 0.6 fusion.15
  71.1 0.1 multiply_dynamic-update-slice_fusion.3
  71.2 0.1 multiply_dynamic-update-slice_fusion.2
  71.4 0.0 copy-start.17
  71.4 0.0 copy-start.4
  71.4 0.0 copy-start.12
  71.5 0.0 copy-start.14
  71.5 0.0 copy-start.15
  71.5 2.0 %fusion.4 = f32[8,256,128]{1,2,0:T(8,128)S(1)} fusion(f32[8,256,128]{1,2,0:T(8,128)S(1)} %get-tuple-element.47, f32[8,256,128]{1,2,0:T(8,128)S(1)} %fusion.7, f32[8,192,128]{2,1,0:T(8,128)S(1)} %multiply_dynamic-update-slice_fusion, f32[256,192,1]{0,1,2:T(8,128)S(1)} %copy-done, f32[4,64,128]{1,2,0:T(8,128)S(1)} %get-tuple-element.36, ...), kind=kOutput, calls=%fused_computation.6 | convolution fusion | flops 606601216 | bytes 5439488 | tf_op jit(solution)/shard_map/ck,skr->scr/dot_general | solution.py:120
  73.5 0.3 fusion.35
  73.8 0.2 multiply_reduce_fusion
  74.0 0.8 fusion.37
  74.8 18.9 %all-to-all-start.1 = ((f32[256,1,4]{2,1,0:T(1,128)}), f32[256,1,4]{2,1,0:T(1,128)S(1)}, u32[]{:S(2)}, u32[]{:S(2)}) async-start(f32[256,1,4]{2,1,0:T(1,128)} %bitcast.54), calls=%async_computation.1 | async-start | bytes 262144 | tf_op jit(solution)/shard_map/all_to_all | solution.py:189
  93.7 0.1 fusion.66
  93.8 1.0 copy.40
  94.8 1.0 copy.41
  95.8 10.8 %all-to-all-done.1 = f32[256,1,4]{2,1,0:T(1,128)S(1)} async-done(((f32[256,1,4]{2,1,0:T(1,128)}), f32[256,1,4]{2,1,0:T(1,128)S(1)}, u32[]{:S(2)}, u32[]{:S(2)}) %all-to-all-start.1) | async-done | bytes 4128 | tf_op jit(solution)/shard_map/all_to_all | solution.py:189
  106.6 0.8 reduce_sum.9
  (61 shorter events, 0.7 us)
Async XLA Ops:
  0.6 19.6 %copy-start = (f32[256,192,1]{0,1,2:T(8,128)S(1)}, f32[256,192,1]{0,1,2:T(8,128)}, u32[]{:S(2)}) copy-start(f32[256,192,1]{0,1,2:T(8,128)} %constant.70) | copy-start | bytes 589828
  0.6 19.4 %copy-start.5 = (f32[4,256,128]{2,1,0:T(8,128)S(1)}, f32[4,256,128]{2,1,0:T(8,128)}, u32[]{:S(2)}) copy-start(f32[4,256,128]{2,1,0:T(8,128)} %param.20) | copy-start | bytes 1572868
  2.1 40.2 %all-to-all-start = ((f32[256,1,4]{2,1,0:T(1,128)}), f32[256,1,4]{2,1,0:T(1,128)}, u32[]{:S(2)}, u32[]{:S(2)}) async-start(f32[256,1,4]{2,1,0:T(1,128)} %broadcast_in_dim.134), calls=%async_computation | async-start | bytes 262144 | tf_op jit(solution)/shard_map/all_to_all | solution.py:185
  20.2 14.5 %copy-start.6 = (f32[256,128]{1,0:T(8,128)S(1)}, f32[256,128]{1,0:T(8,128)}, u32[]{:S(2)}) copy-start(f32[256,128]{1,0:T(8,128)} %param.19) | copy-start | bytes 393220
  21.5 13.3 %copy-start.7 = (f32[256,128]{1,0:T(8,128)S(1)}, f32[256,128]{1,0:T(8,128)}, u32[]{:S(2)}) copy-start(f32[256,128]{1,0:T(8,128)} %param.18) | copy-start | bytes 393220
  21.5 14.1 %copy-start.8 = (f32[256,64]{1,0:T(8,128)S(1)}, f32[256,64]{1,0:T(8,128)}, u32[]{:S(2)}) copy-start(f32[256,64]{1,0:T(8,128)} %constant.67) | copy-start | bytes 196612
  21.5 15.0 %copy-start.13 = (f32[128]{0:T(128)S(1)}, f32[128]{0:T(128)}, u32[]{:S(2)}) copy-start(f32[128]{0:T(128)} %param.23) | copy-start | bytes 1540
  21.5 15.0 %copy-start.19 = (f32[128]{0:T(128)S(1)}, f32[128]{0:T(128)}, u32[]{:S(2)}) copy-start(f32[128]{0:T(128)} %param.22) | copy-start | bytes 1540
  22.3 22.1 %collective-permute-start.3 = (f32[8,32,128]{2,1,0:T(8,128)}, f32[8,32,128]{2,1,0:T(8,128)}, u32[]{:S(2)}, u32[]{:S(2)}) collective-permute-start(f32[8,32,128]{2,1,0:T(8,128)} %get-tuple-element.24), channel_id=1, source_target_pairs={{0,15},{1,0},{2,1},{3,2},{4,3},{5,4},{6,5},{7,6},{8,7},{9,8},{10,9... | collective-permute-start | bytes 393224 | tf_op jit(solution)/shard_map/ppermute | solution.py:21
  28.3 16.2 %collective-permute-start.2 = (f32[8,32,128]{2,1,0:T(8,128)}, f32[8,32,128]{2,1,0:T(8,128)}, u32[]{:S(2)}, u32[]{:S(2)}) collective-permute-start(f32[8,32,128]{2,1,0:T(8,128)} %get-tuple-element.25), channel_id=1, source_target_pairs={{0,1},{1,2},{2,3},{3,4},{4,5},{5,6},{6,7},{7,8},{8,9},{9,10},{10,1... | collective-permute-start | bytes 393224 | tf_op jit(solution)/shard_map/ppermute | solution.py:21
  28.3 16.2 %collective-permute-start.1 = (f32[8,32,128]{2,1,0:T(8,128)}, f32[8,32,128]{2,1,0:T(8,128)}, u32[]{:S(2)}, u32[]{:S(2)}) collective-permute-start(f32[8,32,128]{2,1,0:T(8,128)} %get-tuple-element.26), channel_id=1, source_target_pairs={{16,0},{32,16},{48,32},{64,48},{80,64},{96,80},{112,96},{128,112},... | collective-permute-start | bytes 393224 | tf_op jit(solution)/shard_map/ppermute | solution.py:15
  30.9 13.6 %collective-permute-start = (f32[8,32,128]{2,1,0:T(8,128)}, f32[8,32,128]{2,1,0:T(8,128)}, u32[]{:S(2)}, u32[]{:S(2)}) collective-permute-start(f32[8,32,128]{2,1,0:T(8,128)} %get-tuple-element.23), channel_id=1, source_target_pairs={{0,16},{16,32},{32,48},{48,64},{64,80},{80,96},{96,112},{112,128},... | collective-permute-start | bytes 393224 | tf_op jit(solution)/shard_map/ppermute | solution.py:15
  37.0 3.0 %copy-start.16 = (s32[4,128]{1,0:T(4,128)S(1)}, s32[4,128]{1,0:T(4,128)}, u32[]{:S(2)}) copy-start(s32[4,128]{1,0:T(4,128)} %param.24) | copy-start | bytes 6148
  43.5 3.0 %copy-start.10 = (f32[32,32,1,1]{1,0,3,2:T(8,128)S(1)}, f32[32,32,1,1]{1,0,3,2:T(8,128)}, u32[]{:S(2)}) copy-start(f32[32,32,1,1]{1,0,3,2:T(8,128)} %constant.72) | copy-start | bytes 12292
  43.5 3.0 %copy-start.11 = (pred[4,128]{1,0:T(4,128)(4,1)S(1)}, pred[4,128]{1,0:T(4,128)(4,1)}, u32[]{:S(2)}) copy-start(pred[4,128]{1,0:T(4,128)(4,1)} %get-tuple-element.39) | copy-start | bytes 1540
  44.5 2.5 %copy-start.9 = (f32[32,32,1,1]{1,0,3,2:T(8,128)S(1)}, f32[32,32,1,1]{1,0,3,2:T(8,128)}, u32[]{:S(2)}) copy-start(f32[32,32,1,1]{1,0,3,2:T(8,128)} %constant.73) | copy-start | bytes 12292
  47.6 0.9 copy-start.2
  47.7 1.1 copy-start.1
  50.8 12.0 %copy-start.3 = (f32[256,256,1]{1,0,2:T(8,128)S(1)}, f32[256,256,1]{1,0,2:T(8,128)}, u32[]{:S(2)}) copy-start(f32[256,256,1]{1,0,2:T(8,128)} %constant.69) | copy-start | bytes 786436
  52.1 10.6 %collective-permute-start.4 = (f32[8,32,128]{2,1,0:T(8,128)S(1)}, f32[8,32,128]{2,1,0:T(8,128)S(1)}, u32[]{:S(2)}, u32[]{:S(2)}) collective-permute-start(f32[8,32,128]{2,1,0:T(8,128)S(1)} %get-tuple-element.20), channel_id=1, source_target_pairs={{0,16},{16,32},{32,48},{48,64},{64,80},{80,96},{96,112},{112,128},... | collective-permute-start | bytes 393224 | tf_op jit(solution)/shard_map/ppermute | solution.py:15
  54.5 9.3 %collective-permute-start.7 = (f32[8,32,128]{2,1,0:T(8,128)S(1)}, f32[8,32,128]{2,1,0:T(8,128)S(1)}, u32[]{:S(2)}, u32[]{:S(2)}) collective-permute-start(f32[8,32,128]{2,1,0:T(8,128)S(1)} %get-tuple-element.18), channel_id=1, source_target_pairs={{0,15},{1,0},{2,1},{3,2},{4,3},{5,4},{6,5},{7,6},{8,7},{9,8},{10,9... | collective-permute-start | bytes 393224 | tf_op jit(solution)/shard_map/ppermute | solution.py:21
  60.4 8.7 %collective-permute-start.6 = (f32[8,32,128]{2,1,0:T(8,128)S(1)}, f32[8,32,128]{2,1,0:T(8,128)S(1)}, u32[]{:S(2)}, u32[]{:S(2)}) collective-permute-start(f32[8,32,128]{2,1,0:T(8,128)S(1)} %get-tuple-element.19), channel_id=1, source_target_pairs={{0,1},{1,2},{2,3},{3,4},{4,5},{5,6},{6,7},{7,8},{8,9},{9,10},{10,1... | collective-permute-start | bytes 393224 | tf_op jit(solution)/shard_map/ppermute | solution.py:21
  60.4 8.7 %collective-permute-start.5 = (f32[8,32,128]{2,1,0:T(8,128)S(1)}, f32[8,32,128]{2,1,0:T(8,128)S(1)}, u32[]{:S(2)}, u32[]{:S(2)}) collective-permute-start(f32[8,32,128]{2,1,0:T(8,128)S(1)} %get-tuple-element.17), channel_id=1, source_target_pairs={{16,0},{32,16},{48,32},{64,48},{80,64},{96,80},{112,96},{128,112},... | collective-permute-start | bytes 393224 | tf_op jit(solution)/shard_map/ppermute | solution.py:15
  62.7 6.4 %copy-start.18 = (pred[4,128]{1,0:T(4,128)(4,1)S(1)}, pred[4,128]{1,0:T(4,128)(4,1)}, u32[]{:S(2)}) copy-start(pred[4,128]{1,0:T(4,128)(4,1)} %get-tuple-element.38) | copy-start | bytes 1540
  62.8 6.4 %copy-start.20 = (f32[32,32,1,1]{1,0,3,2:T(8,128)S(1)}, f32[32,32,1,1]{1,0,3,2:T(8,128)}, u32[]{:S(2)}) copy-start(f32[32,32,1,1]{1,0,3,2:T(8,128)} %constant.71) | copy-start | bytes 12292
  71.4 2.0 %copy-start.17 = (f32[64,1,1]{0,1,2:T(1,128)S(1)}, f32[64,1,1]{0,1,2:T(1,128)}, u32[]{:S(2)}) copy-start(f32[64,1,1]{0,1,2:T(1,128)} %constant.74) | copy-start | bytes 772
  71.4 2.4 %copy-start.4 = (f32[128,256]{1,0:T(8,128)S(1)}, f32[128,256]{1,0:T(8,128)}, u32[]{:S(2)}) copy-start(f32[128,256]{1,0:T(8,128)} %copy.54) | copy-start | bytes 393220
  71.4 2.5 %copy-start.12 = (s32[128]{0:T(128)S(1)}, s32[128]{0:T(128)}, u32[]{:S(2)}) copy-start(s32[128]{0:T(128)} %param.25) | copy-start | bytes 1540
  71.5 2.5 %copy-start.14 = (f32[128]{0:T(128)S(1)}, f32[128]{0:T(128)}, u32[]{:S(2)}) copy-start(f32[128]{0:T(128)} %param.23) | copy-start | bytes 1540
  71.5 2.5 %copy-start.15 = (f32[128]{0:T(128)S(1)}, f32[128]{0:T(128)}, u32[]{:S(2)}) copy-start(f32[128]{0:T(128)} %get-tuple-element.40) | copy-start | bytes 1540
  74.8 31.8 %all-to-all-start.1 = ((f32[256,1,4]{2,1,0:T(1,128)}), f32[256,1,4]{2,1,0:T(1,128)S(1)}, u32[]{:S(2)}, u32[]{:S(2)}) async-start(f32[256,1,4]{2,1,0:T(1,128)} %bitcast.54), calls=%async_computation.1 | async-start | bytes 262144 | tf_op jit(solution)/shard_map/all_to_all | solution.py:189

commit v8 on v6

--- a/solution.py
+++ b/solution.py
@@ -3,6 +3,7 @@
 import numpy as np
 from jax import lax
 from jax.sharding import PartitionSpec as P
+from jax.experimental.layout import Layout, with_layout_constraint
 
 TIME_STEP = 0.05
 PENALTY = 1.0
@@ -229,6 +230,7 @@
     batch = jnp.concatenate(
         [inc_forward, inc_adjoint, forward_state[None], adjoint_state[None]], 0
     )
+    batch = with_layout_constraint(batch, Layout(major_to_minor=(0, 1, 2)))
     mixed = jnp.einsum("cd,scr->sdr", coupling, batch, precision=lax.Precision.HIGHEST)
     forward_div = -inverse_size * mixed[2 * probe_count, :64]
     adjoint_div = -inverse_size * mixed[2 * probe_count + 1, :64]

time: 106 us -> 103 us (0.972)
  waiting for transfers between devices: 18.5 us -> 22.5 us
  local copies, waits for them, and re-layouts: 9.31 us -> 5.35 us
  matrix products: 17.6 us -> 16.1 us
    unnamed x51 -> x43, local copies, waits for them, and re-layouts: 6.76 us -> 1.99 us
    all_to_all x1, waiting for transfers between devices: 3.97 us -> 6.64 us  [gather_blocks(): return lax.all_to_all(spread, ('lat', 'lon'), 0, 0, tiled=True).T]
    mul x2, other arithmetic: 1.7 us -> 0.04 us  [pressure_source(): perturb[:, None, :] * forward_div[None]]
    dot_general x2, matrix products: 3.84 us -> 2.45 us  [rate_of(): jnp.einsum('ck,skr->scr', selects, face_rates, precision=lax.Precision.HI...]
    all_to_all x1, waiting for transfers between devices: 10.8 us -> 12.1 us  [scatter_sums(): pieces = lax.all_to_all(partial.T, ('lat', 'lon'), 0, 0, tiled=True)]
  transfers between devices with their start and end apart: 10 -> 10, of which waited for: 3 -> 3; matrix products, arithmetic and copies ran while one was open for 13% -> 8% of each run, Pallas kernels for 0% -> 0%
where the time goes in v8:
time: 103 us
  starting transfers between devices  53.8 us (52%)
  waiting for transfers between devices  22.5 us (22%)
  matrix products  16.1 us (16%)
  local copies, waits for them, and re-layouts  5.35 us (5%)
  other arithmetic  3.72 us (4%)
  between operations  1.27 us (1%)
    all_to_all x1, starting transfers between devices, gather_blocks(): return lax.all_to_all(spread, ('lat', 'lon'), 0, 0, tiled=True).T  17 us
    all_to_all x1, starting transfers between devices, scatter_sums(): pieces = lax.all_to_all(partial.T, ('lat', 'lon'), 0, 0, tiled=True)  13.5 us
    ppermute x4, starting transfers between devices, from_behind(): return lax.ppermute(value, axis, pairs)  13 us
    all_to_all x1, waiting for transfers between devices, scatter_sums(): pieces = lax.all_to_all(partial.T, ('lat', 'lon'), 0, 0, tiled=True)  12.1 us
    ppermute x4, starting transfers between devices, shifted(): return lax.ppermute(block, axis, route)  10.3 us
    all_to_all x1, waiting for transfers between devices, gather_blocks(): return lax.all_to_all(spread, ('lat', 'lon'), 0, 0, tiled=True).T  6.64 us
    dot_general x6, matrix products, reorient(): jnp.einsum('kj,fsjr->fskr', face_map(kind), stacked, precision=lax.Precis...  4.76 us
    ppermute x4, waiting for transfers between devices, from_behind(): return lax.ppermute(value, axis, pairs)  3.72 us
  transfers between devices with their start and end apart: 10, of which 3 were waited for; matrix products, arithmetic and copies ran while one was open for 8% of the time, Pallas kernels for 0%

profile of v8, /device:TPU:1, one launch (start us, length us, event | category | flops | bytes accessed | tf_op | source)
XLA Modules:
  0.0 102.8 jit_solution(10705441172920073220)
XLA Ops:
  0.6 0.0 copy-start
  0.6 0.0 copy-start.1
  0.7 1.1 %constant_dynamic-update-slice_fusion.1 = f32[8,256,128]{2,1,0:T(8,128)S(1)} fusion(f32[4,256,128]{2,1,0:T(8,128)} %param.20), kind=kLoop, calls=%fused_computation.135 | loop fusion | bytes 1048576
  1.8 0.1 copy-done.1
  1.9 0.0 copy-start.16
  1.9 0.9 convolution_bitcast_fusion.5
  2.9 0.0 copy-start.12
  2.9 0.0 copy-start.19
  2.9 0.0 copy-start.6
  2.9 0.0 copy-start.7
  2.9 0.8 fusion.70
  3.7 2.5 %collective-permute-start.2 = (f32[8,32,128]{2,1,0:T(8,128)}, f32[8,32,128]{2,1,0:T(8,128)}, u32[]{:S(2)}, u32[]{:S(2)}) collective-permute-start(f32[8,32,128]{2,1,0:T(8,128)} %get-tuple-element.17), channel_id=1, source_target_pairs={{0,1},{1,2},{2,3},{3,4},{4,5},{5,6},{6,7},{7,8},{8,9},{9,10},{10,1... | collective-permute-start | bytes 393224 | tf_op jit(solution)/shard_map/ppermute | solution.py:22
  6.2 4.9 %collective-permute-start.3 = (f32[8,32,128]{2,1,0:T(8,128)}, f32[8,32,128]{2,1,0:T(8,128)}, u32[]{:S(2)}, u32[]{:S(2)}) collective-permute-start(f32[8,32,128]{2,1,0:T(8,128)} %get-tuple-element.16), channel_id=1, source_target_pairs={{0,15},{1,0},{2,1},{3,2},{4,3},{5,4},{6,5},{7,6},{8,7},{9,8},{10,9... | collective-permute-start | bytes 393224 | tf_op jit(solution)/shard_map/ppermute | solution.py:22
  11.1 4.0 %collective-permute-start = (f32[8,32,128]{2,1,0:T(8,128)}, f32[8,32,128]{2,1,0:T(8,128)}, u32[]{:S(2)}, u32[]{:S(2)}) collective-permute-start(f32[8,32,128]{2,1,0:T(8,128)} %get-tuple-element.15), channel_id=1, source_target_pairs={{0,16},{16,32},{32,48},{48,64},{64,80},{80,96},{96,112},{112,128},... | collective-permute-start | bytes 393224 | tf_op jit(solution)/shard_map/ppermute | solution.py:16
  15.1 1.9 %collective-permute-start.1 = (f32[8,32,128]{2,1,0:T(8,128)}, f32[8,32,128]{2,1,0:T(8,128)}, u32[]{:S(2)}, u32[]{:S(2)}) collective-permute-start(f32[8,32,128]{2,1,0:T(8,128)} %get-tuple-element.18), channel_id=1, source_target_pairs={{16,0},{32,16},{48,32},{64,48},{80,64},{96,80},{112,96},{128,112},... | collective-permute-start | bytes 393224 | tf_op jit(solution)/shard_map/ppermute | solution.py:16
  17.0 0.7 broadcast_in_dim.134
  17.8 17.0 %all-to-all-start = ((f32[256,1,4]{2,1,0:T(1,128)}), f32[256,1,4]{2,1,0:T(1,128)}, u32[]{:S(2)}, u32[]{:S(2)}) async-start(f32[256,1,4]{2,1,0:T(1,128)} %broadcast_in_dim.134), calls=%async_computation | async-start | bytes 262144 | tf_op jit(solution)/shard_map/all_to_all | solution.py:184
  34.8 0.8 fusion.69
  35.6 0.5 fusion.61
  36.1 0.9 convolution_bitcast_fusion.12
  37.0 2.7 %convolution_bitcast_fusion = f32[10,256,128]{2,1,0:T(8,128)S(1)} fusion(f32[256,256,1]{1,0,2:T(8,128)} %constant.69, f32[1,256,128]{2,1,0:T(8,128)S(1)} %bitcast.134, f32[1,256,128]{2,1,0:T(8,128)} %bitcast.135, f32[4,256,128]{2,1,0:T(8,128)} %param.21, f32[4,256,128]{2,1,0:T(8,128)} %param.20), kind=kOutput, calls=%fused_computation | convolution fusion | flops 1007616000 | bytes 2883584 | tf_op jit(solution)/shard_map/cd,scr->sdr/dot_general | solution.py:234
  39.7 0.1 broadcast_select_fusion
  39.8 0.5 and_compare_fusion.2
  40.3 6.6 %all-to-all-done = f32[256,1,4]{2,1,0:T(1,128)} async-done(((f32[256,1,4]{2,1,0:T(1,128)}), f32[256,1,4]{2,1,0:T(1,128)}, u32[]{:S(2)}, u32[]{:S(2)}) %all-to-all-start) | async-done | bytes 4128 | tf_op jit(solution)/shard_map/all_to_all | solution.py:184
  47.0 1.2 %convolution_bitcast_fusion.13 = f32[4,128]{1,0:T(4,128)S(1)} fusion(f32[256,4]{1,0:T(8,128)} %bitcast.27, s32[128]{0:T(128)} %param.25), kind=kOutput, calls=%fused_computation.34 | convolution fusion | flops 1605632 | bytes 6656 | tf_op jit(solution)/shard_map/qb,be->qe/dot_general | solution.py:226
  48.2 0.0 collective-permute-done.2
  48.2 0.0 collective-permute-done.3
  48.2 0.0 copy-start.8
  48.2 1.9 %fusion.20 = f32[4,8,32,128]{3,2,1,0:T(8,128)S(1)} fusion(f32[32,32,1,1]{1,0,3,2:T(8,128)} %constant.71, f32[1,8,32,128]{3,2,1,0:T(8,128)} %bitcast.11, f32[1,8,32,128]{3,2,1,0:T(8,128)} %bitcast.10, f32[1,8,32,128]{3,2,1,0:T(8,128)} %bitcast.9, f32[1,8,32,128]{3,2,1,0:T(8,128)} %bitcast.8, pred[4,128]{1,0:T(4,128)(4,1)} %get-tuple-element.30), kind=kOutput, calls=%fused_computation.32 | convolution fusion | flops 51249152 | bytes 1053184 | tf_op jit(solution)/shard_map/kj,fsjr->fskr/dot_general | solution.py:174
  50.1 0.6 fusion.19
  50.7 0.6 fusion.18
  51.6 0.7 copy-done.3
  52.3 0.1 multiply_dynamic-update-slice_fusion.15
  52.4 0.1 multiply_dynamic-update-slice_fusion.14
  52.6 1.1 %fusion.6 = f32[8,256,128]{2,1,0:T(8,128)S(1)} fusion(f32[8,192,128]{2,1,0:T(8,128)S(1)} %multiply_dynamic-update-slice_fusion.12, f32[256,192,1]{0,1,2:T(8,128)S(1)} %copy-done, f32[10,256,128]{2,1,0:T(8,128)S(1)} %convolution_bitcast_fusion, f32[4,64,128]{2,1,0:T(8,128)S(1)} %get-tuple-element.28, f32[4,64,128]{2,1,0:T(8,128)S(1)} %get-tuple-element.27, ...), kind=kOutput, calls=%fused_computation.10 | convolution fusion | flops 605814784 | bytes 3473408 | tf_op jit(solution)/shard_map/ck,skr->scr/dot_general | solution.py:121
  53.7 0.0 copy-start.4
  53.7 1.0 convolution_bitcast_fusion.4
  54.7 1.2 %fusion.7 = f32[8,256,128]{2,1,0:T(8,128)S(1)} fusion(f32[256,256,1]{1,0,2:T(8,128)S(1)} %copy-done.4, f32[256,128]{1,0:T(8,128)S(1)} %broadcast_select_fusion, f32[8,256,128]{2,1,0:T(8,128)S(1)} %constant_dynamic-update-slice_fusion, f32[8,256,128]{2,1,0:T(8,128)S(1)} %fusion.6), kind=kOutput, calls=%fused_computation.11 | convolution fusion | flops 806092800 | bytes 3538944 | tf_op jit(solution)/shard_map/cd,scr->sdr/dot_general | solution.py:80
  56.0 0.0 copy-start.20
  56.0 2.5 %collective-permute-start.4 = (f32[8,32,128]{2,1,0:T(8,128)S(1)}, f32[8,32,128]{2,1,0:T(8,128)S(1)}, u32[]{:S(2)}, u32[]{:S(2)}) collective-permute-start(f32[8,32,128]{2,1,0:T(8,128)S(1)} %get-tuple-element.9), channel_id=1, source_target_pairs={{0,16},{16,32},{32,48},{48,64},{64,80},{80,96},{96,112},{112,128},... | collective-permute-start | bytes 393224 | tf_op jit(solution)/shard_map/ppermute | solution.py:16
  58.5 1.9 %collective-permute-start.5 = (f32[8,32,128]{2,1,0:T(8,128)S(1)}, f32[8,32,128]{2,1,0:T(8,128)S(1)}, u32[]{:S(2)}, u32[]{:S(2)}) collective-permute-start(f32[8,32,128]{2,1,0:T(8,128)S(1)} %get-tuple-element.12), channel_id=1, source_target_pairs={{16,0},{32,16},{48,32},{64,48},{80,64},{96,80},{112,96},{128,112},... | collective-permute-start | bytes 393224 | tf_op jit(solution)/shard_map/ppermute | solution.py:16
  60.4 1.3 %collective-permute-start.6 = (f32[8,32,128]{2,1,0:T(8,128)S(1)}, f32[8,32,128]{2,1,0:T(8,128)S(1)}, u32[]{:S(2)}, u32[]{:S(2)}) collective-permute-start(f32[8,32,128]{2,1,0:T(8,128)S(1)} %get-tuple-element.11), channel_id=1, source_target_pairs={{0,1},{1,2},{2,3},{3,4},{4,5},{5,6},{6,7},{7,8},{8,9},{9,10},{10,1... | collective-permute-start | bytes 393224 | tf_op jit(solution)/shard_map/ppermute | solution.py:22
  61.7 4.4 %collective-permute-start.7 = (f32[8,32,128]{2,1,0:T(8,128)S(1)}, f32[8,32,128]{2,1,0:T(8,128)S(1)}, u32[]{:S(2)}, u32[]{:S(2)}) collective-permute-start(f32[8,32,128]{2,1,0:T(8,128)S(1)} %get-tuple-element.10), channel_id=1, source_target_pairs={{0,15},{1,0},{2,1},{3,2},{4,3},{5,4},{6,5},{7,6},{8,7},{9,8},{10,9... | collective-permute-start | bytes 393224 | tf_op jit(solution)/shard_map/ppermute | solution.py:22
  66.0 0.1 fusion.67
  66.1 3.7 %collective-permute-done.6 = f32[8,32,128]{2,1,0:T(8,128)S(1)} collective-permute-done((f32[8,32,128]{2,1,0:T(8,128)S(1)}, f32[8,32,128]{2,1,0:T(8,128)S(1)}, u32[]{:S(2)}, u32[]{:S(2)}) %collective-permute-start.6) | collective-permute-done | bytes 131104 | tf_op jit(solution)/shard_map/ppermute | solution.py:22
  69.8 0.0 collective-permute-done.7
  69.9 0.6 fusion.17
  70.5 0.6 fusion.16
  71.0 0.6 fusion.15
  71.9 0.1 multiply_dynamic-update-slice_fusion.3
  72.0 0.1 multiply_dynamic-update-slice_fusion.2
  72.2 0.0 copy-start.17
  72.2 0.0 copy-start.5
  72.2 1.3 %fusion.4 = f32[8,256,128]{2,1,0:T(8,128)S(1)} fusion(f32[8,256,128]{2,1,0:T(8,128)S(1)} %constant_dynamic-update-slice_fusion, f32[8,256,128]{2,1,0:T(8,128)S(1)} %fusion.6, f32[8,256,128]{2,1,0:T(8,128)S(1)} %fusion.7, f32[8,192,128]{2,1,0:T(8,128)S(1)} %multiply_dynamic-update-slice_fusion, f32[256,192,1]{0,1,2:T(8,128)S(1)} %copy-done, ...), kind=kOutput, calls=%fused_computation.6 | convolution fusion | flops 606339072 | bytes 5439488 | tf_op jit(solution)/shard_map/ck,skr->scr/dot_general | solution.py:121
  73.6 0.0 copy-start.11
  73.6 0.0 copy-start.13
  73.6 0.0 copy-start.14
  73.6 0.2 fusion.35
  73.8 0.8 multiply_reduce_fusion
  74.6 0.8 fusion.36
  75.5 13.5 %all-to-all-start.1 = ((f32[256,1,4]{2,1,0:T(1,128)}), f32[256,1,4]{2,1,0:T(1,128)S(1)}, u32[]{:S(2)}, u32[]{:S(2)}) async-start(f32[256,1,4]{2,1,0:T(1,128)} %bitcast.54), calls=%async_computation.1 | async-start | bytes 262144 | tf_op jit(solution)/shard_map/all_to_all | solution.py:188
  89.0 0.8 slice.406
  89.9 12.1 %all-to-all-done.1 = f32[256,1,4]{2,1,0:T(1,128)S(1)} async-done(((f32[256,1,4]{2,1,0:T(1,128)}), f32[256,1,4]{2,1,0:T(1,128)S(1)}, u32[]{:S(2)}, u32[]{:S(2)}) %all-to-all-start.1) | async-done | bytes 4128 | tf_op jit(solution)/shard_map/all_to_all | solution.py:188
  102.0 0.8 reduce_sum.9
  (56 shorter events, 0.7 us)
Async XLA Ops:
  0.6 1.3 %copy-start = (f32[256,192,1]{0,1,2:T(8,128)S(1)}, f32[256,192,1]{0,1,2:T(8,128)}, u32[]{:S(2)}) copy-start(f32[256,192,1]{0,1,2:T(8,128)} %constant.70) | copy-start | bytes 589828
  0.6 1.2 %copy-start.1 = (f32[4,256,128]{2,1,0:T(8,128)S(1)}, f32[4,256,128]{2,1,0:T(8,128)}, u32[]{:S(2)}) copy-start(f32[4,256,128]{2,1,0:T(8,128)} %param.21) | copy-start | bytes 1572868
  1.9 15.1 %copy-start.16 = (f32[4,1]{0,1:T(1,128)S(1)}, f32[4,1]{0,1:T(1,128)}, u32[]{:S(2)}) copy-start(f32[4,1]{0,1:T(1,128)} %param.26) | copy-start | bytes 52
  2.9 32.7 %copy-start.12 = (f32[128]{0:T(128)S(1)}, f32[128]{0:T(128)}, u32[]{:S(2)}) copy-start(f32[128]{0:T(128)} %param.23) | copy-start | bytes 1540
  2.9 32.7 %copy-start.19 = (f32[128]{0:T(128)S(1)}, f32[128]{0:T(128)}, u32[]{:S(2)}) copy-start(f32[128]{0:T(128)} %param.22) | copy-start | bytes 1540
  2.9 33.2 %copy-start.6 = (f32[256,128]{1,0:T(8,128)S(1)}, f32[256,128]{1,0:T(8,128)}, u32[]{:S(2)}) copy-start(f32[256,128]{1,0:T(8,128)} %param.19) | copy-start | bytes 393220
  2.9 33.2 %copy-start.7 = (f32[256,64]{1,0:T(8,128)S(1)}, f32[256,64]{1,0:T(8,128)}, u32[]{:S(2)}) copy-start(f32[256,64]{1,0:T(8,128)} %constant.67) | copy-start | bytes 196612
  3.7 44.5 %collective-permute-start.2 = (f32[8,32,128]{2,1,0:T(8,128)}, f32[8,32,128]{2,1,0:T(8,128)}, u32[]{:S(2)}, u32[]{:S(2)}) collective-permute-start(f32[8,32,128]{2,1,0:T(8,128)} %get-tuple-element.17), channel_id=1, source_target_pairs={{0,1},{1,2},{2,3},{3,4},{4,5},{5,6},{6,7},{7,8},{8,9},{9,10},{10,1... | collective-permute-start | bytes 393224 | tf_op jit(solution)/shard_map/ppermute | solution.py:22
  6.2 42.0 %collective-permute-start.3 = (f32[8,32,128]{2,1,0:T(8,128)}, f32[8,32,128]{2,1,0:T(8,128)}, u32[]{:S(2)}, u32[]{:S(2)}) collective-permute-start(f32[8,32,128]{2,1,0:T(8,128)} %get-tuple-element.16), channel_id=1, source_target_pairs={{0,15},{1,0},{2,1},{3,2},{4,3},{5,4},{6,5},{7,6},{8,7},{9,8},{10,9... | collective-permute-start | bytes 393224 | tf_op jit(solution)/shard_map/ppermute | solution.py:22
  11.1 37.1 %collective-permute-start = (f32[8,32,128]{2,1,0:T(8,128)}, f32[8,32,128]{2,1,0:T(8,128)}, u32[]{:S(2)}, u32[]{:S(2)}) collective-permute-start(f32[8,32,128]{2,1,0:T(8,128)} %get-tuple-element.15), channel_id=1, source_target_pairs={{0,16},{16,32},{32,48},{48,64},{64,80},{80,96},{96,112},{112,128},... | collective-permute-start | bytes 393224 | tf_op jit(solution)/shard_map/ppermute | solution.py:16
  15.1 33.1 %collective-permute-start.1 = (f32[8,32,128]{2,1,0:T(8,128)}, f32[8,32,128]{2,1,0:T(8,128)}, u32[]{:S(2)}, u32[]{:S(2)}) collective-permute-start(f32[8,32,128]{2,1,0:T(8,128)} %get-tuple-element.18), channel_id=1, source_target_pairs={{16,0},{32,16},{48,32},{64,48},{80,64},{96,80},{112,96},{128,112},... | collective-permute-start | bytes 393224 | tf_op jit(solution)/shard_map/ppermute | solution.py:16
  17.8 29.2 %all-to-all-start = ((f32[256,1,4]{2,1,0:T(1,128)}), f32[256,1,4]{2,1,0:T(1,128)}, u32[]{:S(2)}, u32[]{:S(2)}) async-start(f32[256,1,4]{2,1,0:T(1,128)} %broadcast_in_dim.134), calls=%async_computation | async-start | bytes 262144 | tf_op jit(solution)/shard_map/all_to_all | solution.py:184
  37.0 2.8 %copy-start.15 = (s32[4,128]{1,0:T(4,128)S(1)}, s32[4,128]{1,0:T(4,128)}, u32[]{:S(2)}) copy-start(s32[4,128]{1,0:T(4,128)} %param.24) | copy-start | bytes 6148
  47.0 3.2 %copy-start.9 = (f32[32,32,1,1]{1,0,3,2:T(8,128)S(1)}, f32[32,32,1,1]{1,0,3,2:T(8,128)}, u32[]{:S(2)}) copy-start(f32[32,32,1,1]{1,0,3,2:T(8,128)} %constant.72) | copy-start | bytes 12292
  47.0 3.2 %copy-start.10 = (pred[4,128]{1,0:T(4,128)(4,1)S(1)}, pred[4,128]{1,0:T(4,128)(4,1)}, u32[]{:S(2)}) copy-start(pred[4,128]{1,0:T(4,128)(4,1)} %get-tuple-element.31) | copy-start | bytes 1540
  48.2 2.5 %copy-start.8 = (f32[32,32,1,1]{1,0,3,2:T(8,128)S(1)}, f32[32,32,1,1]{1,0,3,2:T(8,128)}, u32[]{:S(2)}) copy-start(f32[32,32,1,1]{1,0,3,2:T(8,128)} %constant.73) | copy-start | bytes 12292
  51.4 0.9 copy-start.3
  51.4 1.1 %copy-start.2 = (f32[8,32,127]{2,1,0:T(8,128)S(1)}, f32[8,32,127]{2,1,0:T(8,128)}, u32[]{:S(2)}) copy-start(f32[8,32,127]{2,1,0:T(8,128)} %get-tuple-element.13) | copy-start | bytes 390148
  53.7 1.0 copy-start.4
  55.9 13.9 %copy-start.18 = (pred[4,128]{1,0:T(4,128)(4,1)S(1)}, pred[4,128]{1,0:T(4,128)(4,1)}, u32[]{:S(2)}) copy-start(pred[4,128]{1,0:T(4,128)(4,1)} %get-tuple-element.30) | copy-start | bytes 1540
  56.0 13.9 %copy-start.20 = (f32[32,32,1,1]{1,0,3,2:T(8,128)S(1)}, f32[32,32,1,1]{1,0,3,2:T(8,128)}, u32[]{:S(2)}) copy-start(f32[32,32,1,1]{1,0,3,2:T(8,128)} %constant.71) | copy-start | bytes 12292
  56.0 10.1 %collective-permute-start.4 = (f32[8,32,128]{2,1,0:T(8,128)S(1)}, f32[8,32,128]{2,1,0:T(8,128)S(1)}, u32[]{:S(2)}, u32[]{:S(2)}) collective-permute-start(f32[8,32,128]{2,1,0:T(8,128)S(1)} %get-tuple-element.9), channel_id=1, source_target_pairs={{0,16},{16,32},{32,48},{48,64},{64,80},{80,96},{96,112},{112,128},... | collective-permute-start | bytes 393224 | tf_op jit(solution)/shard_map/ppermute | solution.py:16
  58.5 7.7 %collective-permute-start.5 = (f32[8,32,128]{2,1,0:T(8,128)S(1)}, f32[8,32,128]{2,1,0:T(8,128)S(1)}, u32[]{:S(2)}, u32[]{:S(2)}) collective-permute-start(f32[8,32,128]{2,1,0:T(8,128)S(1)} %get-tuple-element.12), channel_id=1, source_target_pairs={{16,0},{32,16},{48,32},{64,48},{80,64},{96,80},{112,96},{128,112},... | collective-permute-start | bytes 393224 | tf_op jit(solution)/shard_map/ppermute | solution.py:16
  60.4 9.4 %collective-permute-start.6 = (f32[8,32,128]{2,1,0:T(8,128)S(1)}, f32[8,32,128]{2,1,0:T(8,128)S(1)}, u32[]{:S(2)}, u32[]{:S(2)}) collective-permute-start(f32[8,32,128]{2,1,0:T(8,128)S(1)} %get-tuple-element.11), channel_id=1, source_target_pairs={{0,1},{1,2},{2,3},{3,4},{4,5},{5,6},{6,7},{7,8},{8,9},{9,10},{10,1... | collective-permute-start | bytes 393224 | tf_op jit(solution)/shard_map/ppermute | solution.py:22
  61.7 8.2 %collective-permute-start.7 = (f32[8,32,128]{2,1,0:T(8,128)S(1)}, f32[8,32,128]{2,1,0:T(8,128)S(1)}, u32[]{:S(2)}, u32[]{:S(2)}) collective-permute-start(f32[8,32,128]{2,1,0:T(8,128)S(1)} %get-tuple-element.10), channel_id=1, source_target_pairs={{0,15},{1,0},{2,1},{3,2},{4,3},{5,4},{6,5},{7,6},{8,7},{9,8},{10,9... | collective-permute-start | bytes 393224 | tf_op jit(solution)/shard_map/ppermute | solution.py:22
  72.2 1.4 %copy-start.17 = (f32[64,1,1]{0,1,2:T(1,128)S(1)}, f32[64,1,1]{0,1,2:T(1,128)}, u32[]{:S(2)}) copy-start(f32[64,1,1]{0,1,2:T(1,128)} %constant.74) | copy-start | bytes 772
  72.2 1.6 %copy-start.5 = (f32[128,256]{0,1:T(8,128)S(1)}, f32[128,256]{0,1:T(8,128)}, u32[]{:S(2)}) copy-start(f32[128,256]{0,1:T(8,128)} %convolution_bitcast_fusion.12) | copy-start | bytes 393220
  73.6 1.1 %copy-start.11 = (s32[128]{0:T(128)S(1)}, s32[128]{0:T(128)}, u32[]{:S(2)}) copy-start(s32[128]{0:T(128)} %param.25) | copy-start | bytes 1540
  73.6 1.1 %copy-start.13 = (f32[128]{0:T(128)S(1)}, f32[128]{0:T(128)}, u32[]{:S(2)}) copy-start(f32[128]{0:T(128)} %param.23) | copy-start | bytes 1540
  73.6 1.1 %copy-start.14 = (f32[128]{0:T(128)S(1)}, f32[128]{0:T(128)}, u32[]{:S(2)}) copy-start(f32[128]{0:T(128)} %get-tuple-element.32) | copy-start | bytes 1540
  75.5 26.5 %all-to-all-start.1 = ((f32[256,1,4]{2,1,0:T(1,128)}), f32[256,1,4]{2,1,0:T(1,128)S(1)}, u32[]{:S(2)}, u32[]{:S(2)}) async-start(f32[256,1,4]{2,1,0:T(1,128)} %bitcast.54), calls=%async_computation.1 | async-start | bytes 262144 | tf_op jit(solution)/shard_map/all_to_all | solution.py:188
